TPU v7x, 512 devices: a whole 4x4x16 slice. The times are simulated.
512 devices in a mesh: segment: 4 (over x), seq: 16 (over y, z_hi), mp: 8 (over z_lo, core).
Axes of the slice: x: 4, y: 4, z: 16 (z_hi: 4, z_lo: 4; z = z_hi * 4 + z_lo), core: 2. Of those that a mesh axis runs over, the one named last changes fastest.
Arguments:
- sources: bfloat16 [4, 2048, 7168], P('segment', 'seq', 'mp'), may hold values from -6 to 6
- unite_weight: bfloat16 [4, 7168, 7168], P('segment', 'mp', 'seq'), may hold values from -4 to 4
- norm_gain: float32 [7168], P('seq'), may hold values from 0.5 to 1.5
- head_weight: bfloat16 [7168, 16000], P('seq', ('segment', 'mp')), may hold values from -6 to 6
- doc_lengths: int32 [12], replicated, may hold values from 1 to 512, 2048 in all
- target_ids: int32 [2048], P('seq'), may hold values from 0 to 19999
- teacher_ids: int32 [2048, 8], P('seq'), may hold values from 0 to 15999
- teacher_probs: float32 [2048, 8], P('seq'), may hold values from 0.001 to 0.5
Outputs:
- mean_loss: float32 [], replicated
- head_grad: float32 [7168, 16000], P('seq', ('segment', 'mp'))
Inputs may be any that keep to these rules, and one draw needn't show every extreme that they name: `doc_lengths`: the longest document has exactly 512 tokens.
All inputs are finite; a program needn't handle non-finite values.
Results may differ from a plain program's by a relative error of at most 0.0042.
Values may be sent and summed in bfloat16 or wider, within the bound.
No kernel may reach another device: no remote copies, remote signals or barrier semaphores. Data moves between devices by JAX's collectives and lax.ppermute only.
A program may use at most 64 MiB of HBM per device.

v0:
```python
import jax
import jax.numpy as jnp
from jax import lax
from jax.sharding import PartitionSpec as P

D = 7168
VOCAB = 16000


norm_eps = 1e-06


def rounded_product(rows, weight_slab):
    product = jnp.dot(rows, weight_slab, preferred_element_type=jnp.float32)
    return lax.optimization_barrier(product.astype(jnp.bfloat16)).astype(jnp.float32)


def on_device(
    sources,
    unite_weight,
    norm_gain,
    head_weight,
    doc_lengths,
    target_ids,
    teacher_ids,
    teacher_probs,
):
    tok_local = sources.shape[1]
    weight_slab = unite_weight[0]
    partial_value = rounded_product(
        lax.all_gather(sources, "seq", axis=1, tiled=True)[0], weight_slab
    )
    united = lax.psum(partial_value, ("segment", "mp"))
    squares = lax.psum(jnp.sum(united * united, axis=1), "seq")
    hidden = (united * lax.rsqrt(squares / D + norm_eps)[:, None] * norm_gain[None, :]).astype(
        jnp.bfloat16
    )
    row_block = hidden
    logits = lax.psum_scatter(
        jnp.dot(row_block, head_weight, preferred_element_type=jnp.float32),
        "seq",
        scatter_dimension=0,
        tiled=True,
    )
    targets, teacher_top, teacher_share = (target_ids, teacher_ids, teacher_probs)
    positions = lax.axis_index("seq") * tok_local + jnp.arange(tok_local, dtype=jnp.int32)
    vocab_width = head_weight.shape[1]
    offset = lax.axis_index(("segment", "mp")) * vocab_width
    columns = offset + jnp.arange(vocab_width, dtype=jnp.int32)
    target_weight = (targets[:, None] == columns[None, :]).astype(jnp.float32)
    for top_slot in range(teacher_top.shape[1]):
        hits = (teacher_top[:, top_slot : top_slot + 1] == columns[None, :]).astype(jnp.float32)
        target_weight = target_weight + teacher_share[:, top_slot : top_slot + 1] * hits
    picked = jnp.sum(target_weight * logits, axis=1)
    row_peak = jnp.max(logits, axis=1)
    global_peak = lax.pmax(row_peak, ("segment", "mp"))
    exp_total = jnp.sum(jnp.exp(logits - global_peak[:, None]), axis=1)
    exp_total, picked = lax.psum((exp_total, picked), ("segment", "mp"))
    lse = global_peak + jnp.log(exp_total)
    target_mass = 1.0 + jnp.sum(teacher_share, axis=1)
    doc_ends = jnp.cumsum(doc_lengths)
    is_last = jnp.any(positions[:, None] + 1 == doc_ends[None, :], axis=1)
    in_vocab = (targets < VOCAB).astype(jnp.float32)
    valid_rows = jnp.where(is_last, 0.0, in_vocab)
    per_token = valid_rows * (target_mass * lse - picked)
    loss_sum, count = lax.psum((jnp.sum(per_token), jnp.sum(valid_rows)), "seq")
    mean_loss = loss_sum / jnp.maximum(count, 1.0)
    logit_grad = (
        valid_rows[:, None]
        * (target_mass[:, None] * jnp.exp(logits - lse[:, None]) - target_weight)
    ).astype(jnp.bfloat16)
    row_block = hidden
    head_grad = lax.dot_general(
        row_block,
        lax.all_gather(logit_grad, "seq", axis=0, tiled=True),
        (((0,), (0,)), ((), ())),
        preferred_element_type=jnp.float32,
    )
    return (mean_loss, head_grad)


def solution(mesh):
    placed = (
        P("segment", "seq", "mp"),
        P("segment", "mp", "seq"),
        P("seq"),
        P("seq", ("segment", "mp")),
        P(),
        P("seq"),
        P("seq", None),
        P("seq", None),
    )
    return jax.shard_map(
        on_device,
        mesh=mesh,
        in_specs=placed,
        out_specs=(P(), P("seq", ("segment", "mp"))),
        check_vma=False,
    )
```

profile of v0, /device:TPU:1, one launch (start us, length us, event | category | flops | bytes accessed | tf_op | source)
XLA Modules:
  0.0 763.8 jit_solution(10741729072304638073)
XLA Ops:
  7.2 0.0 copy-start
  7.2 0.0 all-gather.3.cloned.1.call-start
  7.2 0.7 all-gather.3.cloned.1.call-update
  7.9 0.0 reduce-scatter.2.cloned.1.call-start
  8.0 131.0 %all-gather.3.cloned.1.call-done = bf16[1,2048,896]{2,1,0:T(8,128)(2,1)} async-done(((bf16[1,128,896]{2,1,0:T(8,128)(2,1)}), bf16[1,2048,896]{2,1,0:T(8,128)(2,1)}) %all-gather.3.cloned.1.call-update) | async-done | bytes 3670032 | tf_op jit(solution)/shard_map/all_gather | solution.py:31
  139.0 0.0 copy-done
  139.0 4.1 fusion.2
  143.1 0.0 copy-start.1
  143.1 0.0 copy-start.2
  143.1 160.2 %all-reduce.3 = f32[2048,448]{0,1:T(8,128)} all-reduce(bf16[2048,448]{0,1:T(8,128)(2,1)S(1)} %fusion.2), channel_id=1, replica_groups=mesh['segment'=4,'seq'=16,'mp'=8] {'segment','mp'}, use_global_device_ids=true, to_apply=%region_3.0 | all-reduce | flops 917504 | bytes 5505024 | tf_op jit(solution)/shard_map/psum | solution.py:33
  303.3 2.4 multiply_reduce_fusion
  305.7 46.5 %psum.43 = f32[2048]{0:T(1024)S(1)} all-reduce(f32[2048]{0:T(1024)S(1)} %multiply_reduce_fusion), channel_id=1, replica_groups=mesh['segment'=4,'seq'=16,'mp'=8] {'seq'}, use_global_device_ids=true, to_apply=%region_5.0 | all-reduce | flops 2048 | bytes 16384 | tf_op jit(solution)/shard_map/psum | solution.py:34
  352.2 0.0 copy-done.1
  352.2 0.0 copy-done.2
  352.3 5.3 fusion.8
  357.6 0.0 copy-start.6
  357.6 0.0 copy-start.3
  357.6 0.0 copy-start.5
  357.6 0.0 copy-start.4
  357.6 0.0 reduce-scatter.2.cloned.1.call-update
  357.6 0.0 all-gather.5.cloned.1.call-start
  357.7 0.6 copy-done.6
  358.2 0.2 reduce-window.8
  358.4 0.0 copy-done.3
  358.5 0.1 compare_reduce_fusion
  358.6 0.0 copy-done.5
  358.6 158.6 %reduce-scatter.2.cloned.1.call-done = f32[128,500]{0,1:T(8,128)} async-done(((f32[2048,500]{0,1:T(8,128)}), f32[128,500]{0,1:T(8,128)}) %reduce-scatter.2.cloned.1.call-update) | async-done | bytes 256016 | tf_op jit(solution)/shard_map/reduce_scatter | solution.py:39
  517.1 1.0 reduce_max.9
  518.2 67.6 %pmax.7 = f32[128]{0:T(128)S(1)} all-reduce(f32[128]{0:T(128)S(1)} %reduce_max.9), channel_id=1, replica_groups=mesh['segment'=4,'seq'=16,'mp'=8] {'segment','mp'}, use_global_device_ids=true, to_apply=%region_8.0 | all-reduce | flops 128 | bytes 1024 | tf_op jit(solution)/shard_map/pmax | solution.py:56
  585.7 1.0 exponential_reduce_fusion
  586.8 0.0 copy-done.4
  586.8 1.3 multiply_reduce_fusion.1
  588.0 70.0 %all-reduce = (f32[128]{0:T(128)S(1)}, f32[128]{0:T(128)S(1)}) all-reduce(f32[128]{0:T(128)S(1)} %multiply_reduce_fusion.1, f32[128]{0:T(128)S(1)} %exponential_reduce_fusion), channel_id=1, replica_groups=mesh['segment'=4,'seq'=16,'mp'=8] {'segment','mp'}, use_global_device_ids=true, to_apply=%region_12.13 | all-reduce | flops 256 | bytes 2048 | tf_op jit(solution)/shard_map/psum | solution.py:58
  658.0 0.7 fusion.9
  658.7 1.9 multiply_convert_fusion.1
  660.6 0.0 all-gather.5.cloned.1.call-update
  660.7 45.6 %all-reduce.1 = (f32[]{:T(128)}, f32[]{:T(128)}) all-reduce(f32[]{:T(128)} %get-tuple-element.3, f32[]{:T(128)} %get-tuple-element.2), channel_id=1, replica_groups=mesh['segment'=4,'seq'=16,'mp'=8] {'seq'}, use_global_device_ids=true, to_apply=%region_14.15 | all-reduce | flops 2 | bytes 16 | tf_op jit(solution)/shard_map/psum | solution.py:66
  707.5 43.9 %all-gather.5.cloned.1.call-done = bf16[2048,500]{0,1:T(8,128)(2,1)} async-done(((bf16[128,500]{0,1:T(8,128)(2,1)}), bf16[2048,500]{0,1:T(8,128)(2,1)}) %all-gather.5.cloned.1.call-update) | async-done | bytes 2048016 | tf_op jit(solution)/shard_map/all_gather | solution.py:75
  751.3 4.8 fusion.7
  (6 shorter events, 0.0 us)
Async XLA Ops:
  7.2 131.8 %copy-start = (bf16[1,896,448]{1,2,0:T(8,128)(2,1)S(1)}, bf16[1,896,448]{1,2,0:T(8,128)(2,1)}, u32[]{:S(2)}) copy-start(bf16[1,896,448]{1,2,0:T(8,128)(2,1)} %param.9) | copy-start | bytes 2408452
  7.2 131.8 %all-gather.3.cloned.1.call-start = ((), (), s32[]{:S(2)}) async-start(), calls=%async_computation.1 | async-start | bytes 3899392 | tf_op jit(solution)/shard_map/all_gather | solution.py:31
  7.9 509.2 %reduce-scatter.2.cloned.1.call-start = ((), (), s32[]{:S(2)}) async-start(), calls=%async_computation.2 | async-start | bytes 4386816 | tf_op jit(solution)/shard_map/reduce_scatter | solution.py:39
  143.1 209.1 %copy-start.1 = (bf16[448,500]{1,0:T(8,128)(2,1)S(1)}, bf16[448,500]{1,0:T(8,128)(2,1)}, u32[]{:S(2)}) copy-start(bf16[448,500]{1,0:T(8,128)(2,1)} %param.11) | copy-start | bytes 1344004
  143.1 209.1 %copy-start.2 = (f32[448]{0:T(512)S(1)}, f32[448]{0:T(512)}, u32[]{:S(2)}) copy-start(f32[448]{0:T(512)} %param.10) | copy-start | bytes 5380
  357.6 0.7 copy-start.6
  357.6 0.8 copy-start.3
  357.6 1.0 copy-start.5
  357.6 229.2 %copy-start.4 = (s32[128]{0:T(128)S(1)}, s32[128]{0:T(128)}, u32[]{:S(2)}) copy-start(s32[128]{0:T(128)} %param.13) | copy-start | bytes 1540
  357.6 393.7 %all-gather.5.cloned.1.call-start = ((), (), s32[]{:S(2)}) async-start(), calls=%async_computation.3 | async-start | bytes 2193408 | tf_op jit(solution)/shard_map/all_gather | solution.py:75
Sparse Core Ops, SparseCore 0:
  11.1 127.8 all-gather.2
  357.7 159.3 reduce-scatter.1
  660.8 90.4 all-gather.4
where the time goes:
time: 767 us; the launch traced here: 764 us
  blocking collectives  390 us (51%)
  waiting for transfers between devices  334 us (44%)
  between operations  16.2 us (2%)
  matrix products  14.3 us (2%)
  other arithmetic  8.62 us (1%)
    psum x1, blocking collectives, on_device(): united = lax.psum(partial_value, ('segment', 'mp'))  160 us
    reduce_scatter x1, waiting for transfers between devices, on_device(): lax.psum_scatter(jnp.dot(row_block, head_weight, preferred_element_type=j...  159 us
    all_gather x1, waiting for transfers between devices, on_device(): lax.all_gather(sources, 'seq', axis=1, tiled=True)[0]  131 us
    psum x1, blocking collectives, on_device(): exp_total, picked = lax.psum((exp_total, picked), ('segment', 'mp'))  70 us
    pmax x1, blocking collectives, on_device(): global_peak = lax.pmax(row_peak, ('segment', 'mp'))  67.6 us
    psum x1, blocking collectives, on_device(): squares = lax.psum(jnp.sum(united * united, axis=1), 'seq')  46.5 us
    psum x1, blocking collectives, on_device(): loss_sum, count = lax.psum((jnp.sum(per_token), jnp.sum(valid_rows)), 'seq')  45.6 us
    all_gather x1, waiting for transfers between devices, on_device(): lax.all_gather(logit_grad, 'seq', axis=0, tiled=True)  43.9 us
  transfers between devices with their start and end apart: 3, of which 3 were waited for; matrix products, arithmetic and copies ran while one was open for 0% of the time, Pallas kernels for 0%

commit v1 on v0

v1 whole, which is shorter than its diff:
```python
import jax
import jax.numpy as jnp
from jax import lax
from jax.sharding import Mesh
from jax.sharding import PartitionSpec as P

D = 7168
VOCAB = 16000

norm_eps = 1e-06

SEQ = ("y", "zhi")
SM = ("segment", "zlo", "core")


def butterfly(value, axis, size, combine):
    step = 1
    while step < size:
        pairs = [(i, i ^ step) for i in range(size)]
        value = combine(value, lax.ppermute(value, axis, pairs))
        step *= 2
    return value


def add(a, b):
    return a + b


def merge_stats(a, b):
    peak = jnp.maximum(a[0], b[0])
    total = a[1] * jnp.exp(a[0] - peak) + b[1] * jnp.exp(b[0] - peak)
    return jnp.stack([peak, total, a[2] + b[2]])


def on_device(
    sources,
    unite_weight,
    norm_gain,
    head_weight,
    doc_lengths,
    target_ids,
    teacher_ids,
    teacher_probs,
    sizes,
):
    tok_local = sources.shape[1]
    n_sm = sizes["segment"] * sizes["zlo"] * sizes["core"]

    rows = lax.all_gather(sources[0], "zhi", axis=0, tiled=True)
    rows = lax.all_gather(rows, "y", axis=0, tiled=True)
    tokens = rows.shape[0]
    product = jnp.dot(rows, unite_weight[0], preferred_element_type=jnp.float32)
    product = lax.optimization_barrier(product.astype(jnp.bfloat16))

    pieces = lax.all_to_all(product, SM, 0, 0, tiled=True)
    slice_len = tokens // n_sm
    united = jnp.sum(
        pieces.reshape(n_sm, slice_len, -1).astype(jnp.float32), axis=0
    )

    squares = jnp.sum(united * united, axis=1)
    squares = butterfly(squares, "y", sizes["y"], add)
    squares = butterfly(squares, "zhi", sizes["zhi"], add)
    hidden_part = (
        united * lax.rsqrt(squares / D + norm_eps)[:, None] * norm_gain[None, :]
    ).astype(jnp.bfloat16)
    spread = jnp.broadcast_to(hidden_part[None], (n_sm,) + hidden_part.shape)
    hidden = lax.all_to_all(
        spread.reshape(tokens, -1), SM, 0, 0, tiled=True
    )

    logits = jnp.dot(hidden, head_weight, preferred_element_type=jnp.float32)
    logits = lax.psum_scatter(logits, "y", scatter_dimension=0, tiled=True)
    logits = lax.psum_scatter(logits, "zhi", scatter_dimension=0, tiled=True)

    seq_index = lax.axis_index("y") * sizes["zhi"] + lax.axis_index("zhi")
    positions = seq_index * tok_local + jnp.arange(tok_local, dtype=jnp.int32)
    vocab_width = head_weight.shape[1]
    offset = lax.axis_index(SM) * vocab_width
    columns = offset + jnp.arange(vocab_width, dtype=jnp.int32)
    target_weight = (target_ids[:, None] == columns[None, :]).astype(jnp.float32)
    for top_slot in range(teacher_ids.shape[1]):
        hits = (teacher_ids[:, top_slot : top_slot + 1] == columns[None, :]).astype(
            jnp.float32
        )
        target_weight = target_weight + teacher_probs[:, top_slot : top_slot + 1] * hits

    row_peak = jnp.max(logits, axis=1)
    stats = jnp.stack(
        [
            row_peak,
            jnp.sum(jnp.exp(logits - row_peak[:, None]), axis=1),
            jnp.sum(target_weight * logits, axis=1),
        ]
    )
    for axis in SM:
        stats = butterfly(stats, axis, sizes[axis], merge_stats)
    lse = stats[0] + jnp.log(stats[1])
    picked = stats[2]

    target_mass = 1.0 + jnp.sum(teacher_probs, axis=1)
    doc_ends = jnp.cumsum(doc_lengths)
    is_last = jnp.any(positions[:, None] + 1 == doc_ends[None, :], axis=1)
    in_vocab = (target_ids < VOCAB).astype(jnp.float32)
    valid_rows = jnp.where(is_last, 0.0, in_vocab)
    per_token = valid_rows * (target_mass * lse - picked)
    loss_hi = per_token.astype(jnp.bfloat16)
    loss_lo = (per_token - loss_hi.astype(jnp.float32)).astype(jnp.bfloat16)

    logit_grad = (
        valid_rows[:, None]
        * (target_mass[:, None] * jnp.exp(logits - lse[:, None]) - target_weight)
    ).astype(jnp.bfloat16)
    extra = jnp.stack(
        [loss_hi, loss_lo, valid_rows.astype(jnp.bfloat16), jnp.zeros_like(loss_hi)],
        axis=1,
    )
    carried = jnp.concatenate([logit_grad, extra], axis=1)
    carried = lax.all_gather(carried, "zhi", axis=0, tiled=True)
    carried = lax.all_gather(carried, "y", axis=0, tiled=True)

    loss_sum = jnp.sum(
        carried[:, vocab_width].astype(jnp.float32)
        + carried[:, vocab_width + 1].astype(jnp.float32)
    )
    count = jnp.sum(carried[:, vocab_width + 2].astype(jnp.float32))
    mean_loss = loss_sum / jnp.maximum(count, 1.0)

    head_grad = lax.dot_general(
        hidden,
        carried[:, :vocab_width],
        (((0,), (0,)), ((), ())),
        preferred_element_type=jnp.float32,
    )
    return (mean_loss, head_grad)


def solution(mesh):
    n_seg, n_seq, n_mp = (mesh.shape[a] for a in ("segment", "seq", "mp"))
    sizes = {"segment": n_seg, "y": n_seq // 4, "zhi": 4, "zlo": n_mp // 2, "core": 2}
    fine = Mesh(
        mesh.devices.reshape(n_seg, sizes["y"], sizes["zhi"], sizes["zlo"], sizes["core"]),
        ("segment", "y", "zhi", "zlo", "core"),
    )
    placed = (
        P("segment", SEQ, ("zlo", "core")),
        P("segment", ("zlo", "core"), SEQ),
        P(SEQ),
        P(SEQ, SM),
        P(),
        P(SEQ),
        P(SEQ, None),
        P(SEQ, None),
    )

    def body(*args):
        return on_device(*args, sizes=sizes)

    return jax.shard_map(
        body,
        mesh=fine,
        in_specs=placed,
        out_specs=(P(), P(SEQ, SM)),
        check_vma=False,
    )
```

time: 767 us -> 501 us (0.65)
  blocking collectives: 390 us -> 199 us
  waiting for transfers between devices: 334 us -> 218 us
  starting transfers between devices: 0.12 us -> 44.2 us
    psum x4 -> x0, blocking collectives: 322 us -> none  [the longest x1 160 us: on_device(): united = lax.psum(partial_value, ('segment', 'mp'))]
    all_to_all x0 -> x2, blocking collectives: none -> 117 us  [the longest x1 58.6 us: on_device(): hidden = lax.all_to_all(spread.reshape(tokens, -1), SM, 0, 0, tiled=True)]
    all_gather x2, waiting for transfers between devices: 175 us -> 90.8 us  [the longest x1 50.1 us: on_device(): rows = lax.all_gather(rows, 'y', axis=0, tiled=True)]
    all_gather x0 -> x2, blocking collectives: none -> 81.9 us  [the longest x1 45.3 us: on_device(): rows = lax.all_gather(sources[0], 'zhi', axis=0, tiled=True)]
    pmax x1 -> x0, blocking collectives: 67.6 us -> none  [on_device(): global_peak = lax.pmax(row_peak, ('segment', 'mp'))]
    reduce_scatter x1 -> x2, waiting for transfers between devices: 159 us -> 111 us  [the longest x1 61.2 us: on_device(): logits = lax.psum_scatter(logits, 'zhi', scatter_dimension=0, tiled=True)]
    ppermute x0 -> x9, starting transfers between devices: none -> 44.1 us  [butterfly(): value = combine(value, lax.ppermute(value, axis, pairs))]
    ppermute x0 -> x9, waiting for transfers between devices: none -> 16.2 us  [butterfly(): value = combine(value, lax.ppermute(value, axis, pairs))]
  transfers between devices with their start and end apart: 3 -> 13, of which waited for: 3 -> 13; matrix products, arithmetic and copies ran while one was open for 0% -> 0% of each run, Pallas kernels for 0% -> 0%
where the time goes in v1:
time: 501 us; the launch traced here: 500 us
  waiting for transfers between devices  218 us (44%)
  blocking collectives  199 us (40%)
  starting transfers between devices  44.2 us (9%)
  between operations  16.5 us (3%)
  matrix products  12.5 us (2%)
  other arithmetic  7.1 us (1%)
    reduce_scatter x1, waiting for transfers between devices, on_device(): logits = lax.psum_scatter(logits, 'zhi', scatter_dimension=0, tiled=True)  61.2 us
    all_to_all x1, blocking collectives, on_device(): hidden = lax.all_to_all(spread.reshape(tokens, -1), SM, 0, 0, tiled=True)  58.6 us
    all_to_all x1, blocking collectives, on_device(): pieces = lax.all_to_all(product, SM, 0, 0, tiled=True)  58.2 us
    all_gather x1, waiting for transfers between devices, on_device(): rows = lax.all_gather(rows, 'y', axis=0, tiled=True)  50.1 us
    reduce_scatter x1, waiting for transfers between devices, on_device(): logits = lax.psum_scatter(logits, 'y', scatter_dimension=0, tiled=True)  49.8 us
    all_gather x1, blocking collectives, on_device(): rows = lax.all_gather(sources[0], 'zhi', axis=0, tiled=True)  45.3 us
    ppermute x9, starting transfers between devices, butterfly(): value = combine(value, lax.ppermute(value, axis, pairs))  44.1 us
    all_gather x1, waiting for transfers between devices, on_device(): carried = lax.all_gather(carried, 'y', axis=0, tiled=True)  40.7 us
  transfers between devices with their start and end apart: 13, of which 13 were waited for; matrix products, arithmetic and copies ran while one was open for 0% of the time, Pallas kernels for 0%

profile of v1, /device:TPU:1, one launch (start us, length us, event | category | flops | bytes accessed | tf_op | source)
XLA Modules:
  0.0 500.2 jit_solution(34114228269662318)
XLA Ops:
  7.2 0.0 all-gather.7.cloned.1.call-start
  7.2 45.3 %all-gather = bf16[1,512,896]{2,1,0:T(8,128)(2,1)} all-gather(bf16[1,128,896]{2,1,0:T(8,128)(2,1)} %param.8), channel_id=2, replica_groups=mesh['segment'=4,'y'=4,'zhi'=4,'zlo'=4,'core'=2] {'zhi'}, dimensions={1}, use_global_device_ids=true | all-gather | bytes 1146880 | tf_op jit(solution)/shard_map/all_gather | solution.py:49
  52.5 0.0 all-gather.7.cloned.1.call-update
  52.5 0.0 reduce-scatter.3.cloned.1.call-start
  52.6 50.1 %all-gather.7.cloned.1.call-done = bf16[1,2048,896]{2,1,0:T(8,128)(2,1)} async-done(((bf16[1,512,896]{2,1,0:T(8,128)(2,1)}), bf16[1,2048,896]{2,1,0:T(8,128)(2,1)}) %all-gather.7.cloned.1.call-update) | async-done | bytes 3670032 | tf_op jit(solution)/shard_map/all_gather | solution.py:50
  102.7 5.4 %fusion.2 = bf16[2048,448]{0,1:T(8,128)(2,1)} fusion(bf16[1,2048,896]{2,1,0:T(8,128)(2,1)} %all-gather.7.cloned.1.call-done, bf16[1,896,448]{1,2,0:T(8,128)(2,1)S(1)} %copy-done), kind=kOutput, calls=%fused_computation.3 | convolution fusion | flops 1645084672 | bytes 6307840 | tf_op jit(solution)/shard_map/dot_general | solution.py:52
  108.1 2.8 copy.11
  110.9 58.2 %all_to_all.18 = bf16[32,64,448]{2,1,0:T(8,128)(2,1)S(1)} all-to-all(bf16[32,64,448]{2,1,0:T(8,128)(2,1)S(1)} %bitcast.218), channel_id=1, replica_groups=mesh['segment'=4,'y'=4,'zhi'=4,'zlo'=4,'core'=2] {'segment','zlo','core'}, dimensions={0} | all-to-all | bytes 3670016 | tf_op jit(solution)/shard_map/all_to_all | solution.py:55
  169.1 0.3 convert_reduce_fusion
  169.4 0.1 multiply_reduce_fusion.1
  169.5 2.4 collective-permute-start
  171.9 1.9 collective-permute-done
  173.8 3.6 collective-permute-start.1
  177.4 2.2 collective-permute-done.1
  179.6 7.4 %collective-permute-start.2 = (f32[64]{0:T(128)S(1)}, f32[64]{0:T(128)S(1)}, u32[]{:S(2)}, u32[]{:S(2)}) collective-permute-start(f32[64]{0:T(128)S(1)} %add.201), channel_id=1, source_target_pairs={{0,8},{8,0},{16,24},{24,16},{1,9},{9,1},{17,25},{25,17},{2,10},{10... | collective-permute-start | bytes 776 | tf_op jit(solution)/shard_map/ppermute | solution.py:20
  186.9 0.9 collective-permute-done.2
  187.9 9.7 %collective-permute-start.3 = (f32[64]{0:T(128)S(1)}, f32[64]{0:T(128)S(1)}, u32[]{:S(2)}, u32[]{:S(2)}) collective-permute-start(f32[64]{0:T(128)S(1)} %add.202), channel_id=1, source_target_pairs={{0,16},{8,24},{16,0},{24,8},{1,17},{9,25},{17,1},{25,9},{2,18},{10... | collective-permute-start | bytes 776 | tf_op jit(solution)/shard_map/ppermute | solution.py:20
  197.6 3.2 collective-permute-done.3
  200.9 0.1 multiply_convert_fusion.1
  200.9 0.2 broadcast_in_dim.6
  201.2 58.6 %all_to_all.19 = bf16[32,64,448]{2,1,0:T(8,128)(2,1)S(1)} all-to-all(bf16[32,64,448]{2,1,0:T(8,128)(2,1)S(1)} %broadcast_in_dim.6), channel_id=1, replica_groups=mesh['segment'=4,'y'=4,'zhi'=4,'zlo'=4,'core'=2] {'segment','zlo','core'}, dimensions={0} | all-to-all | bytes 3670016 | tf_op jit(solution)/shard_map/all_to_all | solution.py:68
  259.8 3.2 fusion.44
  263.1 0.0 reduce-scatter.5.cloned.1.call-start
  263.1 49.8 %reduce-scatter.3.cloned.1.call-done = f32[512,500]{0,1:T(8,128)} async-done(((f32[2048,500]{0,1:T(8,128)}), f32[512,500]{0,1:T(8,128)}) %reduce-scatter.3.cloned.1.call-update) | async-done | bytes 1024016 | tf_op jit(solution)/shard_map/reduce_scatter | solution.py:73
  313.0 0.0 all-gather.5.cloned.1.call-start
  313.1 61.2 %reduce-scatter.5.cloned.1.call-done = f32[128,500]{0,1:T(8,128)} async-done(((f32[512,500]{0,1:T(8,128)}), f32[128,500]{0,1:T(8,128)}) %reduce-scatter.5.cloned.1.call-update) | async-done | bytes 256016 | tf_op jit(solution)/shard_map/reduce_scatter | solution.py:74
  374.3 1.0 reduce_max.9
  375.3 1.0 exponential_reduce_fusion
  376.4 1.3 multiply_reduce_fusion
  377.6 3.4 collective-permute-start.4
  381.1 1.0 collective-permute-done.4
  382.1 4.9 collective-permute-start.5
  387.0 1.0 collective-permute-done.5
  387.9 1.9 collective-permute-start.6
  389.9 0.2 reduce-window.8
  390.1 2.2 collective-permute-done.6
  392.3 2.0 collective-permute-start.7
  394.3 0.1 compare_reduce_fusion
  394.5 3.1 collective-permute-done.7
  397.6 8.7 %collective-permute-start.8 = (f32[3,128]{1,0:T(4,128)S(1)}, f32[3,128]{1,0:T(4,128)S(1)}, u32[]{:S(2)}, u32[]{:S(2)}) collective-permute-start(f32[3,128]{1,0:T(4,128)S(1)} %pad_maximum_fusion.4), channel_id=1, source_target_pairs={{0,1},{1,0},{2,3},{3,2},{4,5},{5,4},{6,7},{7,6},{8,9},{9,8},{10,11... | collective-permute-start | bytes 4616 | tf_op jit(solution)/shard_map/ppermute | solution.py:20
  406.3 0.8 collective-permute-done.8
  407.1 1.3 multiply_convert_fusion
  408.4 0.1 concatenate.3
  408.5 36.6 %all_gather.14 = bf16[512,504]{0,1:T(8,128)(2,1)} all-gather(bf16[128,504]{0,1:T(8,128)(2,1)S(1)} %concatenate.3), channel_id=1, replica_groups=mesh['segment'=4,'y'=4,'zhi'=4,'zlo'=4,'core'=2] {'zhi'}, dimensions={0}, use_global_device_ids=true | all-gather | bytes 645120 | tf_op jit(solution)/shard_map/all_gather | solution.py:119
  445.1 0.0 all-gather.5.cloned.1.call-update
  445.1 40.7 %all-gather.5.cloned.1.call-done = bf16[2048,504]{0,1:T(8,128)(2,1)} async-done(((bf16[512,504]{0,1:T(8,128)(2,1)}), bf16[2048,504]{0,1:T(8,128)(2,1)}) %all-gather.5.cloned.1.call-update) | async-done | bytes 2064400 | tf_op jit(solution)/shard_map/all_gather | solution.py:120
  485.8 1.5 fusion.8
  488.6 4.0 fusion.5
  (37 shorter events, 0.3 us)
Async XLA Ops:
  7.2 95.5 %copy-start = (bf16[1,896,448]{1,2,0:T(8,128)(2,1)S(1)}, bf16[1,896,448]{1,2,0:T(8,128)(2,1)}, u32[]{:S(2)}) copy-start(bf16[1,896,448]{1,2,0:T(8,128)(2,1)} %param.9) | copy-start | bytes 2408452
  7.2 95.5 %all-gather.7.cloned.1.call-start = ((), (), s32[]{:S(2)}) async-start(), calls=%async_computation.7 | async-start | bytes 4587520 | tf_op jit(solution)/shard_map/all_gather | solution.py:50
  52.5 260.4 %reduce-scatter.3.cloned.1.call-start = ((), (), s32[]{:S(2)}) async-start(), calls=%async_computation.4 | async-start | bytes 5160960 | tf_op jit(solution)/shard_map/reduce_scatter | solution.py:73
  169.1 31.8 %copy-start.5 = (f32[448]{0:T(512)S(1)}, f32[448]{0:T(512)}, u32[]{:S(2)}) copy-start(f32[448]{0:T(512)} %param.10) | copy-start | bytes 5380
  169.5 4.3 collective-permute-start
  173.8 5.8 %collective-permute-start.1 = (f32[64]{0:T(128)S(1)}, f32[64]{0:T(128)S(1)}, u32[]{:S(2)}, u32[]{:S(2)}) collective-permute-start(f32[64]{0:T(128)S(1)} %add.200), channel_id=1, source_target_pairs={{0,64},{32,96},{64,0},{96,32},{1,65},{33,97},{65,1},{97,33},{2,66}... | collective-permute-start | bytes 776 | tf_op jit(solution)/shard_map/ppermute | solution.py:20
  179.6 8.3 %collective-permute-start.2 = (f32[64]{0:T(128)S(1)}, f32[64]{0:T(128)S(1)}, u32[]{:S(2)}, u32[]{:S(2)}) collective-permute-start(f32[64]{0:T(128)S(1)} %add.201), channel_id=1, source_target_pairs={{0,8},{8,0},{16,24},{24,16},{1,9},{9,1},{17,25},{25,17},{2,10},{10... | collective-permute-start | bytes 776 | tf_op jit(solution)/shard_map/ppermute | solution.py:20
  187.9 13.0 %collective-permute-start.3 = (f32[64]{0:T(128)S(1)}, f32[64]{0:T(128)S(1)}, u32[]{:S(2)}, u32[]{:S(2)}) collective-permute-start(f32[64]{0:T(128)S(1)} %add.202), channel_id=1, source_target_pairs={{0,16},{8,24},{16,0},{24,8},{1,17},{9,25},{17,1},{25,9},{2,18},{10... | collective-permute-start | bytes 776 | tf_op jit(solution)/shard_map/ppermute | solution.py:20
  201.2 58.7 %copy-start.1 = (bf16[448,500]{1,0:T(8,128)(2,1)S(1)}, bf16[448,500]{1,0:T(8,128)(2,1)}, u32[]{:S(2)}) copy-start(bf16[448,500]{1,0:T(8,128)(2,1)} %param.11) | copy-start | bytes 1344004
  263.1 50.0 %copy-start.4 = (s32[128,8]{0,1:T(8,128)S(1)}, s32[128,8]{0,1:T(8,128)}, u32[]{:S(2)}) copy-start(s32[128,8]{0,1:T(8,128)} %param.14) | copy-start | bytes 12292
  263.1 50.0 %copy-start.2 = (f32[128,8]{0,1:T(8,128)S(1)}, f32[128,8]{0,1:T(8,128)}, u32[]{:S(2)}) copy-start(f32[128,8]{0,1:T(8,128)} %param.15) | copy-start | bytes 12292
  263.1 113.3 %copy-start.3 = (s32[128]{0:T(128)S(1)}, s32[128]{0:T(128)}, u32[]{:S(2)}) copy-start(s32[128]{0:T(128)} %param.13) | copy-start | bytes 1540
  263.1 126.8 %copy-start.6 = (s32[12]{0:T(128)S(1)}, s32[12]{0:T(128)}, u32[]{:S(2)}) copy-start(s32[12]{0:T(128)} %param.12) | copy-start | bytes 148
  263.1 111.2 %reduce-scatter.5.cloned.1.call-start = ((), (), s32[]{:S(2)}) async-start(), calls=%async_computation.5 | async-start | bytes 1290240 | tf_op jit(solution)/shard_map/reduce_scatter | solution.py:74
  313.0 172.8 %all-gather.5.cloned.1.call-start = ((), (), s32[]{:S(2)}) async-start(), calls=%async_computation.6 | async-start | bytes 2580480 | tf_op jit(solution)/shard_map/all_gather | solution.py:120
  377.6 4.4 collective-permute-start.4
  382.1 5.8 %collective-permute-start.5 = (f32[3,128]{1,0:T(4,128)S(1)}, f32[3,128]{1,0:T(4,128)S(1)}, u32[]{:S(2)}, u32[]{:S(2)}) collective-permute-start(f32[3,128]{1,0:T(4,128)S(1)} %pad_maximum_fusion.1), channel_id=1, source_target_pairs={{0,256},{128,384},{256,0},{384,128},{1,257},{129,385},{257,1},{385... | collective-permute-start | bytes 4616 | tf_op jit(solution)/shard_map/ppermute | solution.py:20
  387.9 4.3 collective-permute-start.6
  392.3 5.2 %collective-permute-start.7 = (f32[3,128]{1,0:T(4,128)S(1)}, f32[3,128]{1,0:T(4,128)S(1)}, u32[]{:S(2)}, u32[]{:S(2)}) collective-permute-start(f32[3,128]{1,0:T(4,128)S(1)} %pad_maximum_fusion.3), channel_id=1, source_target_pairs={{0,4},{2,6},{4,0},{6,2},{1,5},{3,7},{5,1},{7,3},{8,12},{10,14},{12... | collective-permute-start | bytes 4616 | tf_op jit(solution)/shard_map/ppermute | solution.py:20
  397.6 9.5 %collective-permute-start.8 = (f32[3,128]{1,0:T(4,128)S(1)}, f32[3,128]{1,0:T(4,128)S(1)}, u32[]{:S(2)}, u32[]{:S(2)}) collective-permute-start(f32[3,128]{1,0:T(4,128)S(1)} %pad_maximum_fusion.4), channel_id=1, source_target_pairs={{0,1},{1,0},{2,3},{3,2},{4,5},{5,4},{6,7},{7,6},{8,9},{9,8},{10,11... | collective-permute-start | bytes 4616 | tf_op jit(solution)/shard_map/ppermute | solution.py:20
Sparse Core Ops, SparseCore 0:
  52.7 49.9 all-gather.6
  263.2 49.7 reduce-scatter.2
  316.1 58.2 reduce-scatter.4
  445.2 40.5 all-gather.4

commit v2 on v1

--- a/solution.py
+++ b/solution.py
@@ -13,13 +13,39 @@
 SM = ("segment", "zlo", "core")
 
 
-def butterfly(value, axis, size, combine):
-    step = 1
-    while step < size:
-        pairs = [(i, i ^ step) for i in range(size)]
-        value = combine(value, lax.ppermute(value, axis, pairs))
-        step *= 2
-    return value
+def gather_axis(value, axis, size):
+    got = [value]
+    for shift in range(1, size):
+        pairs = [(i, (i + shift) % size) for i in range(size)]
+        got.append(lax.ppermute(value, axis, pairs))
+    rotated = jnp.stack([got[0]] + got[1:][::-1])
+    me = lax.axis_index(axis)
+    doubled = jnp.concatenate([rotated, rotated], axis=0)
+    return lax.dynamic_slice_in_dim(doubled, (size - me) % size, size, axis=0)
+
+
+def reduce_axis(value, axis, size, combine):
+    every = gather_axis(value, axis, size)
+    total = every[0]
+    for k in range(1, size):
+        total = combine(total, every[k])
+    return total
+
+
+def scatter_sum_axis(value, axis, size):
+    me = lax.axis_index(axis)
+    part = value.shape[0] // size
+    total = lax.dynamic_slice_in_dim(value, me * part, part, axis=0)
+    for shift in range(1, size):
+        pairs = [(i, (i + shift) % size) for i in range(size)]
+        chunk = lax.dynamic_slice_in_dim(value, ((me + shift) % size) * part, part, axis=0)
+        total = total + lax.ppermute(chunk, axis, pairs)
+    return total
+
+
+def gather_rows_axis(value, axis, size):
+    every = gather_axis(value, axis, size)
+    return every.reshape((size * value.shape[0],) + value.shape[1:])
 
 
 def add(a, b):
@@ -46,7 +72,7 @@
     tok_local = sources.shape[1]
     n_sm = sizes["segment"] * sizes["zlo"] * sizes["core"]
 
-    rows = lax.all_gather(sources[0], "zhi", axis=0, tiled=True)
+    rows = gather_rows_axis(sources[0], "zhi", sizes["zhi"])
     rows = lax.all_gather(rows, "y", axis=0, tiled=True)
     tokens = rows.shape[0]
     product = jnp.dot(rows, unite_weight[0], preferred_element_type=jnp.float32)
@@ -59,8 +85,8 @@
     )
 
     squares = jnp.sum(united * united, axis=1)
-    squares = butterfly(squares, "y", sizes["y"], add)
-    squares = butterfly(squares, "zhi", sizes["zhi"], add)
+    squares = reduce_axis(squares, "y", sizes["y"], add)
+    squares = reduce_axis(squares, "zhi", sizes["zhi"], add)
     hidden_part = (
         united * lax.rsqrt(squares / D + norm_eps)[:, None] * norm_gain[None, :]
     ).astype(jnp.bfloat16)
@@ -71,7 +97,7 @@
 
     logits = jnp.dot(hidden, head_weight, preferred_element_type=jnp.float32)
     logits = lax.psum_scatter(logits, "y", scatter_dimension=0, tiled=True)
-    logits = lax.psum_scatter(logits, "zhi", scatter_dimension=0, tiled=True)
+    logits = scatter_sum_axis(logits, "zhi", sizes["zhi"])
 
     seq_index = lax.axis_index("y") * sizes["zhi"] + lax.axis_index("zhi")
     positions = seq_index * tok_local + jnp.arange(tok_local, dtype=jnp.int32)
@@ -94,7 +120,7 @@
         ]
     )
     for axis in SM:
-        stats = butterfly(stats, axis, sizes[axis], merge_stats)
+        stats = reduce_axis(stats, axis, sizes[axis], merge_stats)
     lse = stats[0] + jnp.log(stats[1])
     picked = stats[2]
 
@@ -116,7 +142,7 @@
         axis=1,
     )
     carried = jnp.concatenate([logit_grad, extra], axis=1)
-    carried = lax.all_gather(carried, "zhi", axis=0, tiled=True)
+    carried = gather_rows_axis(carried, "zhi", sizes["zhi"])
     carried = lax.all_gather(carried, "y", axis=0, tiled=True)
 
     loss_sum = jnp.sum(

time: 501 us -> 504 us (level)
  blocking collectives: 199 us -> 58.2 us
  starting transfers between devices: 44.2 us -> 121 us
  waiting for transfers between devices: 218 us -> 281 us
  local copies, waits for them, and re-layouts: 3.14 us -> 8.82 us
    ppermute x9 -> x22, waiting for transfers between devices: 16.2 us -> 98.8 us  [the longest x19 61.7 us: gather_axis(): got.append(lax.ppermute(value, axis, pairs))]
    all_gather x2 -> x0, blocking collectives: 81.9 us -> none  [the longest x1 45.3 us: on_device(): rows = lax.all_gather(sources[0], 'zhi', axis=0, tiled=True)]
    ppermute x9 -> x22, starting transfers between devices: 44.1 us -> 113 us  [the longest x19 91.5 us: gather_axis(): got.append(lax.ppermute(value, axis, pairs))]
    reduce_scatter x1 -> x0, waiting for transfers between devices: 61.2 us -> none  [on_device(): logits = lax.psum_scatter(logits, 'zhi', scatter_dimension=0, tiled=True)]
    all_to_all x1 -> x0, blocking collectives: 58.2 us -> none  [on_device(): pieces = lax.all_to_all(product, SM, 0, 0, tiled=True)]
    all_to_all x0 -> x1, waiting for transfers between devices: none -> 49.7 us  [on_device(): pieces = lax.all_to_all(product, SM, 0, 0, tiled=True)]
    all_gather x1, waiting for transfers between devices: 40.7 us -> 31.1 us  [on_device(): carried = lax.all_gather(carried, 'y', axis=0, tiled=True)]
    all_to_all x0 -> x1, starting transfers between devices: none -> 8.05 us  [on_device(): pieces = lax.all_to_all(product, SM, 0, 0, tiled=True)]
  transfers between devices with their start and end apart: 13 -> 26, of which waited for: 13 -> 18; matrix products, arithmetic and copies ran while one was open for 0% -> 0% of each run, Pallas kernels for 0% -> 0%
where the time goes in v2:
time: 504 us; the launch traced here: 503 us
  waiting for transfers between devices  281 us (56%)
  starting transfers between devices  121 us (24%)
  blocking collectives  58.2 us (12%)
  between operations  16.9 us (3%)
  matrix products  11 us (2%)
  local copies, waits for them, and re-layouts  8.82 us (2%)
  other arithmetic  5.92 us (1%)
    ppermute x19, starting transfers between devices, gather_axis(): got.append(lax.ppermute(value, axis, pairs))  91.5 us
    ppermute x19, waiting for transfers between devices, gather_axis(): got.append(lax.ppermute(value, axis, pairs))  61.7 us
    all_to_all x1, blocking collectives, on_device(): hidden = lax.all_to_all(spread.reshape(tokens, -1), SM, 0, 0, tiled=True)  58.2 us
    all_gather x1, waiting for transfers between devices, on_device(): rows = lax.all_gather(rows, 'y', axis=0, tiled=True)  58.1 us
    all_to_all x1, waiting for transfers between devices, on_device(): pieces = lax.all_to_all(product, SM, 0, 0, tiled=True)  49.7 us
    reduce_scatter x1, waiting for transfers between devices, on_device(): logits = lax.psum_scatter(logits, 'y', scatter_dimension=0, tiled=True)  43.2 us
    ppermute x3, waiting for transfers between devices, scatter_sum_axis(): total = total + lax.ppermute(chunk, axis, pairs)  37.1 us
    all_gather x1, waiting for transfers between devices, on_device(): carried = lax.all_gather(carried, 'y', axis=0, tiled=True)  31.1 us
  transfers between devices with their start and end apart: 26, of which 18 were waited for; matrix products, arithmetic and copies ran while one was open for 0% of the time, Pallas kernels for 0%

profile of v2, /device:TPU:1, one launch (start us, length us, event | category | flops | bytes accessed | tf_op | source)
XLA Modules:
  0.0 503.2 jit_solution(17988154032129839541)
XLA Ops:
  7.2 13.4 %collective-permute-start = (bf16[128,896]{1,0:T(8,128)(2,1)}, bf16[128,896]{1,0:T(8,128)(2,1)S(1)}, u32[]{:S(2)}, u32[]{:S(2)}) collective-permute-start(bf16[128,896]{1,0:T(8,128)(2,1)} %bitcast.301), channel_id=1, source_target_pairs={{0,24},{8,0},{16,8},{24,16},{1,25},{9,1},{17,9},{25,17},{2,26},{10... | collective-permute-start | bytes 688136 | tf_op jit(solution)/shard_map/ppermute | solution.py:20
  20.7 4.9 collective-permute-start.1
  25.6 7.3 %collective-permute-start.2 = (bf16[128,896]{1,0:T(8,128)(2,1)}, bf16[128,896]{1,0:T(8,128)(2,1)S(1)}, u32[]{:S(2)}, u32[]{:S(2)}) collective-permute-start(bf16[128,896]{1,0:T(8,128)(2,1)} %bitcast.303), channel_id=1, source_target_pairs={{0,8},{8,16},{16,24},{24,0},{1,9},{9,17},{17,25},{25,1},{2,10},{10... | collective-permute-start | bytes 688136 | tf_op jit(solution)/shard_map/ppermute | solution.py:20
  33.9 26.3 %collective-permute-done = bf16[128,896]{1,0:T(8,128)(2,1)S(1)} collective-permute-done((bf16[128,896]{1,0:T(8,128)(2,1)}, bf16[128,896]{1,0:T(8,128)(2,1)S(1)}, u32[]{:S(2)}, u32[]{:S(2)}) %collective-permute-start) | collective-permute-done | bytes 229408 | tf_op jit(solution)/shard_map/ppermute | solution.py:20
  60.4 1.0 constant_dynamic-slice_fusion.34
  61.5 58.1 %all-gather.3.cloned.1.call-done = bf16[2048,896]{1,0:T(8,128)(2,1)} async-done(((bf16[512,896]{1,0:T(8,128)(2,1)}), bf16[2048,896]{1,0:T(8,128)(2,1)}) %all-gather.3.cloned.1.call-update) | async-done | bytes 3670032 | tf_op jit(solution)/shard_map/all_gather | solution.py:76
  119.6 4.1 convolution_convert_fusion
  123.7 2.5 copy.12
  126.2 8.1 %all-to-all-start = ((bf16[32,64,448]{2,1,0:T(8,128)(2,1)}), bf16[32,64,448]{2,1,0:T(8,128)(2,1)S(1)}, u32[]{:S(2)}, u32[]{:S(2)}) async-start(bf16[32,64,448]{2,1,0:T(8,128)(2,1)} %bitcast.298), calls=%async_computation | async-start | bytes 4194304 | tf_op jit(solution)/shard_map/all_to_all | solution.py:81
  134.3 49.7 %all-to-all-done = bf16[32,64,448]{2,1,0:T(8,128)(2,1)S(1)} async-done(((bf16[32,64,448]{2,1,0:T(8,128)(2,1)}), bf16[32,64,448]{2,1,0:T(8,128)(2,1)S(1)}, u32[]{:S(2)}, u32[]{:S(2)}) %all-to-all-start) | async-done | bytes 1835040 | tf_op jit(solution)/shard_map/all_to_all | solution.py:81
  184.5 2.6 collective-permute-start.3
  187.1 3.4 collective-permute-start.4
  190.5 2.2 collective-permute-start.5
  192.9 3.1 collective-permute-done.5
  196.1 5.4 %collective-permute-start.6 = (f32[64]{0:T(128)S(1)}, f32[64]{0:T(128)S(1)}, u32[]{:S(2)}, u32[]{:S(2)}) collective-permute-start(f32[64]{0:T(128)S(1)} %fusion.73), channel_id=1, source_target_pairs={{0,24},{8,0},{16,8},{24,16},{1,25},{9,1},{17,9},{25,17},{2,26},{10... | collective-permute-start | bytes 776 | tf_op jit(solution)/shard_map/ppermute | solution.py:20
  201.5 9.0 %collective-permute-start.7 = (f32[64]{0:T(128)S(1)}, f32[64]{0:T(128)S(1)}, u32[]{:S(2)}, u32[]{:S(2)}) collective-permute-start(f32[64]{0:T(128)S(1)} %fusion.73), channel_id=1, source_target_pairs={{0,16},{8,24},{16,0},{24,8},{1,17},{9,25},{17,1},{25,9},{2,18},{10... | collective-permute-start | bytes 776 | tf_op jit(solution)/shard_map/ppermute | solution.py:20
  210.5 4.7 collective-permute-start.8
  215.2 3.5 collective-permute-done.8
  219.1 58.2 %all_to_all.18 = bf16[32,64,448]{2,1,0:T(8,128)(2,1)S(1)} all-to-all(bf16[32,64,448]{2,1,0:T(8,128)(2,1)S(1)} %broadcast_in_dim.6), channel_id=1, replica_groups=mesh['segment'=4,'y'=4,'zhi'=4,'zlo'=4,'core'=2] {'segment','zlo','core'}, dimensions={0} | all-to-all | bytes 3670016 | tf_op jit(solution)/shard_map/all_to_all | solution.py:94
  277.3 3.2 fusion.68
  281.4 43.2 %reduce-scatter.2.cloned.1.call-done = f32[512,500]{0,1:T(8,128)} async-done(((f32[2048,500]{0,1:T(8,128)}), f32[512,500]{0,1:T(8,128)}) %reduce-scatter.2.cloned.1.call-update) | async-done | bytes 1024016 | tf_op jit(solution)/shard_map/reduce_scatter | solution.py:99
  324.6 2.0 constant_dynamic-slice_fusion.31
  326.6 12.5 %collective-permute-start.10 = (f32[128,500]{0,1:T(8,128)}, f32[128,500]{0,1:T(8,128)}, u32[]{:S(2)}, u32[]{:S(2)}) collective-permute-start(f32[128,500]{0,1:T(8,128)} %get-tuple-element.17), channel_id=1, source_target_pairs={{0,16},{8,24},{16,0},{24,8},{1,17},{9,25},{17,1},{25,9},{2,18},{10... | collective-permute-start | bytes 768008 | tf_op jit(solution)/shard_map/ppermute | solution.py:42
  339.1 1.9 collective-permute-start.11
  341.1 7.3 %collective-permute-start.9 = (f32[128,500]{0,1:T(8,128)S(1)}, f32[128,500]{0,1:T(8,128)}, u32[]{:S(2)}, u32[]{:S(2)}) collective-permute-start(f32[128,500]{0,1:T(8,128)S(1)} %get-tuple-element.15), channel_id=1, source_target_pairs={{0,8},{8,16},{16,24},{24,0},{1,9},{9,17},{17,25},{25,1},{2,10},{10... | collective-permute-start | bytes 768008 | tf_op jit(solution)/shard_map/ppermute | solution.py:42
  348.4 3.5 collective-permute-done.10
  352.0 33.5 %collective-permute-done.11 = f32[128,500]{0,1:T(8,128)} collective-permute-done((f32[128,500]{0,1:T(8,128)S(1)}, f32[128,500]{0,1:T(8,128)}, u32[]{:S(2)}, u32[]{:S(2)}) %collective-permute-start.11) | collective-permute-done | bytes 256032 | tf_op jit(solution)/shard_map/ppermute | solution.py:42
  385.5 1.4 fusion.67
  387.3 4.2 collective-permute-start.12
  391.6 2.6 collective-permute-start.13
  394.1 2.4 collective-permute-start.14
  397.4 2.3 collective-permute-done.14
  399.8 4.0 collective-permute-start.15
  403.9 1.9 collective-permute-start.16
  405.8 2.2 collective-permute-start.17
  408.0 1.1 collective-permute-done.16
  409.1 2.8 collective-permute-done.17
  412.1 5.6 %collective-permute-start.18 = (f32[3,128]{1,0:T(4,128)S(1)}, f32[3,128]{1,0:T(4,128)S(1)}, u32[]{:S(2)}, u32[]{:S(2)}) collective-permute-start(f32[3,128]{1,0:T(4,128)S(1)} %get-tuple-element.35), channel_id=1, source_target_pairs={{0,1},{1,0},{2,3},{3,2},{4,5},{5,4},{6,7},{7,6},{8,9},{9,8},{10,11... | collective-permute-start | bytes 4616 | tf_op jit(solution)/shard_map/ppermute | solution.py:20
  418.9 5.3 %collective-permute-start.19 = (bf16[128,504]{0,1:T(8,128)(2,1)S(1)}, bf16[128,504]{0,1:T(8,128)(2,1)S(1)}, u32[]{:S(2)}, u32[]{:S(2)}) collective-permute-start(bf16[128,504]{0,1:T(8,128)(2,1)S(1)} %concatenate.37), channel_id=1, source_target_pairs={{0,24},{8,0},{16,8},{24,16},{1,25},{9,1},{17,9},{25,17},{2,26},{10... | collective-permute-start | bytes 387080 | tf_op jit(solution)/shard_map/ppermute | solution.py:20
  424.3 8.4 %collective-permute-start.20 = (bf16[128,504]{0,1:T(8,128)(2,1)S(1)}, bf16[128,504]{0,1:T(8,128)(2,1)S(1)}, u32[]{:S(2)}, u32[]{:S(2)}) collective-permute-start(bf16[128,504]{0,1:T(8,128)(2,1)S(1)} %concatenate.37), channel_id=1, source_target_pairs={{0,16},{8,24},{16,0},{24,8},{1,17},{9,25},{17,1},{25,9},{2,18},{10... | collective-permute-start | bytes 387080 | tf_op jit(solution)/shard_map/ppermute | solution.py:20
  432.7 1.9 collective-permute-start.21
  434.6 2.7 collective-permute-done.19
  437.4 12.1 %collective-permute-done.20 = bf16[128,504]{0,1:T(8,128)(2,1)S(1)} collective-permute-done((bf16[128,504]{0,1:T(8,128)(2,1)S(1)}, bf16[128,504]{0,1:T(8,128)(2,1)S(1)}, u32[]{:S(2)}, u32[]{:S(2)}) %collective-permute-start.20) | collective-permute-done | bytes 129056 | tf_op jit(solution)/shard_map/ppermute | solution.py:20
  449.5 6.1 %collective-permute-done.21 = bf16[128,504]{0,1:T(8,128)(2,1)S(1)} collective-permute-done((bf16[128,504]{0,1:T(8,128)(2,1)S(1)}, bf16[128,504]{0,1:T(8,128)(2,1)S(1)}, u32[]{:S(2)}, u32[]{:S(2)}) %collective-permute-start.21) | collective-permute-done | bytes 129056 | tf_op jit(solution)/shard_map/ppermute | solution.py:20
  455.8 1.0 copy.13
  456.8 31.1 %all-gather.5.cloned.1.call-done = bf16[2048,504]{1,0:T(8,128)(2,1)} async-done(((bf16[512,504]{1,0:T(8,128)(2,1)}), bf16[2048,504]{1,0:T(8,128)(2,1)}) %all-gather.5.cloned.1.call-update) | async-done | bytes 2064400 | tf_op jit(solution)/shard_map/all_gather | solution.py:146
  487.9 2.7 convert_reduce_fusion.1
  491.9 3.7 fusion
  (99 shorter events, 6.1 us)
Async XLA Ops:
  7.2 112.4 %copy-start = (bf16[1,896,448]{1,2,0:T(8,128)(2,1)S(1)}, bf16[1,896,448]{1,2,0:T(8,128)(2,1)}, u32[]{:S(2)}) copy-start(bf16[1,896,448]{1,2,0:T(8,128)(2,1)} %param.9) | copy-start | bytes 2408452
  7.2 53.1 %copy-start.1 = (bf16[1,128,896]{2,1,0:T(8,128)(2,1)S(1)}, bf16[1,128,896]{2,1,0:T(8,128)(2,1)}, u32[]{:S(2)}) copy-start(bf16[1,128,896]{2,1,0:T(8,128)(2,1)} %param.8) | copy-start | bytes 688132
  7.2 112.4 %all-gather.3.cloned.1.call-start = ((), (), s32[]{:S(2)}) async-start(), calls=%async_computation.3 | async-start | bytes 4587520 | tf_op jit(solution)/shard_map/all_gather | solution.py:76
  7.2 52.9 %collective-permute-start = (bf16[128,896]{1,0:T(8,128)(2,1)}, bf16[128,896]{1,0:T(8,128)(2,1)S(1)}, u32[]{:S(2)}, u32[]{:S(2)}) collective-permute-start(bf16[128,896]{1,0:T(8,128)(2,1)} %bitcast.301), channel_id=1, source_target_pairs={{0,24},{8,0},{16,8},{24,16},{1,25},{9,1},{17,9},{25,17},{2,26},{10... | collective-permute-start | bytes 688136 | tf_op jit(solution)/shard_map/ppermute | solution.py:20
  20.7 39.5 %collective-permute-start.1 = (bf16[128,896]{1,0:T(8,128)(2,1)}, bf16[128,896]{1,0:T(8,128)(2,1)S(1)}, u32[]{:S(2)}, u32[]{:S(2)}) collective-permute-start(bf16[128,896]{1,0:T(8,128)(2,1)} %bitcast.302), channel_id=1, source_target_pairs={{0,16},{8,24},{16,0},{24,8},{1,17},{9,25},{17,1},{25,9},{2,18},{10... | collective-permute-start | bytes 688136 | tf_op jit(solution)/shard_map/ppermute | solution.py:20
  25.6 34.7 %collective-permute-start.2 = (bf16[128,896]{1,0:T(8,128)(2,1)}, bf16[128,896]{1,0:T(8,128)(2,1)S(1)}, u32[]{:S(2)}, u32[]{:S(2)}) collective-permute-start(bf16[128,896]{1,0:T(8,128)(2,1)} %bitcast.303), channel_id=1, source_target_pairs={{0,8},{8,16},{16,24},{24,0},{1,9},{9,17},{17,25},{25,1},{2,10},{10... | collective-permute-start | bytes 688136 | tf_op jit(solution)/shard_map/ppermute | solution.py:20
  126.2 57.8 %all-to-all-start = ((bf16[32,64,448]{2,1,0:T(8,128)(2,1)}), bf16[32,64,448]{2,1,0:T(8,128)(2,1)S(1)}, u32[]{:S(2)}, u32[]{:S(2)}) async-start(bf16[32,64,448]{2,1,0:T(8,128)(2,1)} %bitcast.298), calls=%async_computation | async-start | bytes 4194304 | tf_op jit(solution)/shard_map/all_to_all | solution.py:81
  134.3 84.5 %copy-start.6 = (f32[448]{0:T(512)S(1)}, f32[448]{0:T(512)}, u32[]{:S(2)}) copy-start(f32[448]{0:T(512)} %param.10) | copy-start | bytes 5380
  134.3 190.4 %reduce-scatter.2.cloned.1.call-start = ((), (), s32[]{:S(2)}) async-start(), calls=%async_computation.4 | async-start | bytes 5160960 | tf_op jit(solution)/shard_map/reduce_scatter | solution.py:99
  184.5 8.3 %collective-permute-start.3 = (f32[64]{0:T(128)S(1)}, f32[64]{0:T(128)S(1)}, u32[]{:S(2)}, u32[]{:S(2)}) collective-permute-start(f32[64]{0:T(128)S(1)} %multiply_reduce_fusion.1), channel_id=1, source_target_pairs={{0,96},{32,0},{64,32},{96,64},{1,97},{33,1},{65,33},{97,65},{2,98}... | collective-permute-start | bytes 776 | tf_op jit(solution)/shard_map/ppermute | solution.py:20
  187.1 5.8 %collective-permute-start.4 = (f32[64]{0:T(128)S(1)}, f32[64]{0:T(128)S(1)}, u32[]{:S(2)}, u32[]{:S(2)}) collective-permute-start(f32[64]{0:T(128)S(1)} %multiply_reduce_fusion.1), channel_id=1, source_target_pairs={{0,64},{32,96},{64,0},{96,32},{1,65},{33,97},{65,1},{97,33},{2,66}... | collective-permute-start | bytes 776 | tf_op jit(solution)/shard_map/ppermute | solution.py:20
  190.5 5.5 %collective-permute-start.5 = (f32[64]{0:T(128)S(1)}, f32[64]{0:T(128)S(1)}, u32[]{:S(2)}, u32[]{:S(2)}) collective-permute-start(f32[64]{0:T(128)S(1)} %multiply_reduce_fusion.1), channel_id=1, source_target_pairs={{0,32},{32,64},{64,96},{96,0},{1,33},{33,65},{65,97},{97,1},{2,34}... | collective-permute-start | bytes 776 | tf_op jit(solution)/shard_map/ppermute | solution.py:20
  196.1 19.1 %collective-permute-start.6 = (f32[64]{0:T(128)S(1)}, f32[64]{0:T(128)S(1)}, u32[]{:S(2)}, u32[]{:S(2)}) collective-permute-start(f32[64]{0:T(128)S(1)} %fusion.73), channel_id=1, source_target_pairs={{0,24},{8,0},{16,8},{24,16},{1,25},{9,1},{17,9},{25,17},{2,26},{10... | collective-permute-start | bytes 776 | tf_op jit(solution)/shard_map/ppermute | solution.py:20
  201.5 13.7 %collective-permute-start.7 = (f32[64]{0:T(128)S(1)}, f32[64]{0:T(128)S(1)}, u32[]{:S(2)}, u32[]{:S(2)}) collective-permute-start(f32[64]{0:T(128)S(1)} %fusion.73), channel_id=1, source_target_pairs={{0,16},{8,24},{16,0},{24,8},{1,17},{9,25},{17,1},{25,9},{2,18},{10... | collective-permute-start | bytes 776 | tf_op jit(solution)/shard_map/ppermute | solution.py:20
  210.5 8.2 %collective-permute-start.8 = (f32[64]{0:T(128)S(1)}, f32[64]{0:T(128)S(1)}, u32[]{:S(2)}, u32[]{:S(2)}) collective-permute-start(f32[64]{0:T(128)S(1)} %fusion.73), channel_id=1, source_target_pairs={{0,8},{8,16},{16,24},{24,0},{1,9},{9,17},{17,25},{25,1},{2,10},{10... | collective-permute-start | bytes 776 | tf_op jit(solution)/shard_map/ppermute | solution.py:20
  219.1 58.2 %copy-start.2 = (bf16[448,500]{1,0:T(8,128)(2,1)S(1)}, bf16[448,500]{1,0:T(8,128)(2,1)}, u32[]{:S(2)}) copy-start(bf16[448,500]{1,0:T(8,128)(2,1)} %param.11) | copy-start | bytes 1344004
  280.5 0.7 copy-start.7
  280.5 0.9 copy-start.5
  280.5 67.9 %copy-start.3 = (f32[128,8]{0,1:T(8,128)S(1)}, f32[128,8]{0,1:T(8,128)}, u32[]{:S(2)}) copy-start(f32[128,8]{0,1:T(8,128)} %param.15) | copy-start | bytes 12292
  280.5 106.5 %copy-start.4 = (s32[128]{0:T(128)S(1)}, s32[128]{0:T(128)}, u32[]{:S(2)}) copy-start(s32[128]{0:T(128)} %param.13) | copy-start | bytes 1540
  280.5 207.4 %all-gather.5.cloned.1.call-start = ((), (), s32[]{:S(2)}) async-start(), calls=%async_computation.5 | async-start | bytes 2621440 | tf_op jit(solution)/shard_map/all_gather | solution.py:146
  326.6 25.4 %collective-permute-start.10 = (f32[128,500]{0,1:T(8,128)}, f32[128,500]{0,1:T(8,128)}, u32[]{:S(2)}, u32[]{:S(2)}) collective-permute-start(f32[128,500]{0,1:T(8,128)} %get-tuple-element.17), channel_id=1, source_target_pairs={{0,16},{8,24},{16,0},{24,8},{1,17},{9,25},{17,1},{25,9},{2,18},{10... | collective-permute-start | bytes 768008 | tf_op jit(solution)/shard_map/ppermute | solution.py:42
  339.1 46.3 %collective-permute-start.11 = (f32[128,500]{0,1:T(8,128)S(1)}, f32[128,500]{0,1:T(8,128)}, u32[]{:S(2)}, u32[]{:S(2)}) collective-permute-start(f32[128,500]{0,1:T(8,128)S(1)} %get-tuple-element.16), channel_id=1, source_target_pairs={{0,24},{8,0},{16,8},{24,16},{1,25},{9,1},{17,9},{25,17},{2,26},{10... | collective-permute-start | bytes 768008 | tf_op jit(solution)/shard_map/ppermute | solution.py:42
  341.1 44.4 %collective-permute-start.9 = (f32[128,500]{0,1:T(8,128)S(1)}, f32[128,500]{0,1:T(8,128)}, u32[]{:S(2)}, u32[]{:S(2)}) collective-permute-start(f32[128,500]{0,1:T(8,128)S(1)} %get-tuple-element.15), channel_id=1, source_target_pairs={{0,8},{8,16},{16,24},{24,0},{1,9},{9,17},{17,25},{25,1},{2,10},{10... | collective-permute-start | bytes 768008 | tf_op jit(solution)/shard_map/ppermute | solution.py:42
  387.3 9.3 %collective-permute-start.12 = (f32[3,128]{1,0:T(4,128)S(1)}, f32[3,128]{1,0:T(4,128)S(1)}, u32[]{:S(2)}, u32[]{:S(2)}) collective-permute-start(f32[3,128]{1,0:T(4,128)S(1)} %pad_maximum_fusion), channel_id=1, source_target_pairs={{0,384},{128,0},{256,128},{384,256},{1,385},{129,1},{257,129},{385... | collective-permute-start | bytes 4616 | tf_op jit(solution)/shard_map/ppermute | solution.py:20
  391.6 5.8 %collective-permute-start.13 = (f32[3,128]{1,0:T(4,128)S(1)}, f32[3,128]{1,0:T(4,128)S(1)}, u32[]{:S(2)}, u32[]{:S(2)}) collective-permute-start(f32[3,128]{1,0:T(4,128)S(1)} %pad_maximum_fusion), channel_id=1, source_target_pairs={{0,256},{128,384},{256,0},{384,128},{1,257},{129,385},{257,1},{385... | collective-permute-start | bytes 4616 | tf_op jit(solution)/shard_map/ppermute | solution.py:20
  394.1 5.5 %collective-permute-start.14 = (f32[3,128]{1,0:T(4,128)S(1)}, f32[3,128]{1,0:T(4,128)S(1)}, u32[]{:S(2)}, u32[]{:S(2)}) collective-permute-start(f32[3,128]{1,0:T(4,128)S(1)} %pad_maximum_fusion), channel_id=1, source_target_pairs={{0,128},{128,256},{256,384},{384,0},{1,129},{129,257},{257,385},{3... | collective-permute-start | bytes 4616 | tf_op jit(solution)/shard_map/ppermute | solution.py:20
  399.8 8.2 %collective-permute-start.15 = (f32[3,128]{1,0:T(4,128)S(1)}, f32[3,128]{1,0:T(4,128)S(1)}, u32[]{:S(2)}, u32[]{:S(2)}) collective-permute-start(f32[3,128]{1,0:T(4,128)S(1)} %pad_maximum_fusion.1), channel_id=1, source_target_pairs={{0,6},{2,0},{4,2},{6,4},{1,7},{3,1},{5,3},{7,5},{8,14},{10,8},{12,... | collective-permute-start | bytes 4616 | tf_op jit(solution)/shard_map/ppermute | solution.py:20
  403.9 5.2 %collective-permute-start.16 = (f32[3,128]{1,0:T(4,128)S(1)}, f32[3,128]{1,0:T(4,128)S(1)}, u32[]{:S(2)}, u32[]{:S(2)}) collective-permute-start(f32[3,128]{1,0:T(4,128)S(1)} %pad_maximum_fusion.1), channel_id=1, source_target_pairs={{0,4},{2,6},{4,0},{6,2},{1,5},{3,7},{5,1},{7,3},{8,12},{10,14},{12... | collective-permute-start | bytes 4616 | tf_op jit(solution)/shard_map/ppermute | solution.py:20
  405.8 6.1 %collective-permute-start.17 = (f32[3,128]{1,0:T(4,128)S(1)}, f32[3,128]{1,0:T(4,128)S(1)}, u32[]{:S(2)}, u32[]{:S(2)}) collective-permute-start(f32[3,128]{1,0:T(4,128)S(1)} %pad_maximum_fusion.1), channel_id=1, source_target_pairs={{0,2},{2,4},{4,6},{6,0},{1,3},{3,5},{5,7},{7,1},{8,10},{10,12},{12... | collective-permute-start | bytes 4616 | tf_op jit(solution)/shard_map/ppermute | solution.py:20
  412.1 6.4 %collective-permute-start.18 = (f32[3,128]{1,0:T(4,128)S(1)}, f32[3,128]{1,0:T(4,128)S(1)}, u32[]{:S(2)}, u32[]{:S(2)}) collective-permute-start(f32[3,128]{1,0:T(4,128)S(1)} %get-tuple-element.35), channel_id=1, source_target_pairs={{0,1},{1,0},{2,3},{3,2},{4,5},{5,4},{6,7},{7,6},{8,9},{9,8},{10,11... | collective-permute-start | bytes 4616 | tf_op jit(solution)/shard_map/ppermute | solution.py:20
  418.9 18.4 %collective-permute-start.19 = (bf16[128,504]{0,1:T(8,128)(2,1)S(1)}, bf16[128,504]{0,1:T(8,128)(2,1)S(1)}, u32[]{:S(2)}, u32[]{:S(2)}) collective-permute-start(bf16[128,504]{0,1:T(8,128)(2,1)S(1)} %concatenate.37), channel_id=1, source_target_pairs={{0,24},{8,0},{16,8},{24,16},{1,25},{9,1},{17,9},{25,17},{2,26},{10... | collective-permute-start | bytes 387080 | tf_op jit(solution)/shard_map/ppermute | solution.py:20
  424.3 25.2 %collective-permute-start.20 = (bf16[128,504]{0,1:T(8,128)(2,1)S(1)}, bf16[128,504]{0,1:T(8,128)(2,1)S(1)}, u32[]{:S(2)}, u32[]{:S(2)}) collective-permute-start(bf16[128,504]{0,1:T(8,128)(2,1)S(1)} %concatenate.37), channel_id=1, source_target_pairs={{0,16},{8,24},{16,0},{24,8},{1,17},{9,25},{17,1},{25,9},{2,18},{10... | collective-permute-start | bytes 387080 | tf_op jit(solution)/shard_map/ppermute | solution.py:20
  432.7 22.9 %collective-permute-start.21 = (bf16[128,504]{0,1:T(8,128)(2,1)S(1)}, bf16[128,504]{0,1:T(8,128)(2,1)S(1)}, u32[]{:S(2)}, u32[]{:S(2)}) collective-permute-start(bf16[128,504]{0,1:T(8,128)(2,1)S(1)} %concatenate.37), channel_id=1, source_target_pairs={{0,8},{8,16},{16,24},{24,0},{1,9},{9,17},{17,25},{25,1},{2,10},{10... | collective-permute-start | bytes 387080 | tf_op jit(solution)/shard_map/ppermute | solution.py:20
Sparse Core Ops, SparseCore 0:
  61.6 57.9 all-gather.2
  280.6 43.9 reduce-scatter.1
  457.0 30.8 all-gather.4

commit v3 on v2

v3 whole, which is shorter than its diff:
```python
import jax
import jax.numpy as jnp
from jax import lax
from jax.sharding import Mesh
from jax.sharding import PartitionSpec as P

D = 7168
VOCAB = 16000

norm_eps = 1e-06

SEQ = ("y", "zhi")
SM = ("segment", "zlo", "core")


def gather_axis(value, axis, size):
    got = [value]
    for shift in range(1, size):
        pairs = [(i, (i + shift) % size) for i in range(size)]
        got.append(lax.ppermute(value, axis, pairs))
    rotated = jnp.stack([got[0]] + got[1:][::-1])
    me = lax.axis_index(axis)
    doubled = jnp.concatenate([rotated, rotated], axis=0)
    return lax.dynamic_slice_in_dim(doubled, (size - me) % size, size, axis=0)


def reduce_axis(value, axis, size, combine):
    every = gather_axis(value, axis, size)
    total = every[0]
    for k in range(1, size):
        total = combine(total, every[k])
    return total


def scatter_sum_axis(value, axis, size):
    me = lax.axis_index(axis)
    part = value.shape[0] // size
    total = lax.dynamic_slice_in_dim(value, me * part, part, axis=0)
    for shift in range(1, size):
        pairs = [(i, (i + shift) % size) for i in range(size)]
        chunk = lax.dynamic_slice_in_dim(value, ((me + shift) % size) * part, part, axis=0)
        total = total + lax.ppermute(chunk, axis, pairs)
    return total


def gather_rows_axis(value, axis, size):
    every = gather_axis(value, axis, size)
    return every.reshape((size * value.shape[0],) + value.shape[1:])


def add(a, b):
    return a + b


def merge_stats(a, b):
    peak = jnp.maximum(a[0], b[0])
    total = a[1] * jnp.exp(a[0] - peak) + b[1] * jnp.exp(b[0] - peak)
    return jnp.stack([peak, total, a[2] + b[2]])


def half_pipeline(
    sources,
    unite_weight,
    norm_gain,
    head_weight,
    doc_lengths,
    target_ids,
    teacher_ids,
    teacher_probs,
    sizes,
    first,
    block,
):
    tok_local = sources.shape[1]
    n_sm = sizes["segment"] * sizes["zlo"] * sizes["core"]

    rows = gather_rows_axis(sources[0], "zhi", sizes["zhi"])
    rows = lax.all_gather(rows, "y", axis=0, tiled=True)
    tokens = rows.shape[0]
    product = jnp.dot(rows, unite_weight[0], preferred_element_type=jnp.float32)
    product = lax.optimization_barrier(product.astype(jnp.bfloat16))

    pieces = lax.all_to_all(product, SM, 0, 0, tiled=True)
    slice_len = tokens // n_sm
    united = jnp.sum(
        pieces.reshape(n_sm, slice_len, -1).astype(jnp.float32), axis=0
    )

    squares = jnp.sum(united * united, axis=1)
    squares = reduce_axis(squares, "y", sizes["y"], add)
    squares = reduce_axis(squares, "zhi", sizes["zhi"], add)
    hidden_part = (
        united * lax.rsqrt(squares / D + norm_eps)[:, None] * norm_gain[None, :]
    ).astype(jnp.bfloat16)
    spread = jnp.broadcast_to(hidden_part[None], (n_sm,) + hidden_part.shape)
    hidden = lax.all_to_all(
        spread.reshape(tokens, -1), SM, 0, 0, tiled=True
    )

    logits = jnp.dot(hidden, head_weight, preferred_element_type=jnp.float32)
    logits = lax.psum_scatter(logits, "y", scatter_dimension=0, tiled=True)
    logits = scatter_sum_axis(logits, "zhi", sizes["zhi"])

    seq_index = lax.axis_index("y") * sizes["zhi"] + lax.axis_index("zhi")
    positions = seq_index * block + first + jnp.arange(tok_local, dtype=jnp.int32)
    vocab_width = head_weight.shape[1]
    offset = lax.axis_index(SM) * vocab_width
    columns = offset + jnp.arange(vocab_width, dtype=jnp.int32)
    target_weight = (target_ids[:, None] == columns[None, :]).astype(jnp.float32)
    for top_slot in range(teacher_ids.shape[1]):
        hits = (teacher_ids[:, top_slot : top_slot + 1] == columns[None, :]).astype(
            jnp.float32
        )
        target_weight = target_weight + teacher_probs[:, top_slot : top_slot + 1] * hits

    row_peak = jnp.max(logits, axis=1)
    stats = jnp.stack(
        [
            row_peak,
            jnp.sum(jnp.exp(logits - row_peak[:, None]), axis=1),
            jnp.sum(target_weight * logits, axis=1),
        ]
    )
    for axis in SM:
        stats = reduce_axis(stats, axis, sizes[axis], merge_stats)
    lse = stats[0] + jnp.log(stats[1])
    picked = stats[2]

    target_mass = 1.0 + jnp.sum(teacher_probs, axis=1)
    doc_ends = jnp.cumsum(doc_lengths)
    is_last = jnp.any(positions[:, None] + 1 == doc_ends[None, :], axis=1)
    in_vocab = (target_ids < VOCAB).astype(jnp.float32)
    valid_rows = jnp.where(is_last, 0.0, in_vocab)
    per_token = valid_rows * (target_mass * lse - picked)
    loss_hi = per_token.astype(jnp.bfloat16)
    loss_lo = (per_token - loss_hi.astype(jnp.float32)).astype(jnp.bfloat16)

    logit_grad = (
        valid_rows[:, None]
        * (target_mass[:, None] * jnp.exp(logits - lse[:, None]) - target_weight)
    ).astype(jnp.bfloat16)
    extra = jnp.stack(
        [loss_hi, loss_lo, valid_rows.astype(jnp.bfloat16), jnp.zeros_like(loss_hi)],
        axis=1,
    )
    carried = jnp.concatenate([logit_grad, extra], axis=1)
    carried = gather_rows_axis(carried, "zhi", sizes["zhi"])
    carried = lax.all_gather(carried, "y", axis=0, tiled=True)

    loss_sum = jnp.sum(
        carried[:, vocab_width].astype(jnp.float32)
        + carried[:, vocab_width + 1].astype(jnp.float32)
    )
    count = jnp.sum(carried[:, vocab_width + 2].astype(jnp.float32))

    head_grad = lax.dot_general(
        hidden,
        carried[:, :vocab_width],
        (((0,), (0,)), ((), ())),
        preferred_element_type=jnp.float32,
    )
    return loss_sum, count, head_grad


def on_device(
    sources,
    unite_weight,
    norm_gain,
    head_weight,
    doc_lengths,
    target_ids,
    teacher_ids,
    teacher_probs,
    sizes,
    halves,
):
    block = sources.shape[1]
    width = block // halves
    loss_sum, count, head_grad = 0.0, 0.0, None
    for h in range(halves):
        cut = slice(h * width, (h + 1) * width)
        part_loss, part_count, part_grad = half_pipeline(
            sources[:, cut],
            unite_weight,
            norm_gain,
            head_weight,
            doc_lengths,
            target_ids[cut],
            teacher_ids[cut],
            teacher_probs[cut],
            sizes,
            h * width,
            block,
        )
        loss_sum = loss_sum + part_loss
        count = count + part_count
        head_grad = part_grad if head_grad is None else head_grad + part_grad
    mean_loss = loss_sum / jnp.maximum(count, 1.0)
    return (mean_loss, head_grad)


def solution(mesh):
    n_seg, n_seq, n_mp = (mesh.shape[a] for a in ("segment", "seq", "mp"))
    sizes = {"segment": n_seg, "y": n_seq // 4, "zhi": 4, "zlo": n_mp // 2, "core": 2}
    fine = Mesh(
        mesh.devices.reshape(n_seg, sizes["y"], sizes["zhi"], sizes["zlo"], sizes["core"]),
        ("segment", "y", "zhi", "zlo", "core"),
    )
    placed = (
        P("segment", SEQ, ("zlo", "core")),
        P("segment", ("zlo", "core"), SEQ),
        P(SEQ),
        P(SEQ, SM),
        P(),
        P(SEQ),
        P(SEQ, None),
        P(SEQ, None),
    )

    def body(*args):
        return on_device(*args, sizes=sizes, halves=2)

    return jax.shard_map(
        body,
        mesh=fine,
        in_specs=placed,
        out_specs=(P(), P(SEQ, SM)),
        check_vma=False,
    )
```

time: 504 us -> 580 us (1.15); the launches traced: 503 us -> 573 us
  waiting for transfers between devices: 281 us -> 162 us
  starting transfers between devices: 121 us -> 237 us
  blocking collectives: 58.2 us -> 92.6 us
  local copies, waits for them, and re-layouts: 8.82 us -> 37 us
  other arithmetic: 5.92 us -> 12.5 us
    ppermute x19 -> x38, starting transfers between devices: 91.5 us -> 180 us  [gather_axis(): got.append(lax.ppermute(value, axis, pairs))]
    ppermute x19 -> x38, waiting for transfers between devices: 61.7 us -> 28.8 us  [gather_axis(): got.append(lax.ppermute(value, axis, pairs))]
    all_to_all x1 -> x2, waiting for transfers between devices: 49.7 us -> 19.5 us  [half_pipeline(): pieces = lax.all_to_all(product, SM, 0, 0, tiled=True)]
    reduce_scatter x1 -> x2, waiting for transfers between devices: 43.2 us -> 16.1 us  [half_pipeline(): logits = lax.psum_scatter(logits, 'y', scatter_dimension=0, tiled=True)]
    all_gather x0 -> x2, blocking collectives: none -> 26.1 us  [half_pipeline(): carried = lax.all_gather(carried, 'y', axis=0, tiled=True)]
    ppermute x3 -> x6, starting transfers between devices: 21.7 us -> 40.3 us  [scatter_sum_axis(): total = total + lax.ppermute(chunk, axis, pairs)]
    all_gather x2, waiting for transfers between devices: 89.2 us -> 71.8 us  [half_pipeline(): rows = lax.all_gather(rows, 'y', axis=0, tiled=True)]
    unnamed x40 -> x103, local copies, waits for them, and re-layouts: 1.91 us -> 17.5 us
  transfers between devices with their start and end apart: 26 -> 50, of which waited for: 18 -> 11; matrix products, arithmetic and copies ran while one was open for 0% -> 7% of each run, Pallas kernels for 0% -> 0%
where the time goes in v3:
time: 580 us; the launch traced here: 573 us
  starting transfers between devices  237 us (41%)
  waiting for transfers between devices  162 us (28%)
  blocking collectives  92.6 us (16%)
  local copies, waits for them, and re-layouts  37 us (6%)
  between operations  18.9 us (3%)
  matrix products  12.6 us (2%)
  other arithmetic  12.5 us (2%)
    ppermute x38, starting transfers between devices, gather_axis(): got.append(lax.ppermute(value, axis, pairs))  180 us
    all_gather x2, waiting for transfers between devices, half_pipeline(): rows = lax.all_gather(rows, 'y', axis=0, tiled=True)  71.8 us
    all_to_all x2, blocking collectives, half_pipeline(): hidden = lax.all_to_all(spread.reshape(tokens, -1), SM, 0, 0, tiled=True)  66.5 us
    ppermute x6, starting transfers between devices, scatter_sum_axis(): total = total + lax.ppermute(chunk, axis, pairs)  40.3 us
    ppermute x38, waiting for transfers between devices, gather_axis(): got.append(lax.ppermute(value, axis, pairs))  28.8 us
    ppermute x6, waiting for transfers between devices, scatter_sum_axis(): total = total + lax.ppermute(chunk, axis, pairs)  26.1 us
    all_gather x2, blocking collectives, half_pipeline(): carried = lax.all_gather(carried, 'y', axis=0, tiled=True)  26.1 us
    all_to_all x2, waiting for transfers between devices, half_pipeline(): pieces = lax.all_to_all(product, SM, 0, 0, tiled=True)  19.5 us
  transfers between devices with their start and end apart: 50, of which 11 were waited for; matrix products, arithmetic and copies ran while one was open for 7% of the time, Pallas kernels for 0%

profile of v3, /device:TPU:1, one launch (start us, length us, event | category | flops | bytes accessed | tf_op | source)
XLA Modules:
  0.0 572.6 jit_solution(2206102510339182477)
XLA Ops:
  9.0 13.3 %collective-permute-start = (bf16[64,896]{1,0:T(8,128)(2,1)S(1)}, bf16[64,896]{1,0:T(8,128)(2,1)S(1)}, u32[]{:S(2)}, u32[]{:S(2)}) collective-permute-start(bf16[64,896]{1,0:T(8,128)(2,1)S(1)} %get-tuple-element.43), channel_id=1, source_target_pairs={{0,24},{8,0},{16,8},{24,16},{1,25},{9,1},{17,9},{25,17},{2,26},{10... | collective-permute-start | bytes 344072 | tf_op jit(solution)/shard_map/ppermute | solution.py:20
  22.3 4.9 collective-permute-start.1
  27.2 7.3 %collective-permute-start.2 = (bf16[64,896]{1,0:T(8,128)(2,1)S(1)}, bf16[64,896]{1,0:T(8,128)(2,1)S(1)}, u32[]{:S(2)}, u32[]{:S(2)}) collective-permute-start(bf16[64,896]{1,0:T(8,128)(2,1)S(1)} %get-tuple-element.43), channel_id=1, source_target_pairs={{0,8},{8,16},{16,24},{24,0},{1,9},{9,17},{17,25},{25,1},{2,10},{10... | collective-permute-start | bytes 344072 | tf_op jit(solution)/shard_map/ppermute | solution.py:20
  36.4 9.1 %collective-permute-start.23 = (bf16[64,896]{1,0:T(8,128)(2,1)S(1)}, bf16[64,896]{1,0:T(8,128)(2,1)S(1)}, u32[]{:S(2)}, u32[]{:S(2)}) collective-permute-start(bf16[64,896]{1,0:T(8,128)(2,1)S(1)} %get-tuple-element.40), channel_id=1, source_target_pairs={{0,16},{8,24},{16,0},{24,8},{1,17},{9,25},{17,1},{25,9},{2,18},{10... | collective-permute-start | bytes 344072 | tf_op jit(solution)/shard_map/ppermute | solution.py:20
  49.4 14.9 %collective-permute-done.22 = bf16[64,896]{1,0:T(8,128)(2,1)S(1)} collective-permute-done((bf16[64,896]{1,0:T(8,128)(2,1)S(1)}, bf16[64,896]{1,0:T(8,128)(2,1)S(1)}, u32[]{:S(2)}, u32[]{:S(2)}) %collective-permute-start.22) | collective-permute-done | bytes 114720 | tf_op jit(solution)/shard_map/ppermute | solution.py:20
  64.3 7.1 %collective-permute-done.23 = bf16[64,896]{1,0:T(8,128)(2,1)S(1)} collective-permute-done((bf16[64,896]{1,0:T(8,128)(2,1)S(1)}, bf16[64,896]{1,0:T(8,128)(2,1)S(1)}, u32[]{:S(2)}, u32[]{:S(2)}) %collective-permute-start.23) | collective-permute-done | bytes 114720 | tf_op jit(solution)/shard_map/ppermute | solution.py:20
  76.0 35.3 %all-gather.3.cloned.1.call-done = bf16[1024,896]{1,0:T(8,128)(2,1)} async-done(((bf16[256,896]{1,0:T(8,128)(2,1)}), bf16[1024,896]{1,0:T(8,128)(2,1)}) %all-gather.3.cloned.1.call-update) | async-done | bytes 1835024 | tf_op jit(solution)/shard_map/all_gather | solution.py:78
  115.3 8.1 %all-to-all-start = ((bf16[32,32,448]{2,1,0:T(8,128)(2,1)}), bf16[32,32,448]{2,1,0:T(8,128)(2,1)S(1)}, u32[]{:S(2)}, u32[]{:S(2)}) async-start(bf16[32,32,448]{2,1,0:T(8,128)(2,1)} %bitcast.8), calls=%async_computation | async-start | bytes 2097152 | tf_op jit(solution)/shard_map/all_to_all | solution.py:83
  124.3 36.5 %all-gather.5.cloned.1.call-done = bf16[1024,896]{1,0:T(8,128)(2,1)} async-done(((bf16[256,896]{1,0:T(8,128)(2,1)}), bf16[1024,896]{1,0:T(8,128)(2,1)}) %all-gather.5.cloned.1.call-update) | async-done | bytes 1835024 | tf_op jit(solution)/shard_map/all_gather | solution.py:78
  160.7 2.6 convolution_convert_fusion
  164.7 8.2 %all-to-all-start.2 = ((bf16[32,32,448]{2,1,0:T(8,128)(2,1)}), bf16[32,32,448]{2,1,0:T(8,128)(2,1)S(1)}, u32[]{:S(2)}, u32[]{:S(2)}) async-start(bf16[32,32,448]{2,1,0:T(8,128)(2,1)} %bitcast.586), calls=%async_computation.3 | async-start | bytes 2097152 | tf_op jit(solution)/shard_map/all_to_all | solution.py:83
  173.3 2.6 collective-permute-start.3
  175.9 3.1 collective-permute-start.4
  181.3 19.5 %all-to-all-done.2 = bf16[32,32,448]{2,1,0:T(8,128)(2,1)S(1)} async-done(((bf16[32,32,448]{2,1,0:T(8,128)(2,1)}), bf16[32,32,448]{2,1,0:T(8,128)(2,1)S(1)}, u32[]{:S(2)}, u32[]{:S(2)}) %all-to-all-start.2) | async-done | bytes 917536 | tf_op jit(solution)/shard_map/all_to_all | solution.py:83
  201.1 2.8 collective-permute-start.25
  203.9 3.1 collective-permute-start.26
  209.3 5.4 collective-permute-start.6
  214.7 9.0 %collective-permute-start.7 = (f32[32]{0:T(128)S(1)}, f32[32]{0:T(128)S(1)}, u32[]{:S(2)}, u32[]{:S(2)}) collective-permute-start(f32[32]{0:T(128)S(1)} %fusion.146), channel_id=1, source_target_pairs={{0,16},{8,24},{16,0},{24,8},{1,17},{9,25},{17,1},{25,9},{2,18},{10... | collective-permute-start | bytes 392 | tf_op jit(solution)/shard_map/ppermute | solution.py:20
  223.7 4.7 collective-permute-start.8
  228.5 4.5 collective-permute-start.28
  233.0 5.0 collective-permute-start.29
  238.1 3.9 collective-permute-start.30
  242.1 3.9 collective-permute-done.29
  246.5 34.9 %all_to_all.36 = bf16[32,32,448]{2,1,0:T(8,128)(2,1)S(1)} all-to-all(bf16[32,32,448]{2,1,0:T(8,128)(2,1)S(1)} %broadcast_in_dim.9), channel_id=1, replica_groups=mesh['segment'=4,'y'=4,'zhi'=4,'zlo'=4,'core'=2] {'segment','zlo','core'}, dimensions={0} | all-to-all | bytes 1835008 | tf_op jit(solution)/shard_map/all_to_all | solution.py:96
  283.7 31.5 %all_to_all.37 = bf16[32,32,448]{2,1,0:T(8,128)(2,1)S(1)} all-to-all(bf16[32,32,448]{2,1,0:T(8,128)(2,1)S(1)} %broadcast_in_dim.10), channel_id=1, replica_groups=mesh['segment'=4,'y'=4,'zhi'=4,'zlo'=4,'core'=2] {'segment','zlo','core'}, dimensions={0} | all-to-all | bytes 1835008 | tf_op jit(solution)/shard_map/all_to_all | solution.py:96
  322.0 9.4 %collective-permute-start.10 = (f32[64,500]{0,1:T(8,128)}, f32[64,500]{0,1:T(8,128)}, u32[]{:S(2)}, u32[]{:S(2)}) collective-permute-start(f32[64,500]{0,1:T(8,128)} %get-tuple-element.37), channel_id=1, source_target_pairs={{0,16},{8,24},{16,0},{24,8},{1,17},{9,25},{17,1},{25,9},{2,18},{10... | collective-permute-start | bytes 384008 | tf_op jit(solution)/shard_map/ppermute | solution.py:42
  333.4 7.3 %collective-permute-start.9 = (f32[64,500]{0,1:T(8,128)S(1)}, f32[64,500]{0,1:T(8,128)}, u32[]{:S(2)}, u32[]{:S(2)}) collective-permute-start(f32[64,500]{0,1:T(8,128)S(1)} %get-tuple-element.35), channel_id=1, source_target_pairs={{0,8},{8,16},{16,24},{24,0},{1,9},{9,17},{17,25},{25,1},{2,10},{10... | collective-permute-start | bytes 384008 | tf_op jit(solution)/shard_map/ppermute | solution.py:42
  340.6 16.0 %reduce-scatter.5.cloned.1.call-done = f32[256,500]{0,1:T(8,128)} async-done(((f32[1024,500]{0,1:T(8,128)}), f32[256,500]{0,1:T(8,128)}) %reduce-scatter.5.cloned.1.call-update) | async-done | bytes 512016 | tf_op jit(solution)/shard_map/reduce_scatter | solution.py:101
  359.0 7.3 %collective-permute-start.31 = (f32[64,500]{0,1:T(8,128)}, f32[64,500]{0,1:T(8,128)}, u32[]{:S(2)}, u32[]{:S(2)}) collective-permute-start(f32[64,500]{0,1:T(8,128)} %get-tuple-element.32), channel_id=1, source_target_pairs={{0,8},{8,16},{16,24},{24,0},{1,9},{9,17},{17,25},{25,1},{2,10},{10... | collective-permute-start | bytes 384008 | tf_op jit(solution)/shard_map/ppermute | solution.py:42
  366.3 7.7 %collective-permute-start.32 = (f32[64,500]{0,1:T(8,128)}, f32[64,500]{0,1:T(8,128)}, u32[]{:S(2)}, u32[]{:S(2)}) collective-permute-start(f32[64,500]{0,1:T(8,128)} %get-tuple-element.34), channel_id=1, source_target_pairs={{0,16},{8,24},{16,0},{24,8},{1,17},{9,25},{17,1},{25,9},{2,18},{10... | collective-permute-start | bytes 384008 | tf_op jit(solution)/shard_map/ppermute | solution.py:42
  374.1 6.6 %collective-permute-start.33 = (f32[64,500]{0,1:T(8,128)}, f32[64,500]{0,1:T(8,128)}, u32[]{:S(2)}, u32[]{:S(2)}) collective-permute-start(f32[64,500]{0,1:T(8,128)} %get-tuple-element.33), channel_id=1, source_target_pairs={{0,24},{8,0},{16,8},{24,16},{1,25},{9,1},{17,9},{25,17},{2,26},{10... | collective-permute-start | bytes 384008 | tf_op jit(solution)/shard_map/ppermute | solution.py:42
  381.4 8.6 %collective-permute-done.32 = f32[64,500]{0,1:T(8,128)} collective-permute-done((f32[64,500]{0,1:T(8,128)}, f32[64,500]{0,1:T(8,128)}, u32[]{:S(2)}, u32[]{:S(2)}) %collective-permute-start.32) | collective-permute-done | bytes 128032 | tf_op jit(solution)/shard_map/ppermute | solution.py:42
  389.9 17.5 %collective-permute-done.33 = f32[64,500]{0,1:T(8,128)} collective-permute-done((f32[64,500]{0,1:T(8,128)}, f32[64,500]{0,1:T(8,128)}, u32[]{:S(2)}, u32[]{:S(2)}) %collective-permute-start.33) | collective-permute-done | bytes 128032 | tf_op jit(solution)/shard_map/ppermute | solution.py:42
  410.4 21.7 %collective-permute-start.12 = (f32[3,64]{1,0:T(4,128)S(1)}, f32[3,64]{1,0:T(4,128)S(1)}, u32[]{:S(2)}, u32[]{:S(2)}) collective-permute-start(f32[3,64]{1,0:T(4,128)S(1)} %pad_maximum_fusion), channel_id=1, source_target_pairs={{0,384},{128,0},{256,128},{384,256},{1,385},{129,1},{257,129},{385... | collective-permute-start | bytes 2312 | tf_op jit(solution)/shard_map/ppermute | solution.py:20
  437.8 4.0 collective-permute-start.34
  441.8 3.7 collective-permute-start.35
  451.4 3.4 collective-permute-start.17
  455.0 4.0 collective-permute-start.37
  461.2 3.4 collective-permute-start.39
  467.5 6.2 %collective-permute-start.18 = (f32[3,64]{1,0:T(4,128)S(1)}, f32[3,64]{1,0:T(4,128)S(1)}, u32[]{:S(2)}, u32[]{:S(2)}) collective-permute-start(f32[3,64]{1,0:T(4,128)S(1)} %get-tuple-element.81), channel_id=1, source_target_pairs={{0,1},{1,0},{2,3},{3,2},{4,5},{5,4},{6,7},{7,6},{8,9},{9,8},{10,11... | collective-permute-start | bytes 2312 | tf_op jit(solution)/shard_map/ppermute | solution.py:20
  478.2 6.4 %collective-permute-start.19 = (bf16[64,504]{0,1:T(8,128)(2,1)S(1)}, bf16[64,504]{0,1:T(8,128)(2,1)S(1)}, u32[]{:S(2)}, u32[]{:S(2)}) collective-permute-start(bf16[64,504]{0,1:T(8,128)(2,1)S(1)} %concatenate.68), channel_id=1, source_target_pairs={{0,24},{8,0},{16,8},{24,16},{1,25},{9,1},{17,9},{25,17},{2,26},{10... | collective-permute-start | bytes 193544 | tf_op jit(solution)/shard_map/ppermute | solution.py:20
  484.6 6.5 %collective-permute-start.20 = (bf16[64,504]{0,1:T(8,128)(2,1)S(1)}, bf16[64,504]{0,1:T(8,128)(2,1)}, u32[]{:S(2)}, u32[]{:S(2)}) collective-permute-start(bf16[64,504]{0,1:T(8,128)(2,1)S(1)} %concatenate.68), channel_id=1, source_target_pairs={{0,16},{8,24},{16,0},{24,8},{1,17},{9,25},{17,1},{25,9},{2,18},{10... | collective-permute-start | bytes 193544 | tf_op jit(solution)/shard_map/ppermute | solution.py:20
  491.2 5.0 collective-permute-start.21
  500.7 4.2 collective-permute-start.41
  504.9 7.5 %collective-permute-start.42 = (bf16[64,504]{0,1:T(8,128)(2,1)S(1)}, bf16[64,504]{0,1:T(8,128)(2,1)}, u32[]{:S(2)}, u32[]{:S(2)}) collective-permute-start(bf16[64,504]{0,1:T(8,128)(2,1)S(1)} %concatenate.76), channel_id=1, source_target_pairs={{0,16},{8,24},{16,0},{24,8},{1,17},{9,25},{17,1},{25,9},{2,18},{10... | collective-permute-start | bytes 193544 | tf_op jit(solution)/shard_map/ppermute | solution.py:20
  512.4 2.7 collective-permute-start.43
  525.4 13.4 %all_gather.13 = bf16[1024,504]{1,0:T(8,128)(2,1)S(1)} all-gather(bf16[256,504]{1,0:T(8,128)(2,1)} %bitcast.589), channel_id=1, replica_groups=mesh['segment'=4,'y'=4,'zhi'=4,'zlo'=4,'core'=2] {'y'}, dimensions={0}, use_global_device_ids=true | all-gather | bytes 1290240 | tf_op jit(solution)/shard_map/all_gather | solution.py:148
  547.2 12.6 %all_gather.15 = bf16[1024,504]{1,0:T(8,128)(2,1)S(1)} all-gather(bf16[256,504]{1,0:T(8,128)(2,1)S(1)} %bitcast.590), channel_id=1, replica_groups=mesh['segment'=4,'y'=4,'zhi'=4,'zlo'=4,'core'=2] {'y'}, dimensions={0}, use_global_device_ids=true | all-gather | bytes 1290240 | tf_op jit(solution)/shard_map/all_gather | solution.py:148
  (257 shorter events, 87.2 us)
Async XLA Ops:
  7.2 104.2 %all-gather.3.cloned.1.call-start = ((), (), s32[]{:S(2)}) async-start(), calls=%async_computation.6 | async-start | bytes 2293760 | tf_op jit(solution)/shard_map/all_gather | solution.py:78
  9.0 36.5 %collective-permute-start = (bf16[64,896]{1,0:T(8,128)(2,1)S(1)}, bf16[64,896]{1,0:T(8,128)(2,1)S(1)}, u32[]{:S(2)}, u32[]{:S(2)}) collective-permute-start(bf16[64,896]{1,0:T(8,128)(2,1)S(1)} %get-tuple-element.43), channel_id=1, source_target_pairs={{0,24},{8,0},{16,8},{24,16},{1,25},{9,1},{17,9},{25,17},{2,26},{10... | collective-permute-start | bytes 344072 | tf_op jit(solution)/shard_map/ppermute | solution.py:20
  22.3 25.8 %collective-permute-start.1 = (bf16[64,896]{1,0:T(8,128)(2,1)S(1)}, bf16[64,896]{1,0:T(8,128)(2,1)S(1)}, u32[]{:S(2)}, u32[]{:S(2)}) collective-permute-start(bf16[64,896]{1,0:T(8,128)(2,1)S(1)} %get-tuple-element.43), channel_id=1, source_target_pairs={{0,16},{8,24},{16,0},{24,8},{1,17},{9,25},{17,1},{25,9},{2,18},{10... | collective-permute-start | bytes 344072 | tf_op jit(solution)/shard_map/ppermute | solution.py:20
  27.2 21.6 %collective-permute-start.2 = (bf16[64,896]{1,0:T(8,128)(2,1)S(1)}, bf16[64,896]{1,0:T(8,128)(2,1)S(1)}, u32[]{:S(2)}, u32[]{:S(2)}) collective-permute-start(bf16[64,896]{1,0:T(8,128)(2,1)S(1)} %get-tuple-element.43), channel_id=1, source_target_pairs={{0,8},{8,16},{16,24},{24,0},{1,9},{9,17},{17,25},{25,1},{2,10},{10... | collective-permute-start | bytes 344072 | tf_op jit(solution)/shard_map/ppermute | solution.py:20
  34.5 29.8 %collective-permute-start.22 = (bf16[64,896]{1,0:T(8,128)(2,1)S(1)}, bf16[64,896]{1,0:T(8,128)(2,1)S(1)}, u32[]{:S(2)}, u32[]{:S(2)}) collective-permute-start(bf16[64,896]{1,0:T(8,128)(2,1)S(1)} %get-tuple-element.40), channel_id=1, source_target_pairs={{0,24},{8,0},{16,8},{24,16},{1,25},{9,1},{17,9},{25,17},{2,26},{10... | collective-permute-start | bytes 344072 | tf_op jit(solution)/shard_map/ppermute | solution.py:20
  36.4 35.1 %collective-permute-start.23 = (bf16[64,896]{1,0:T(8,128)(2,1)S(1)}, bf16[64,896]{1,0:T(8,128)(2,1)S(1)}, u32[]{:S(2)}, u32[]{:S(2)}) collective-permute-start(bf16[64,896]{1,0:T(8,128)(2,1)S(1)} %get-tuple-element.40), channel_id=1, source_target_pairs={{0,16},{8,24},{16,0},{24,8},{1,17},{9,25},{17,1},{25,9},{2,18},{10... | collective-permute-start | bytes 344072 | tf_op jit(solution)/shard_map/ppermute | solution.py:20
  45.5 25.9 %collective-permute-start.24 = (bf16[64,896]{1,0:T(8,128)(2,1)S(1)}, bf16[64,896]{1,0:T(8,128)(2,1)S(1)}, u32[]{:S(2)}, u32[]{:S(2)}) collective-permute-start(bf16[64,896]{1,0:T(8,128)(2,1)S(1)} %get-tuple-element.40), channel_id=1, source_target_pairs={{0,8},{8,16},{16,24},{24,0},{1,9},{9,17},{17,25},{25,1},{2,10},{10... | collective-permute-start | bytes 344072 | tf_op jit(solution)/shard_map/ppermute | solution.py:20
  115.3 49.4 %all-to-all-start = ((bf16[32,32,448]{2,1,0:T(8,128)(2,1)}), bf16[32,32,448]{2,1,0:T(8,128)(2,1)S(1)}, u32[]{:S(2)}, u32[]{:S(2)}) async-start(bf16[32,32,448]{2,1,0:T(8,128)(2,1)} %bitcast.8), calls=%async_computation | async-start | bytes 2097152 | tf_op jit(solution)/shard_map/all_to_all | solution.py:83
  123.4 37.4 %all-gather.5.cloned.1.call-start = ((), (), s32[]{:S(2)}) async-start(), calls=%async_computation.8 | async-start | bytes 2293760 | tf_op jit(solution)/shard_map/all_gather | solution.py:78
  164.7 36.1 %all-to-all-start.2 = ((bf16[32,32,448]{2,1,0:T(8,128)(2,1)}), bf16[32,32,448]{2,1,0:T(8,128)(2,1)S(1)}, u32[]{:S(2)}, u32[]{:S(2)}) async-start(bf16[32,32,448]{2,1,0:T(8,128)(2,1)} %bitcast.586), calls=%async_computation.3 | async-start | bytes 2097152 | tf_op jit(solution)/shard_map/all_to_all | solution.py:83
  172.9 146.9 %reduce-scatter.3.cloned.1.call-start = ((), (), s32[]{:S(2)}) async-start(), calls=%async_computation.7 | async-start | bytes 2580480 | tf_op jit(solution)/shard_map/reduce_scatter | solution.py:101
  173.3 33.7 %collective-permute-start.3 = (f32[32]{0:T(128)S(1)}, f32[32]{0:T(128)S(1)}, u32[]{:S(2)}, u32[]{:S(2)}) collective-permute-start(f32[32]{0:T(128)S(1)} %multiply_reduce_fusion.3), channel_id=1, source_target_pairs={{0,96},{32,0},{64,32},{96,64},{1,97},{33,1},{65,33},{97,65},{2,98}... | collective-permute-start | bytes 392 | tf_op jit(solution)/shard_map/ppermute | solution.py:20
  175.9 33.3 %collective-permute-start.4 = (f32[32]{0:T(128)S(1)}, f32[32]{0:T(128)S(1)}, u32[]{:S(2)}, u32[]{:S(2)}) collective-permute-start(f32[32]{0:T(128)S(1)} %multiply_reduce_fusion.3), channel_id=1, source_target_pairs={{0,64},{32,96},{64,0},{96,32},{1,65},{33,97},{65,1},{97,33},{2,66}... | collective-permute-start | bytes 392 | tf_op jit(solution)/shard_map/ppermute | solution.py:20
  179.1 30.2 %collective-permute-start.5 = (f32[32]{0:T(128)S(1)}, f32[32]{0:T(128)S(1)}, u32[]{:S(2)}, u32[]{:S(2)}) collective-permute-start(f32[32]{0:T(128)S(1)} %multiply_reduce_fusion.3), channel_id=1, source_target_pairs={{0,32},{32,64},{64,96},{96,0},{1,33},{33,65},{65,97},{97,1},{2,34}... | collective-permute-start | bytes 392 | tf_op jit(solution)/shard_map/ppermute | solution.py:20
  201.1 22.6 %collective-permute-start.25 = (f32[32]{0:T(128)S(1)}, f32[32]{0:T(128)S(1)}, u32[]{:S(2)}, u32[]{:S(2)}) collective-permute-start(f32[32]{0:T(128)S(1)} %multiply_reduce_fusion.2), channel_id=1, source_target_pairs={{0,96},{32,0},{64,32},{96,64},{1,97},{33,1},{65,33},{97,65},{2,98}... | collective-permute-start | bytes 392 | tf_op jit(solution)/shard_map/ppermute | solution.py:20
  203.9 24.5 %collective-permute-start.26 = (f32[32]{0:T(128)S(1)}, f32[32]{0:T(128)S(1)}, u32[]{:S(2)}, u32[]{:S(2)}) collective-permute-start(f32[32]{0:T(128)S(1)} %multiply_reduce_fusion.2), channel_id=1, source_target_pairs={{0,64},{32,96},{64,0},{96,32},{1,65},{33,97},{65,1},{97,33},{2,66}... | collective-permute-start | bytes 392 | tf_op jit(solution)/shard_map/ppermute | solution.py:20
  207.0 21.4 %collective-permute-start.27 = (f32[32]{0:T(128)S(1)}, f32[32]{0:T(128)S(1)}, u32[]{:S(2)}, u32[]{:S(2)}) collective-permute-start(f32[32]{0:T(128)S(1)} %multiply_reduce_fusion.2), channel_id=1, source_target_pairs={{0,32},{32,64},{64,96},{96,0},{1,33},{33,65},{65,97},{97,1},{2,34}... | collective-permute-start | bytes 392 | tf_op jit(solution)/shard_map/ppermute | solution.py:20
  209.3 28.7 %collective-permute-start.6 = (f32[32]{0:T(128)S(1)}, f32[32]{0:T(128)S(1)}, u32[]{:S(2)}, u32[]{:S(2)}) collective-permute-start(f32[32]{0:T(128)S(1)} %fusion.146), channel_id=1, source_target_pairs={{0,24},{8,0},{16,8},{24,16},{1,25},{9,1},{17,9},{25,17},{2,26},{10... | collective-permute-start | bytes 392 | tf_op jit(solution)/shard_map/ppermute | solution.py:20
  214.7 27.2 %collective-permute-start.7 = (f32[32]{0:T(128)S(1)}, f32[32]{0:T(128)S(1)}, u32[]{:S(2)}, u32[]{:S(2)}) collective-permute-start(f32[32]{0:T(128)S(1)} %fusion.146), channel_id=1, source_target_pairs={{0,16},{8,24},{16,0},{24,8},{1,17},{9,25},{17,1},{25,9},{2,18},{10... | collective-permute-start | bytes 392 | tf_op jit(solution)/shard_map/ppermute | solution.py:20
  223.7 18.3 %collective-permute-start.8 = (f32[32]{0:T(128)S(1)}, f32[32]{0:T(128)S(1)}, u32[]{:S(2)}, u32[]{:S(2)}) collective-permute-start(f32[32]{0:T(128)S(1)} %fusion.146), channel_id=1, source_target_pairs={{0,8},{8,16},{16,24},{24,0},{1,9},{9,17},{17,25},{25,1},{2,10},{10... | collective-permute-start | bytes 392 | tf_op jit(solution)/shard_map/ppermute | solution.py:20
  228.5 13.6 %collective-permute-start.28 = (f32[32]{0:T(128)S(1)}, f32[32]{0:T(128)S(1)}, u32[]{:S(2)}, u32[]{:S(2)}) collective-permute-start(f32[32]{0:T(128)S(1)} %fusion.147), channel_id=1, source_target_pairs={{0,24},{8,0},{16,8},{24,16},{1,25},{9,1},{17,9},{25,17},{2,26},{10... | collective-permute-start | bytes 392 | tf_op jit(solution)/shard_map/ppermute | solution.py:20
  233.0 13.0 %collective-permute-start.29 = (f32[32]{0:T(128)S(1)}, f32[32]{0:T(128)S(1)}, u32[]{:S(2)}, u32[]{:S(2)}) collective-permute-start(f32[32]{0:T(128)S(1)} %fusion.147), channel_id=1, source_target_pairs={{0,16},{8,24},{16,0},{24,8},{1,17},{9,25},{17,1},{25,9},{2,18},{10... | collective-permute-start | bytes 392 | tf_op jit(solution)/shard_map/ppermute | solution.py:20
  238.1 8.2 %collective-permute-start.30 = (f32[32]{0:T(128)S(1)}, f32[32]{0:T(128)S(1)}, u32[]{:S(2)}, u32[]{:S(2)}) collective-permute-start(f32[32]{0:T(128)S(1)} %fusion.147), channel_id=1, source_target_pairs={{0,8},{8,16},{16,24},{24,0},{1,9},{9,17},{17,25},{25,1},{2,10},{10... | collective-permute-start | bytes 392 | tf_op jit(solution)/shard_map/ppermute | solution.py:20
  283.6 73.1 %reduce-scatter.5.cloned.1.call-start = ((), (), s32[]{:S(2)}) async-start(), calls=%async_computation.9 | async-start | bytes 2580480 | tf_op jit(solution)/shard_map/reduce_scatter | solution.py:101
  322.0 52.1 %collective-permute-start.10 = (f32[64,500]{0,1:T(8,128)}, f32[64,500]{0,1:T(8,128)}, u32[]{:S(2)}, u32[]{:S(2)}) collective-permute-start(f32[64,500]{0,1:T(8,128)} %get-tuple-element.37), channel_id=1, source_target_pairs={{0,16},{8,24},{16,0},{24,8},{1,17},{9,25},{17,1},{25,9},{2,18},{10... | collective-permute-start | bytes 384008 | tf_op jit(solution)/shard_map/ppermute | solution.py:42
  331.4 49.9 %collective-permute-start.11 = (f32[64,500]{0,1:T(8,128)S(1)}, f32[64,500]{0,1:T(8,128)}, u32[]{:S(2)}, u32[]{:S(2)}) collective-permute-start(f32[64,500]{0,1:T(8,128)S(1)} %get-tuple-element.36), channel_id=1, source_target_pairs={{0,24},{8,0},{16,8},{24,16},{1,25},{9,1},{17,9},{25,17},{2,26},{10... | collective-permute-start | bytes 384008 | tf_op jit(solution)/shard_map/ppermute | solution.py:42
  333.4 48.0 %collective-permute-start.9 = (f32[64,500]{0,1:T(8,128)S(1)}, f32[64,500]{0,1:T(8,128)}, u32[]{:S(2)}, u32[]{:S(2)}) collective-permute-start(f32[64,500]{0,1:T(8,128)S(1)} %get-tuple-element.35), channel_id=1, source_target_pairs={{0,8},{8,16},{16,24},{24,0},{1,9},{9,17},{17,25},{25,1},{2,10},{10... | collective-permute-start | bytes 384008 | tf_op jit(solution)/shard_map/ppermute | solution.py:42
  359.0 22.4 %collective-permute-start.31 = (f32[64,500]{0,1:T(8,128)}, f32[64,500]{0,1:T(8,128)}, u32[]{:S(2)}, u32[]{:S(2)}) collective-permute-start(f32[64,500]{0,1:T(8,128)} %get-tuple-element.32), channel_id=1, source_target_pairs={{0,8},{8,16},{16,24},{24,0},{1,9},{9,17},{17,25},{25,1},{2,10},{10... | collective-permute-start | bytes 384008 | tf_op jit(solution)/shard_map/ppermute | solution.py:42
  366.3 23.6 %collective-permute-start.32 = (f32[64,500]{0,1:T(8,128)}, f32[64,500]{0,1:T(8,128)}, u32[]{:S(2)}, u32[]{:S(2)}) collective-permute-start(f32[64,500]{0,1:T(8,128)} %get-tuple-element.34), channel_id=1, source_target_pairs={{0,16},{8,24},{16,0},{24,8},{1,17},{9,25},{17,1},{25,9},{2,18},{10... | collective-permute-start | bytes 384008 | tf_op jit(solution)/shard_map/ppermute | solution.py:42
  374.1 33.4 %collective-permute-start.33 = (f32[64,500]{0,1:T(8,128)}, f32[64,500]{0,1:T(8,128)}, u32[]{:S(2)}, u32[]{:S(2)}) collective-permute-start(f32[64,500]{0,1:T(8,128)} %get-tuple-element.33), channel_id=1, source_target_pairs={{0,24},{8,0},{16,8},{24,16},{1,25},{9,1},{17,9},{25,17},{2,26},{10... | collective-permute-start | bytes 384008 | tf_op jit(solution)/shard_map/ppermute | solution.py:42
  410.4 35.0 %collective-permute-start.12 = (f32[3,64]{1,0:T(4,128)S(1)}, f32[3,64]{1,0:T(4,128)S(1)}, u32[]{:S(2)}, u32[]{:S(2)}) collective-permute-start(f32[3,64]{1,0:T(4,128)S(1)} %pad_maximum_fusion), channel_id=1, source_target_pairs={{0,384},{128,0},{256,128},{384,256},{1,385},{129,1},{257,129},{385... | collective-permute-start | bytes 2312 | tf_op jit(solution)/shard_map/ppermute | solution.py:20
  432.1 15.3 %collective-permute-start.13 = (f32[3,64]{1,0:T(4,128)S(1)}, f32[3,64]{1,0:T(4,128)S(1)}, u32[]{:S(2)}, u32[]{:S(2)}) collective-permute-start(f32[3,64]{1,0:T(4,128)S(1)} %pad_maximum_fusion), channel_id=1, source_target_pairs={{0,256},{128,384},{256,0},{384,128},{1,257},{129,385},{257,1},{385... | collective-permute-start | bytes 2312 | tf_op jit(solution)/shard_map/ppermute | solution.py:20
  434.0 13.4 %collective-permute-start.14 = (f32[3,64]{1,0:T(4,128)S(1)}, f32[3,64]{1,0:T(4,128)S(1)}, u32[]{:S(2)}, u32[]{:S(2)}) collective-permute-start(f32[3,64]{1,0:T(4,128)S(1)} %pad_maximum_fusion), channel_id=1, source_target_pairs={{0,128},{128,256},{256,384},{384,0},{1,129},{129,257},{257,385},{3... | collective-permute-start | bytes 2312 | tf_op jit(solution)/shard_map/ppermute | solution.py:20
  437.8 13.7 %collective-permute-start.34 = (f32[3,64]{1,0:T(4,128)S(1)}, f32[3,64]{1,0:T(4,128)S(1)}, u32[]{:S(2)}, u32[]{:S(2)}) collective-permute-start(f32[3,64]{1,0:T(4,128)S(1)} %pad_maximum_fusion.3), channel_id=1, source_target_pairs={{0,384},{128,0},{256,128},{384,256},{1,385},{129,1},{257,129},{385... | collective-permute-start | bytes 2312 | tf_op jit(solution)/shard_map/ppermute | solution.py:20
  441.8 13.1 %collective-permute-start.35 = (f32[3,64]{1,0:T(4,128)S(1)}, f32[3,64]{1,0:T(4,128)S(1)}, u32[]{:S(2)}, u32[]{:S(2)}) collective-permute-start(f32[3,64]{1,0:T(4,128)S(1)} %pad_maximum_fusion.3), channel_id=1, source_target_pairs={{0,256},{128,384},{256,0},{384,128},{1,257},{129,385},{257,1},{385... | collective-permute-start | bytes 2312 | tf_op jit(solution)/shard_map/ppermute | solution.py:20
  445.4 9.4 %collective-permute-start.36 = (f32[3,64]{1,0:T(4,128)S(1)}, f32[3,64]{1,0:T(4,128)S(1)}, u32[]{:S(2)}, u32[]{:S(2)}) collective-permute-start(f32[3,64]{1,0:T(4,128)S(1)} %pad_maximum_fusion.3), channel_id=1, source_target_pairs={{0,128},{128,256},{256,384},{384,0},{1,129},{129,257},{257,385},{3... | collective-permute-start | bytes 2312 | tf_op jit(solution)/shard_map/ppermute | solution.py:20
  447.6 13.6 %collective-permute-start.15 = (f32[3,64]{1,0:T(4,128)S(1)}, f32[3,64]{1,0:T(4,128)S(1)}, u32[]{:S(2)}, u32[]{:S(2)}) collective-permute-start(f32[3,64]{1,0:T(4,128)S(1)} %pad_maximum_fusion.1), channel_id=1, source_target_pairs={{0,6},{2,0},{4,2},{6,4},{1,7},{3,1},{5,3},{7,5},{8,14},{10,8},{12,... | collective-permute-start | bytes 2312 | tf_op jit(solution)/shard_map/ppermute | solution.py:20
  449.5 15.1 %collective-permute-start.16 = (f32[3,64]{1,0:T(4,128)S(1)}, f32[3,64]{1,0:T(4,128)S(1)}, u32[]{:S(2)}, u32[]{:S(2)}) collective-permute-start(f32[3,64]{1,0:T(4,128)S(1)} %pad_maximum_fusion.1), channel_id=1, source_target_pairs={{0,4},{2,6},{4,0},{6,2},{1,5},{3,7},{5,1},{7,3},{8,12},{10,14},{12... | collective-permute-start | bytes 2312 | tf_op jit(solution)/shard_map/ppermute | solution.py:20
  451.4 13.2 %collective-permute-start.17 = (f32[3,64]{1,0:T(4,128)S(1)}, f32[3,64]{1,0:T(4,128)S(1)}, u32[]{:S(2)}, u32[]{:S(2)}) collective-permute-start(f32[3,64]{1,0:T(4,128)S(1)} %pad_maximum_fusion.1), channel_id=1, source_target_pairs={{0,2},{2,4},{4,6},{6,0},{1,3},{3,5},{5,7},{7,1},{8,10},{10,12},{12... | collective-permute-start | bytes 2312 | tf_op jit(solution)/shard_map/ppermute | solution.py:20
  455.0 9.7 %collective-permute-start.37 = (f32[3,64]{1,0:T(4,128)S(1)}, f32[3,64]{1,0:T(4,128)S(1)}, u32[]{:S(2)}, u32[]{:S(2)}) collective-permute-start(f32[3,64]{1,0:T(4,128)S(1)} %pad_maximum_fusion.4), channel_id=1, source_target_pairs={{0,6},{2,0},{4,2},{6,4},{1,7},{3,1},{5,3},{7,5},{8,14},{10,8},{12,... | collective-permute-start | bytes 2312 | tf_op jit(solution)/shard_map/ppermute | solution.py:20
  467.5 8.9 %collective-permute-start.18 = (f32[3,64]{1,0:T(4,128)S(1)}, f32[3,64]{1,0:T(4,128)S(1)}, u32[]{:S(2)}, u32[]{:S(2)}) collective-permute-start(f32[3,64]{1,0:T(4,128)S(1)} %get-tuple-element.81), channel_id=1, source_target_pairs={{0,1},{1,0},{2,3},{3,2},{4,5},{5,4},{6,7},{7,6},{8,9},{9,8},{10,11... | collective-permute-start | bytes 2312 | tf_op jit(solution)/shard_map/ppermute | solution.py:20
  474.3 21.9 %collective-permute-start.40 = (f32[3,64]{1,0:T(4,128)}, f32[3,64]{1,0:T(4,128)}, u32[]{:S(2)}, u32[]{:S(2)}) collective-permute-start(f32[3,64]{1,0:T(4,128)} %get-tuple-element.79), channel_id=1, source_target_pairs={{0,1},{1,0},{2,3},{3,2},{4,5},{5,4},{6,7},{7,6},{8,9},{9,8},{10,11... | collective-permute-start | bytes 2312 | tf_op jit(solution)/shard_map/ppermute | solution.py:20
  478.2 34.2 %collective-permute-start.19 = (bf16[64,504]{0,1:T(8,128)(2,1)S(1)}, bf16[64,504]{0,1:T(8,128)(2,1)S(1)}, u32[]{:S(2)}, u32[]{:S(2)}) collective-permute-start(bf16[64,504]{0,1:T(8,128)(2,1)S(1)} %concatenate.68), channel_id=1, source_target_pairs={{0,24},{8,0},{16,8},{24,16},{1,25},{9,1},{17,9},{25,17},{2,26},{10... | collective-permute-start | bytes 193544 | tf_op jit(solution)/shard_map/ppermute | solution.py:20
  484.6 31.2 %collective-permute-start.20 = (bf16[64,504]{0,1:T(8,128)(2,1)S(1)}, bf16[64,504]{0,1:T(8,128)(2,1)}, u32[]{:S(2)}, u32[]{:S(2)}) collective-permute-start(bf16[64,504]{0,1:T(8,128)(2,1)S(1)} %concatenate.68), channel_id=1, source_target_pairs={{0,16},{8,24},{16,0},{24,8},{1,17},{9,25},{17,1},{25,9},{2,18},{10... | collective-permute-start | bytes 193544 | tf_op jit(solution)/shard_map/ppermute | solution.py:20
  491.2 26.2 %collective-permute-start.21 = (bf16[64,504]{0,1:T(8,128)(2,1)S(1)}, bf16[64,504]{0,1:T(8,128)(2,1)}, u32[]{:S(2)}, u32[]{:S(2)}) collective-permute-start(bf16[64,504]{0,1:T(8,128)(2,1)S(1)} %concatenate.68), channel_id=1, source_target_pairs={{0,8},{8,16},{16,24},{24,0},{1,9},{9,17},{17,25},{25,1},{2,10},{10... | collective-permute-start | bytes 193544 | tf_op jit(solution)/shard_map/ppermute | solution.py:20
  500.7 39.7 %collective-permute-start.41 = (bf16[64,504]{0,1:T(8,128)(2,1)S(1)}, bf16[64,504]{0,1:T(8,128)(2,1)}, u32[]{:S(2)}, u32[]{:S(2)}) collective-permute-start(bf16[64,504]{0,1:T(8,128)(2,1)S(1)} %concatenate.76), channel_id=1, source_target_pairs={{0,24},{8,0},{16,8},{24,16},{1,25},{9,1},{17,9},{25,17},{2,26},{10... | collective-permute-start | bytes 193544 | tf_op jit(solution)/shard_map/ppermute | solution.py:20
  504.9 36.4 %collective-permute-start.42 = (bf16[64,504]{0,1:T(8,128)(2,1)S(1)}, bf16[64,504]{0,1:T(8,128)(2,1)}, u32[]{:S(2)}, u32[]{:S(2)}) collective-permute-start(bf16[64,504]{0,1:T(8,128)(2,1)S(1)} %concatenate.76), channel_id=1, source_target_pairs={{0,16},{8,24},{16,0},{24,8},{1,17},{9,25},{17,1},{25,9},{2,18},{10... | collective-permute-start | bytes 193544 | tf_op jit(solution)/shard_map/ppermute | solution.py:20
  512.4 30.8 %collective-permute-start.43 = (bf16[64,504]{0,1:T(8,128)(2,1)S(1)}, bf16[64,504]{0,1:T(8,128)(2,1)}, u32[]{:S(2)}, u32[]{:S(2)}) collective-permute-start(bf16[64,504]{0,1:T(8,128)(2,1)S(1)} %concatenate.76), channel_id=1, source_target_pairs={{0,8},{8,16},{16,24},{24,0},{1,9},{9,17},{17,25},{25,1},{2,10},{10... | collective-permute-start | bytes 193544 | tf_op jit(solution)/shard_map/ppermute | solution.py:20
  (31 other events, 2426.4 us)
Sparse Core Ops, SparseCore 0:
  76.1 35.1 all-gather.2
  126.9 33.8 all-gather.4
  283.7 33.0 reduce-scatter.2
  319.8 36.8 reduce-scatter.4

commit v4 on v1

--- a/solution.py
+++ b/solution.py
@@ -52,21 +52,22 @@
     product = jnp.dot(rows, unite_weight[0], preferred_element_type=jnp.float32)
     product = lax.optimization_barrier(product.astype(jnp.bfloat16))
 
-    pieces = lax.all_to_all(product, SM, 0, 0, tiled=True)
-    slice_len = tokens // n_sm
-    united = jnp.sum(
-        pieces.reshape(n_sm, slice_len, -1).astype(jnp.float32), axis=0
-    )
+    n_sc = sizes["segment"] * sizes["core"]
+    pieces = lax.all_to_all(product, ("segment", "core"), 0, 0, tiled=True)
+    chunk = tokens // n_sc
+    united = jnp.sum(pieces.reshape(n_sc, chunk, -1).astype(jnp.float32), axis=0)
+    united = lax.psum_scatter(united, "zlo", scatter_dimension=0, tiled=True)
 
     squares = jnp.sum(united * united, axis=1)
-    squares = butterfly(squares, "y", sizes["y"], add)
-    squares = butterfly(squares, "zhi", sizes["zhi"], add)
+    squares = lax.psum(squares, "y")
+    squares = lax.psum(squares, "zhi")
     hidden_part = (
         united * lax.rsqrt(squares / D + norm_eps)[:, None] * norm_gain[None, :]
     ).astype(jnp.bfloat16)
-    spread = jnp.broadcast_to(hidden_part[None], (n_sm,) + hidden_part.shape)
+    hidden_chunk = lax.all_gather(hidden_part, "zlo", axis=0, tiled=True)
+    spread = jnp.broadcast_to(hidden_chunk[None], (n_sc,) + hidden_chunk.shape)
     hidden = lax.all_to_all(
-        spread.reshape(tokens, -1), SM, 0, 0, tiled=True
+        spread.reshape(tokens, -1), ("segment", "core"), 0, 0, tiled=True
     )
 
     logits = jnp.dot(hidden, head_weight, preferred_element_type=jnp.float32)

time: 501 us -> 475 us (0.948)
  starting transfers between devices: 44.2 us -> 21 us
  blocking collectives: 199 us -> 180 us
  waiting for transfers between devices: 218 us -> 234 us
    all_to_all x2, blocking collectives: 117 us -> 65.3 us  [the longest x1 36.9 us: on_device(): lax.all_to_all(spread.reshape(tokens, -1), ('segment', 'core'), 0, 0, til...]
    reduce_scatter x0 -> x1, waiting for transfers between devices: none -> 29.3 us  [on_device(): united = lax.psum_scatter(united, 'zlo', scatter_dimension=0, tiled=True)]
    ppermute x9 -> x5, starting transfers between devices: 44.1 us -> 20.8 us  [butterfly(): value = combine(value, lax.ppermute(value, axis, pairs))]
    psum x0 -> x2, blocking collectives: none -> 22.3 us  [the longest x1 14 us: on_device(): squares = lax.psum(squares, 'zhi')]
    all_gather x0 -> x1, blocking collectives: none -> 11 us  [on_device(): hidden_chunk = lax.all_gather(hidden_part, 'zlo', axis=0, tiled=True)]
    ppermute x9 -> x5, waiting for transfers between devices: 16.2 us -> 8.1 us  [butterfly(): value = combine(value, lax.ppermute(value, axis, pairs))]
  transfers between devices with their start and end apart: 13 -> 10, of which waited for: 13 -> 10; matrix products, arithmetic and copies ran while one was open for 0% -> 0% of each run, Pallas kernels for 0% -> 0%
where the time goes in v4:
time: 475 us
  waiting for transfers between devices  234 us (49%)
  blocking collectives  180 us (38%)
  starting transfers between devices  21 us (4%)
  between operations  16.5 us (3%)
  matrix products  11 us (2%)
  other arithmetic  7.89 us (2%)
    reduce_scatter x1, waiting for transfers between devices, on_device(): logits = lax.psum_scatter(logits, 'zhi', scatter_dimension=0, tiled=True)  61.1 us
    all_gather x1, waiting for transfers between devices, on_device(): rows = lax.all_gather(rows, 'y', axis=0, tiled=True)  50.1 us
    reduce_scatter x1, waiting for transfers between devices, on_device(): logits = lax.psum_scatter(logits, 'y', scatter_dimension=0, tiled=True)  46.8 us
    all_gather x1, blocking collectives, on_device(): rows = lax.all_gather(sources[0], 'zhi', axis=0, tiled=True)  45.3 us
    all_gather x1, waiting for transfers between devices, on_device(): carried = lax.all_gather(carried, 'y', axis=0, tiled=True)  38.6 us
    all_to_all x1, blocking collectives, on_device(): lax.all_to_all(spread.reshape(tokens, -1), ('segment', 'core'), 0, 0, til...  36.9 us
    all_gather x1, blocking collectives, on_device(): carried = lax.all_gather(carried, 'zhi', axis=0, tiled=True)  36.5 us
    reduce_scatter x1, waiting for transfers between devices, on_device(): united = lax.psum_scatter(united, 'zlo', scatter_dimension=0, tiled=True)  29.3 us
  transfers between devices with their start and end apart: 10, of which 10 were waited for; matrix products, arithmetic and copies ran while one was open for 0% of the time, Pallas kernels for 0%

profile of v4, /device:TPU:1, one launch (start us, length us, event | category | flops | bytes accessed | tf_op | source)
XLA Modules:
  0.0 474.5 jit_solution(11996677095633763132)
XLA Ops:
  7.2 0.0 all-gather.7.cloned.1.call-start
  7.2 45.3 %all-gather = bf16[1,512,896]{2,1,0:T(8,128)(2,1)} all-gather(bf16[1,128,896]{2,1,0:T(8,128)(2,1)} %param.8), channel_id=2, replica_groups=mesh['segment'=4,'y'=4,'zhi'=4,'zlo'=4,'core'=2] {'zhi'}, dimensions={1}, use_global_device_ids=true | all-gather | bytes 1146880 | tf_op jit(solution)/shard_map/all_gather | solution.py:49
  52.5 0.0 reduce-scatter.10.cloned.1.call-start
  52.6 50.1 %all-gather.7.cloned.1.call-done = bf16[1,2048,896]{2,1,0:T(8,128)(2,1)} async-done(((bf16[1,512,896]{2,1,0:T(8,128)(2,1)}), bf16[1,2048,896]{2,1,0:T(8,128)(2,1)}) %all-gather.7.cloned.1.call-update) | async-done | bytes 3670032 | tf_op jit(solution)/shard_map/all_gather | solution.py:50
  102.7 4.1 fusion.2
  106.8 0.1 copy.36
  107.0 28.3 %all_to_all.18 = bf16[8,256,448]{1,2,0:T(8,128)(2,1)S(1)} all-to-all(bf16[8,256,448]{1,2,0:T(8,128)(2,1)S(1)} %bitcast.223), channel_id=1, replica_groups=mesh['segment'=4,'y'=4,'zhi'=4,'zlo'=4,'core'=2] {'segment','core'}, dimensions={0} | all-to-all | bytes 3670016 | tf_op jit(solution)/shard_map/all_to_all | solution.py:56
  135.3 0.2 convert_reduce_fusion
  135.6 1.0 copy.30
  136.6 0.0 reduce-scatter.6.cloned.1.call-start
  136.6 29.3 %reduce-scatter.10.cloned.1.call-done = f32[64,448]{1,0:T(8,128)} async-done(((f32[256,448]{1,0:T(8,128)}), f32[64,448]{1,0:T(8,128)}) %reduce-scatter.10.cloned.1.call-update) | async-done | bytes 114704 | tf_op jit(solution)/shard_map/reduce_scatter | solution.py:59
  166.0 1.0 copy.31
  167.0 0.1 multiply_reduce_fusion.1
  167.1 8.3 %psum.14 = f32[64]{0:T(128)S(1)} all-reduce(f32[64]{0:T(128)S(1)} %multiply_reduce_fusion.1), channel_id=1, replica_groups=mesh['segment'=4,'y'=4,'zhi'=4,'zlo'=4,'core'=2] {'y'}, use_global_device_ids=true, to_apply=%region_6.0 | all-reduce | flops 64 | bytes 512 | tf_op jit(solution)/shard_map/psum | solution.py:62
  175.4 14.0 %psum.15 = f32[64]{0:T(128)S(1)} all-reduce(f32[64]{0:T(128)S(1)} %psum.14), channel_id=1, replica_groups=mesh['segment'=4,'y'=4,'zhi'=4,'zlo'=4,'core'=2] {'zhi'}, use_global_device_ids=true, to_apply=%region_7.0 | all-reduce | flops 64 | bytes 512 | tf_op jit(solution)/shard_map/psum | solution.py:63
  189.4 1.0 multiply_convert_fusion.1
  190.4 11.0 %all_gather.17 = bf16[256,448]{1,0:T(8,128)(2,1)S(1)} all-gather(bf16[64,448]{1,0:T(8,128)(2,1)S(1)} %multiply_convert_fusion.1), channel_id=1, replica_groups=mesh['segment'=4,'y'=4,'zhi'=4,'zlo'=4,'core'=2] {'zlo'}, dimensions={0}, use_global_device_ids=true | all-gather | bytes 286720 | tf_op jit(solution)/shard_map/all_gather | solution.py:67
  201.5 0.1 copy.28
  201.6 0.1 broadcast_in_dim.6
  201.7 36.9 %all_to_all.19 = bf16[8,256,448]{1,2,0:T(8,128)(2,1)S(1)} all-to-all(bf16[8,256,448]{1,2,0:T(8,128)(2,1)S(1)} %broadcast_in_dim.6), channel_id=1, replica_groups=mesh['segment'=4,'y'=4,'zhi'=4,'zlo'=4,'core'=2] {'segment','core'}, dimensions={0} | all-to-all | bytes 3670016 | tf_op jit(solution)/shard_map/all_to_all | solution.py:69
  238.7 0.2 copy.34
  238.9 0.8 copy-done.1
  239.7 3.2 fusion.44
  243.0 0.0 reduce-scatter.8.cloned.1.call-start
  243.0 46.8 %reduce-scatter.6.cloned.1.call-done = f32[512,500]{0,1:T(8,128)} async-done(((f32[2048,500]{0,1:T(8,128)}), f32[512,500]{0,1:T(8,128)}) %reduce-scatter.6.cloned.1.call-update) | async-done | bytes 1024016 | tf_op jit(solution)/shard_map/reduce_scatter | solution.py:74
  289.9 0.0 all-gather.5.cloned.1.call-start
  290.0 61.1 %reduce-scatter.8.cloned.1.call-done = f32[128,500]{0,1:T(8,128)} async-done(((f32[512,500]{0,1:T(8,128)}), f32[128,500]{0,1:T(8,128)}) %reduce-scatter.8.cloned.1.call-update) | async-done | bytes 256016 | tf_op jit(solution)/shard_map/reduce_scatter | solution.py:75
  351.1 1.0 reduce_max.9
  352.1 1.0 exponential_reduce_fusion
  353.1 1.3 multiply_reduce_fusion
  354.4 3.3 collective-permute-start
  357.8 1.0 collective-permute-done
  358.8 4.9 %collective-permute-start.1 = (f32[3,128]{1,0:T(4,128)S(1)}, f32[3,128]{1,0:T(4,128)S(1)}, u32[]{:S(2)}, u32[]{:S(2)}) collective-permute-start(f32[3,128]{1,0:T(4,128)S(1)} %pad_maximum_fusion.1), channel_id=1, source_target_pairs={{0,256},{128,384},{256,0},{384,128},{1,257},{129,385},{257,1},{385... | collective-permute-start | bytes 4616 | tf_op jit(solution)/shard_map/ppermute | solution.py:20
  363.7 1.0 collective-permute-done.1
  364.7 1.9 collective-permute-start.2
  366.6 0.2 reduce-window.8
  366.8 2.2 collective-permute-done.2
  369.0 1.9 collective-permute-start.3
  371.0 0.1 compare_reduce_fusion
  371.1 3.2 collective-permute-done.3
  374.3 8.7 %collective-permute-start.4 = (f32[3,128]{1,0:T(4,128)S(1)}, f32[3,128]{1,0:T(4,128)S(1)}, u32[]{:S(2)}, u32[]{:S(2)}) collective-permute-start(f32[3,128]{1,0:T(4,128)S(1)} %pad_maximum_fusion.4), channel_id=1, source_target_pairs={{0,1},{1,0},{2,3},{3,2},{4,5},{5,4},{6,7},{7,6},{8,9},{9,8},{10,11... | collective-permute-start | bytes 4616 | tf_op jit(solution)/shard_map/ppermute | solution.py:20
  383.0 0.8 collective-permute-done.4
  383.9 1.3 multiply_convert_fusion
  385.2 0.1 concatenate.3
  385.2 36.5 %all_gather.18 = bf16[512,504]{0,1:T(8,128)(2,1)} all-gather(bf16[128,504]{0,1:T(8,128)(2,1)S(1)} %concatenate.3), channel_id=1, replica_groups=mesh['segment'=4,'y'=4,'zhi'=4,'zlo'=4,'core'=2] {'zhi'}, dimensions={0}, use_global_device_ids=true | all-gather | bytes 645120 | tf_op jit(solution)/shard_map/all_gather | solution.py:120
  421.7 38.6 %all-gather.5.cloned.1.call-done = bf16[2048,504]{0,1:T(8,128)(2,1)} async-done(((bf16[512,504]{0,1:T(8,128)(2,1)}), bf16[2048,504]{0,1:T(8,128)(2,1)}) %all-gather.5.cloned.1.call-update) | async-done | bytes 2064400 | tf_op jit(solution)/shard_map/all_gather | solution.py:121
  460.4 1.5 fusion.8
  463.2 3.6 fusion.5
  (36 shorter events, 0.3 us)
Async XLA Ops:
  7.2 95.5 %copy-start = (bf16[1,896,448]{1,2,0:T(8,128)(2,1)S(1)}, bf16[1,896,448]{1,2,0:T(8,128)(2,1)}, u32[]{:S(2)}) copy-start(bf16[1,896,448]{1,2,0:T(8,128)(2,1)} %param.9) | copy-start | bytes 2408452
  7.2 95.5 %all-gather.7.cloned.1.call-start = ((), (), s32[]{:S(2)}) async-start(), calls=%async_computation.8 | async-start | bytes 4587520 | tf_op jit(solution)/shard_map/all_gather | solution.py:50
  52.5 113.4 %reduce-scatter.10.cloned.1.call-start = ((), (), s32[]{:S(2)}) async-start(), calls=%async_computation.9 | async-start | bytes 655360 | tf_op jit(solution)/shard_map/reduce_scatter | solution.py:59
  135.3 54.1 %copy-start.5 = (f32[448]{0:T(512)S(1)}, f32[448]{0:T(512)}, u32[]{:S(2)}) copy-start(f32[448]{0:T(512)} %param.10) | copy-start | bytes 5380
  136.6 153.2 %reduce-scatter.6.cloned.1.call-start = ((), (), s32[]{:S(2)}) async-start(), calls=%async_computation.5 | async-start | bytes 5160960 | tf_op jit(solution)/shard_map/reduce_scatter | solution.py:74
  238.7 1.0 copy-start.1
  242.9 47.0 %copy-start.2 = (f32[128,8]{0,1:T(8,128)S(1)}, f32[128,8]{0,1:T(8,128)}, u32[]{:S(2)}) copy-start(f32[128,8]{0,1:T(8,128)} %param.15) | copy-start | bytes 12292
  242.9 47.0 %copy-start.4 = (s32[128,8]{0,1:T(8,128)S(1)}, s32[128,8]{0,1:T(8,128)}, u32[]{:S(2)}) copy-start(s32[128,8]{0,1:T(8,128)} %param.14) | copy-start | bytes 12292
  242.9 110.2 %copy-start.3 = (s32[128]{0:T(128)S(1)}, s32[128]{0:T(128)}, u32[]{:S(2)}) copy-start(s32[128]{0:T(128)} %param.13) | copy-start | bytes 1540
  242.9 123.7 %copy-start.6 = (s32[12]{0:T(128)S(1)}, s32[12]{0:T(128)}, u32[]{:S(2)}) copy-start(s32[12]{0:T(128)} %param.12) | copy-start | bytes 148
  243.0 108.1 %reduce-scatter.8.cloned.1.call-start = ((), (), s32[]{:S(2)}) async-start(), calls=%async_computation.6 | async-start | bytes 1290240 | tf_op jit(solution)/shard_map/reduce_scatter | solution.py:75
  289.9 170.5 %all-gather.5.cloned.1.call-start = ((), (), s32[]{:S(2)}) async-start(), calls=%async_computation.7 | async-start | bytes 2580480 | tf_op jit(solution)/shard_map/all_gather | solution.py:121
  354.4 4.3 collective-permute-start
  358.8 5.9 %collective-permute-start.1 = (f32[3,128]{1,0:T(4,128)S(1)}, f32[3,128]{1,0:T(4,128)S(1)}, u32[]{:S(2)}, u32[]{:S(2)}) collective-permute-start(f32[3,128]{1,0:T(4,128)S(1)} %pad_maximum_fusion.1), channel_id=1, source_target_pairs={{0,256},{128,384},{256,0},{384,128},{1,257},{129,385},{257,1},{385... | collective-permute-start | bytes 4616 | tf_op jit(solution)/shard_map/ppermute | solution.py:20
  364.7 4.3 collective-permute-start.2
  369.0 5.2 %collective-permute-start.3 = (f32[3,128]{1,0:T(4,128)S(1)}, f32[3,128]{1,0:T(4,128)S(1)}, u32[]{:S(2)}, u32[]{:S(2)}) collective-permute-start(f32[3,128]{1,0:T(4,128)S(1)} %pad_maximum_fusion.3), channel_id=1, source_target_pairs={{0,4},{2,6},{4,0},{6,2},{1,5},{3,7},{5,1},{7,3},{8,12},{10,14},{12... | collective-permute-start | bytes 4616 | tf_op jit(solution)/shard_map/ppermute | solution.py:20
  374.3 9.5 %collective-permute-start.4 = (f32[3,128]{1,0:T(4,128)S(1)}, f32[3,128]{1,0:T(4,128)S(1)}, u32[]{:S(2)}, u32[]{:S(2)}) collective-permute-start(f32[3,128]{1,0:T(4,128)S(1)} %pad_maximum_fusion.4), channel_id=1, source_target_pairs={{0,1},{1,0},{2,3},{3,2},{4,5},{5,4},{6,7},{7,6},{8,9},{9,8},{10,11... | collective-permute-start | bytes 4616 | tf_op jit(solution)/shard_map/ppermute | solution.py:20
Sparse Core Ops, SparseCore 0:
  52.7 49.9 all-gather.6
  136.7 29.2 reduce-scatter.9
  243.1 46.7 reduce-scatter.5
  292.8 58.2 reduce-scatter.7
  421.9 38.4 all-gather.4

commit v5 on v4

--- a/solution.py
+++ b/solution.py
@@ -13,23 +13,16 @@
 SM = ("segment", "zlo", "core")
 
 
-def butterfly(value, axis, size, combine):
-    step = 1
-    while step < size:
-        pairs = [(i, i ^ step) for i in range(size)]
-        value = combine(value, lax.ppermute(value, axis, pairs))
-        step *= 2
-    return value
+def spread_gather(value, axes, size):
+    spread = jnp.broadcast_to(value[None], (size,) + value.shape)
+    return lax.all_to_all(
+        spread.reshape((size * value.shape[0],) + value.shape[1:]), axes, 0, 0, tiled=True
+    )
 
 
-def add(a, b):
-    return a + b
-
-
-def merge_stats(a, b):
-    peak = jnp.maximum(a[0], b[0])
-    total = a[1] * jnp.exp(a[0] - peak) + b[1] * jnp.exp(b[0] - peak)
-    return jnp.stack([peak, total, a[2] + b[2]])
+def scatter_sum(value, axes, size):
+    pieces = lax.all_to_all(value, axes, 0, 0, tiled=True)
+    return jnp.sum(pieces.reshape((size, value.shape[0] // size) + value.shape[1:]), axis=0)
 
 
 def on_device(
@@ -47,7 +40,7 @@
     n_sm = sizes["segment"] * sizes["zlo"] * sizes["core"]
 
     rows = lax.all_gather(sources[0], "zhi", axis=0, tiled=True)
-    rows = lax.all_gather(rows, "y", axis=0, tiled=True)
+    rows = spread_gather(rows, "y", sizes["y"])
     tokens = rows.shape[0]
     product = jnp.dot(rows, unite_weight[0], preferred_element_type=jnp.float32)
     product = lax.optimization_barrier(product.astype(jnp.bfloat16))
@@ -56,7 +49,7 @@
     pieces = lax.all_to_all(product, ("segment", "core"), 0, 0, tiled=True)
     chunk = tokens // n_sc
     united = jnp.sum(pieces.reshape(n_sc, chunk, -1).astype(jnp.float32), axis=0)
-    united = lax.psum_scatter(united, "zlo", scatter_dimension=0, tiled=True)
+    united = scatter_sum(united, "zlo", sizes["zlo"])
 
     squares = jnp.sum(united * united, axis=1)
     squares = lax.psum(squares, "y")
@@ -94,10 +87,12 @@
             jnp.sum(target_weight * logits, axis=1),
         ]
     )
-    for axis in SM:
-        stats = butterfly(stats, axis, sizes[axis], merge_stats)
-    lse = stats[0] + jnp.log(stats[1])
-    picked = stats[2]
+    n_sm = sizes["segment"] * sizes["zlo"] * sizes["core"]
+    every = spread_gather(stats[None], SM, n_sm)
+    peak = jnp.max(every[:, 0], axis=0)
+    total = jnp.sum(every[:, 1] * jnp.exp(every[:, 0] - peak[None]), axis=0)
+    lse = peak + jnp.log(total)
+    picked = jnp.sum(every[:, 2], axis=0)
 
     target_mass = 1.0 + jnp.sum(teacher_probs, axis=1)
     doc_ends = jnp.cumsum(doc_lengths)
@@ -118,7 +113,7 @@
     )
     carried = jnp.concatenate([logit_grad, extra], axis=1)
     carried = lax.all_gather(carried, "zhi", axis=0, tiled=True)
-    carried = lax.all_gather(carried, "y", axis=0, tiled=True)
+    carried = spread_gather(carried, "y", sizes["y"])
 
     loss_sum = jnp.sum(
         carried[:, vocab_width].astype(jnp.float32)

time: 475 us -> 436 us (0.918)
  waiting for transfers between devices: 234 us -> 115 us
  blocking collectives: 180 us -> 271 us
  starting transfers between devices: 21 us -> 6.95 us
    all_gather x2 -> x0, waiting for transfers between devices: 88.7 us -> none  [the longest x1 50.1 us: on_device(): rows = lax.all_gather(rows, 'y', axis=0, tiled=True)]
    all_to_all x0 -> x3, blocking collectives: none -> 87.7 us  [the longest x2 71.8 us: spread_gather(): lax.all_to_all(spread.reshape((size * value.shape[0],) + value.shape[1:])...]
    reduce_scatter x1 -> x0, waiting for transfers between devices: 29.3 us -> none  [on_device(): united = lax.psum_scatter(united, 'zlo', scatter_dimension=0, tiled=True)]
    ppermute x5 -> x0, starting transfers between devices: 20.8 us -> none  [butterfly(): value = combine(value, lax.ppermute(value, axis, pairs))]
    ppermute x5 -> x0, waiting for transfers between devices: 8.1 us -> none  [butterfly(): value = combine(value, lax.ppermute(value, axis, pairs))]
    all_to_all x0 -> x1, waiting for transfers between devices: none -> 7.77 us  [spread_gather(): lax.all_to_all(spread.reshape((size * value.shape[0],) + value.shape[1:])...]
    all_to_all x0 -> x1, starting transfers between devices: none -> 6.87 us  [spread_gather(): lax.all_to_all(spread.reshape((size * value.shape[0],) + value.shape[1:])...]
  transfers between devices with their start and end apart: 10 -> 3, of which waited for: 10 -> 3; matrix products, arithmetic and copies ran while one was open for 0% -> 0% of each run, Pallas kernels for 0% -> 0%
where the time goes in v5:
time: 436 us; the launch traced here: 434 us
  blocking collectives  271 us (62%)
  waiting for transfers between devices  115 us (26%)
  between operations  16.6 us (4%)
  matrix products  8.96 us (2%)
  other arithmetic  8.33 us (2%)
  starting transfers between devices  6.95 us (2%)
  local copies, waits for them, and re-layouts  6.9 us (2%)
    all_to_all x2, blocking collectives, spread_gather(): lax.all_to_all(spread.reshape((size * value.shape[0],) + value.shape[1:])...  71.8 us
    reduce_scatter x1, waiting for transfers between devices, on_device(): logits = lax.psum_scatter(logits, 'zhi', scatter_dimension=0, tiled=True)  61.3 us
    reduce_scatter x1, waiting for transfers between devices, on_device(): logits = lax.psum_scatter(logits, 'y', scatter_dimension=0, tiled=True)  46.3 us
    all_gather x1, blocking collectives, on_device(): rows = lax.all_gather(sources[0], 'zhi', axis=0, tiled=True)  45.8 us
    all_gather x1, blocking collectives, on_device(): carried = lax.all_gather(carried, 'zhi', axis=0, tiled=True)  40.3 us
    all_to_all x1, blocking collectives, on_device(): lax.all_to_all(spread.reshape(tokens, -1), ('segment', 'core'), 0, 0, til...  34.6 us
    all_to_all x1, blocking collectives, on_device(): pieces = lax.all_to_all(product, ('segment', 'core'), 0, 0, tiled=True)  32.4 us
    all_to_all x1, blocking collectives, scatter_sum(): pieces = lax.all_to_all(value, axes, 0, 0, tiled=True)  16 us
  transfers between devices with their start and end apart: 3, of which 3 were waited for; matrix products, arithmetic and copies ran while one was open for 0% of the time, Pallas kernels for 0%

profile of v5, /device:TPU:1, one launch (start us, length us, event | category | flops | bytes accessed | tf_op | source)
XLA Modules:
  0.0 434.1 jit_solution(12303934777028731295)
XLA Ops:
  7.2 0.0 copy-start
  7.2 0.0 reduce-scatter.3.cloned.1.call-start
  7.2 45.8 %all-gather = bf16[1,512,896]{2,1,0:T(8,128)(2,1)S(1)} all-gather(bf16[1,128,896]{2,1,0:T(8,128)(2,1)} %param.8), channel_id=2, replica_groups=mesh['segment'=4,'y'=4,'zhi'=4,'zlo'=4,'core'=2] {'zhi'}, dimensions={1}, use_global_device_ids=true | all-gather | bytes 1146880 | tf_op jit(solution)/shard_map/all_gather | solution.py:42
  53.0 0.3 broadcast_in_dim.10
  53.3 43.4 %all_to_all.50 = bf16[4,512,896]{2,1,0:T(8,128)(2,1)S(1)} all-to-all(bf16[4,512,896]{2,1,0:T(8,128)(2,1)S(1)} %broadcast_in_dim.10), channel_id=1, replica_groups=mesh['segment'=4,'y'=4,'zhi'=4,'zlo'=4,'core'=2] {'y'}, dimensions={0} | all-to-all | bytes 7340032 | tf_op jit(solution)/shard_map/all_to_all | solution.py:18
  96.7 0.0 copy-done
  96.7 2.1 convolution_convert_fusion
  98.8 0.1 copy.47
  98.9 32.4 %all_to_all.51 = bf16[8,256,448]{1,2,0:T(8,128)(2,1)S(1)} all-to-all(bf16[8,256,448]{1,2,0:T(8,128)(2,1)S(1)} %bitcast.68), channel_id=1, replica_groups=mesh['segment'=4,'y'=4,'zhi'=4,'zlo'=4,'core'=2] {'segment','core'}, dimensions={0} | all-to-all | bytes 3670016 | tf_op jit(solution)/shard_map/all_to_all | solution.py:49
  131.4 0.3 convert_reduce_fusion
  131.6 0.2 copy.36
  131.8 16.0 %all_to_all.52 = f32[4,64,448]{2,1,0:T(8,128)S(1)} all-to-all(f32[4,64,448]{2,1,0:T(8,128)S(1)} %bitcast.74), channel_id=1, replica_groups=mesh['segment'=4,'y'=4,'zhi'=4,'zlo'=4,'core'=2] {'zlo'}, dimensions={0} | all-to-all | bytes 917504 | tf_op jit(solution)/shard_map/all_to_all | solution.py:24
  147.8 0.1 multiply_reduce_fusion.1
  147.9 6.9 %psum.14 = f32[64]{0:T(128)S(1)} all-reduce(f32[64]{0:T(128)S(1)} %multiply_reduce_fusion.1), channel_id=1, replica_groups=mesh['segment'=4,'y'=4,'zhi'=4,'zlo'=4,'core'=2] {'y'}, use_global_device_ids=true, to_apply=%region_6.0 | all-reduce | flops 64 | bytes 512 | tf_op jit(solution)/shard_map/psum | solution.py:55
  154.8 12.1 %psum.15 = f32[64]{0:T(128)S(1)} all-reduce(f32[64]{0:T(128)S(1)} %psum.14), channel_id=1, replica_groups=mesh['segment'=4,'y'=4,'zhi'=4,'zlo'=4,'core'=2] {'zhi'}, use_global_device_ids=true, to_apply=%region_7.0 | all-reduce | flops 64 | bytes 512 | tf_op jit(solution)/shard_map/psum | solution.py:56
  166.9 0.0 copy-done.5
  166.9 0.1 multiply_convert_fusion.1
  167.0 11.2 %all_gather.10 = bf16[256,448]{1,0:T(8,128)(2,1)S(1)} all-gather(bf16[64,448]{1,0:T(8,128)(2,1)S(1)} %multiply_convert_fusion.1), channel_id=1, replica_groups=mesh['segment'=4,'y'=4,'zhi'=4,'zlo'=4,'core'=2] {'zlo'}, dimensions={0}, use_global_device_ids=true | all-gather | bytes 286720 | tf_op jit(solution)/shard_map/all_gather | solution.py:60
  178.2 0.1 copy.37
  178.3 0.1 broadcast_in_dim.11
  178.5 34.6 %all_to_all.53 = bf16[8,256,448]{1,2,0:T(8,128)(2,1)S(1)} all-to-all(bf16[8,256,448]{1,2,0:T(8,128)(2,1)S(1)} %broadcast_in_dim.11), channel_id=1, replica_groups=mesh['segment'=4,'y'=4,'zhi'=4,'zlo'=4,'core'=2] {'segment','core'}, dimensions={0} | all-to-all | bytes 3670016 | tf_op jit(solution)/shard_map/all_to_all | solution.py:62
  213.1 0.2 copy.45
  213.3 0.8 copy-done.1
  214.1 3.2 fusion.6
  217.3 0.0 reduce-scatter.3.cloned.1.call-update
  217.3 0.0 reduce-scatter.5.cloned.1.call-start
  217.4 46.3 %reduce-scatter.3.cloned.1.call-done = f32[512,500]{0,1:T(8,128)} async-done(((f32[2048,500]{0,1:T(8,128)}), f32[512,500]{0,1:T(8,128)}) %reduce-scatter.3.cloned.1.call-update) | async-done | bytes 1024016 | tf_op jit(solution)/shard_map/reduce_scatter | solution.py:67
  263.7 0.0 reduce-scatter.5.cloned.1.call-update
  263.7 0.0 copy-done.2
  263.8 0.0 copy-done.6
  263.8 0.2 reduce-window.8
  264.0 0.1 compare_reduce_fusion
  264.1 0.0 copy-done.4
  264.1 61.3 %reduce-scatter.5.cloned.1.call-done = f32[128,500]{0,1:T(8,128)} async-done(((f32[512,500]{0,1:T(8,128)}), f32[128,500]{0,1:T(8,128)}) %reduce-scatter.5.cloned.1.call-update) | async-done | bytes 256016 | tf_op jit(solution)/shard_map/reduce_scatter | solution.py:68
  325.4 1.0 reduce_max.18
  326.4 1.0 exponential_reduce_fusion
  327.5 1.3 multiply_reduce_fusion
  328.7 0.6 reshape.88
  329.4 6.9 %all-to-all-start.4 = ((f32[32,3,128]{2,1,0:T(4,128)}), f32[32,3,128]{2,1,0:T(4,128)S(1)}, u32[]{:S(2)}, u32[]{:S(2)}) async-start(f32[32,3,128]{2,1,0:T(4,128)} %reshape.88), calls=%async_computation.6 | async-start | bytes 131072 | tf_op jit(solution)/shard_map/all_to_all | solution.py:18
  336.3 7.8 %all-to-all-done.4 = f32[32,3,128]{2,1,0:T(4,128)S(1)} async-done(((f32[32,3,128]{2,1,0:T(4,128)}), f32[32,3,128]{2,1,0:T(4,128)S(1)}, u32[]{:S(2)}, u32[]{:S(2)}) %all-to-all-start.4) | async-done | bytes 49184 | tf_op jit(solution)/shard_map/all_to_all | solution.py:18
  344.2 1.3 multiply_convert_fusion
  345.5 0.1 concatenate.3
  345.6 40.3 %all_gather.11 = bf16[512,504]{0,1:T(8,128)(2,1)S(1)} all-gather(bf16[128,504]{0,1:T(8,128)(2,1)S(1)} %concatenate.3), channel_id=1, replica_groups=mesh['segment'=4,'y'=4,'zhi'=4,'zlo'=4,'core'=2] {'zhi'}, dimensions={0}, use_global_device_ids=true | all-gather | bytes 645120 | tf_op jit(solution)/shard_map/all_gather | solution.py:115
  385.8 0.1 broadcast_in_dim.12
  386.0 28.3 %all_to_all.54 = bf16[4,512,504]{1,2,0:T(8,128)(2,1)} all-to-all(bf16[4,512,504]{1,2,0:T(8,128)(2,1)S(1)} %broadcast_in_dim.12), channel_id=1, replica_groups=mesh['segment'=4,'y'=4,'zhi'=4,'zlo'=4,'core'=2] {'y'}, dimensions={0} | all-to-all | bytes 4128768 | tf_op jit(solution)/shard_map/all_to_all | solution.py:18
  414.3 4.1 copy.41
  418.4 2.8 convert_reduce_fusion.1
  421.3 3.6 fusion
  (22 shorter events, 0.2 us)
Async XLA Ops:
  7.2 89.5 %copy-start = (bf16[1,896,448]{1,2,0:T(8,128)(2,1)S(1)}, bf16[1,896,448]{1,2,0:T(8,128)(2,1)}, u32[]{:S(2)}) copy-start(bf16[1,896,448]{1,2,0:T(8,128)(2,1)} %param.9) | copy-start | bytes 2408452
  7.2 256.5 %reduce-scatter.3.cloned.1.call-start = ((), (), s32[]{:S(2)}) async-start(), calls=%async_computation.8 | async-start | bytes 5160960 | tf_op jit(solution)/shard_map/reduce_scatter | solution.py:67
  131.4 35.5 %copy-start.5 = (f32[448]{0:T(512)S(1)}, f32[448]{0:T(512)}, u32[]{:S(2)}) copy-start(f32[448]{0:T(512)} %param.10) | copy-start | bytes 5380
  213.1 1.0 copy-start.1
  217.3 46.4 %copy-start.2 = (f32[128,8]{0,1:T(8,128)S(1)}, f32[128,8]{0,1:T(8,128)}, u32[]{:S(2)}) copy-start(f32[128,8]{0,1:T(8,128)} %param.15) | copy-start | bytes 12292
  217.3 46.5 %copy-start.6 = (s32[12]{0:T(128)S(1)}, s32[12]{0:T(128)}, u32[]{:S(2)}) copy-start(s32[12]{0:T(128)} %param.12) | copy-start | bytes 148
  217.3 46.8 %copy-start.4 = (s32[128,8]{0,1:T(8,128)S(1)}, s32[128,8]{0,1:T(8,128)}, u32[]{:S(2)}) copy-start(s32[128,8]{0,1:T(8,128)} %param.14) | copy-start | bytes 12292
  217.3 110.2 %copy-start.3 = (s32[128]{0:T(128)S(1)}, s32[128]{0:T(128)}, u32[]{:S(2)}) copy-start(s32[128]{0:T(128)} %param.13) | copy-start | bytes 1540
  217.3 108.1 %reduce-scatter.5.cloned.1.call-start = ((), (), s32[]{:S(2)}) async-start(), calls=%async_computation.9 | async-start | bytes 1290240 | tf_op jit(solution)/shard_map/reduce_scatter | solution.py:68
  329.4 14.7 %all-to-all-start.4 = ((f32[32,3,128]{2,1,0:T(4,128)}), f32[32,3,128]{2,1,0:T(4,128)S(1)}, u32[]{:S(2)}, u32[]{:S(2)}) async-start(f32[32,3,128]{2,1,0:T(4,128)} %reshape.88), calls=%async_computation.6 | async-start | bytes 131072 | tf_op jit(solution)/shard_map/all_to_all | solution.py:18
Sparse Core Ops, SparseCore 0:
  217.5 46.1 reduce-scatter.2
  266.8 58.5 reduce-scatter.4

commit v6 on v5

v6 whole, which is shorter than its diff:
```python
import jax
import jax.numpy as jnp
from jax import lax
from jax.sharding import Mesh
from jax.sharding import PartitionSpec as P

D = 7168
VOCAB = 16000

norm_eps = 1e-06

SEQ = ("y", "zhi")
SM = ("segment", "zlo", "core")


def spread_gather(value, axes, size):
    spread = jnp.broadcast_to(value[None], (size,) + value.shape)
    return lax.all_to_all(
        spread.reshape((size * value.shape[0],) + value.shape[1:]), axes, 0, 0, tiled=True
    )


def scatter_sum(value, axes, size):
    pieces = lax.all_to_all(value, axes, 0, 0, tiled=True)
    return jnp.sum(pieces.reshape((size, value.shape[0] // size) + value.shape[1:]), axis=0)


def half_pipeline(sources, unite_weight, norm_gain, head_weight, sizes):
    n_sm = sizes["segment"] * sizes["zlo"] * sizes["core"]

    rows = lax.all_gather(sources[0], "zhi", axis=0, tiled=True)
    rows = spread_gather(rows, "y", sizes["y"])
    tokens = rows.shape[0]
    product = jnp.dot(rows, unite_weight[0], preferred_element_type=jnp.float32)
    product = lax.optimization_barrier(product.astype(jnp.bfloat16))

    n_sc = sizes["segment"] * sizes["core"]
    pieces = lax.all_to_all(product, ("segment", "core"), 0, 0, tiled=True)
    chunk = tokens // n_sc
    united = jnp.sum(pieces.reshape(n_sc, chunk, -1).astype(jnp.float32), axis=0)
    united = scatter_sum(united, "zlo", sizes["zlo"])

    squares = jnp.sum(united * united, axis=1)
    squares = lax.psum(squares, "y")
    squares = lax.psum(squares, "zhi")
    hidden_part = (
        united * lax.rsqrt(squares / D + norm_eps)[:, None] * norm_gain[None, :]
    ).astype(jnp.bfloat16)
    hidden_chunk = lax.all_gather(hidden_part, "zlo", axis=0, tiled=True)
    spread = jnp.broadcast_to(hidden_chunk[None], (n_sc,) + hidden_chunk.shape)
    hidden = lax.all_to_all(
        spread.reshape(tokens, -1), ("segment", "core"), 0, 0, tiled=True
    )

    logits = jnp.dot(hidden, head_weight, preferred_element_type=jnp.float32)
    return hidden, logits


def reduce_logits(logits):
    logits = lax.psum_scatter(logits, "y", scatter_dimension=0, tiled=True)
    return lax.psum_scatter(logits, "zhi", scatter_dimension=0, tiled=True)


def finish_half(
    hidden,
    logits,
    head_weight,
    doc_lengths,
    target_ids,
    teacher_ids,
    teacher_probs,
    sizes,
    first,
    block,
):
    tok_local = target_ids.shape[0]

    seq_index = lax.axis_index("y") * sizes["zhi"] + lax.axis_index("zhi")
    positions = seq_index * block + first + jnp.arange(tok_local, dtype=jnp.int32)
    vocab_width = head_weight.shape[1]
    offset = lax.axis_index(SM) * vocab_width
    columns = offset + jnp.arange(vocab_width, dtype=jnp.int32)
    target_weight = (target_ids[:, None] == columns[None, :]).astype(jnp.float32)
    for top_slot in range(teacher_ids.shape[1]):
        hits = (teacher_ids[:, top_slot : top_slot + 1] == columns[None, :]).astype(
            jnp.float32
        )
        target_weight = target_weight + teacher_probs[:, top_slot : top_slot + 1] * hits

    row_peak = jnp.max(logits, axis=1)
    stats = jnp.stack(
        [
            row_peak,
            jnp.sum(jnp.exp(logits - row_peak[:, None]), axis=1),
            jnp.sum(target_weight * logits, axis=1),
        ]
    )
    n_sm = sizes["segment"] * sizes["zlo"] * sizes["core"]
    every = spread_gather(stats[None], SM, n_sm)
    peak = jnp.max(every[:, 0], axis=0)
    total = jnp.sum(every[:, 1] * jnp.exp(every[:, 0] - peak[None]), axis=0)
    lse = peak + jnp.log(total)
    picked = jnp.sum(every[:, 2], axis=0)

    target_mass = 1.0 + jnp.sum(teacher_probs, axis=1)
    doc_ends = jnp.cumsum(doc_lengths)
    is_last = jnp.any(positions[:, None] + 1 == doc_ends[None, :], axis=1)
    in_vocab = (target_ids < VOCAB).astype(jnp.float32)
    valid_rows = jnp.where(is_last, 0.0, in_vocab)
    per_token = valid_rows * (target_mass * lse - picked)
    loss_hi = per_token.astype(jnp.bfloat16)
    loss_lo = (per_token - loss_hi.astype(jnp.float32)).astype(jnp.bfloat16)

    logit_grad = (
        valid_rows[:, None]
        * (target_mass[:, None] * jnp.exp(logits - lse[:, None]) - target_weight)
    ).astype(jnp.bfloat16)
    extra = jnp.stack(
        [loss_hi, loss_lo, valid_rows.astype(jnp.bfloat16), jnp.zeros_like(loss_hi)],
        axis=1,
    )
    carried = jnp.concatenate([logit_grad, extra], axis=1)
    carried = lax.all_gather(carried, "zhi", axis=0, tiled=True)
    carried = spread_gather(carried, "y", sizes["y"])

    loss_sum = jnp.sum(
        carried[:, vocab_width].astype(jnp.float32)
        + carried[:, vocab_width + 1].astype(jnp.float32)
    )
    count = jnp.sum(carried[:, vocab_width + 2].astype(jnp.float32))

    head_grad = lax.dot_general(
        hidden,
        carried[:, :vocab_width],
        (((0,), (0,)), ((), ())),
        preferred_element_type=jnp.float32,
    )
    return loss_sum, count, head_grad


def on_device(
    sources,
    unite_weight,
    norm_gain,
    head_weight,
    doc_lengths,
    target_ids,
    teacher_ids,
    teacher_probs,
    sizes,
    halves,
):
    block = sources.shape[1]
    width = block // halves
    cuts = [slice(h * width, (h + 1) * width) for h in range(halves)]
    fronts, reduced = [], []
    gate = None
    for h, cut in enumerate(cuts):
        part = sources[:, cut]
        if gate is not None:
            part = lax.optimization_barrier((part, gate))[0]
        hidden, logits = half_pipeline(part, unite_weight, norm_gain, head_weight, sizes)
        fronts.append(hidden)
        reduced.append(reduce_logits(logits))
        gate = logits
    loss_sum, count, head_grad = 0.0, 0.0, None
    for h, cut in enumerate(cuts):
        logits = reduced[h]
        if h + 1 < halves:
            logits = lax.optimization_barrier((logits, fronts[h + 1]))[0]
        part_loss, part_count, part_grad = finish_half(
            fronts[h],
            logits,
            head_weight,
            doc_lengths,
            target_ids[cut],
            teacher_ids[cut],
            teacher_probs[cut],
            sizes,
            h * width,
            block,
        )
        loss_sum = loss_sum + part_loss
        count = count + part_count
        head_grad = part_grad if head_grad is None else head_grad + part_grad
    mean_loss = loss_sum / jnp.maximum(count, 1.0)
    return (mean_loss, head_grad)


def solution(mesh):
    n_seg, n_seq, n_mp = (mesh.shape[a] for a in ("segment", "seq", "mp"))
    sizes = {"segment": n_seg, "y": n_seq // 4, "zhi": 4, "zlo": n_mp // 2, "core": 2}
    fine = Mesh(
        mesh.devices.reshape(n_seg, sizes["y"], sizes["zhi"], sizes["zlo"], sizes["core"]),
        ("segment", "y", "zhi", "zlo", "core"),
    )
    placed = (
        P("segment", SEQ, ("zlo", "core")),
        P("segment", ("zlo", "core"), SEQ),
        P(SEQ),
        P(SEQ, SM),
        P(),
        P(SEQ),
        P(SEQ, None),
        P(SEQ, None),
    )

    def body(*args):
        return on_device(*args, sizes=sizes, halves=2)

    return jax.shard_map(
        body,
        mesh=fine,
        in_specs=placed,
        out_specs=(P(), P(SEQ, SM)),
        check_vma=False,
    )
```

time: 436 us -> 500 us (1.15); the launches traced: 434 us -> 492 us
  starting transfers between devices: 6.95 us -> 41.7 us
  waiting for transfers between devices: 115 us -> 132 us
  local copies, waits for them, and re-layouts: 6.9 us -> 20.1 us
  blocking collectives: 271 us -> 258 us
    reduce_scatter x2, waiting for transfers between devices: 108 us -> 35.4 us  [reduce_logits(): logits = lax.psum_scatter(logits, 'y', scatter_dimension=0, tiled=True)]
    unnamed x2 -> x6, waiting for transfers between devices: 0.03 us -> 52.4 us
    all_to_all x2 -> x1, blocking collectives: 71.8 us -> 22.8 us  [spread_gather(): lax.all_to_all(spread.reshape((size * value.shape[0],) + value.shape[1:])...]
    all_to_all x1 -> x5, waiting for transfers between devices: 7.77 us -> 32.5 us  [spread_gather(): lax.all_to_all(spread.reshape((size * value.shape[0],) + value.shape[1:])...]
    all_to_all x1 -> x5, starting transfers between devices: 6.87 us -> 28 us  [spread_gather(): lax.all_to_all(spread.reshape((size * value.shape[0],) + value.shape[1:])...]
    psum x2 -> x4, blocking collectives: 19 us -> 35.7 us  [the longest x2 21.9 us: half_pipeline(): squares = lax.psum(squares, 'zhi')]
    all_to_all x0 -> x1, starting transfers between devices: none -> 13.6 us  [half_pipeline(): lax.all_to_all(spread.reshape(tokens, -1), ('segment', 'core'), 0, 0, til...]
    all_to_all x0 -> x1, waiting for transfers between devices: none -> 11.6 us  [half_pipeline(): lax.all_to_all(spread.reshape(tokens, -1), ('segment', 'core'), 0, 0, til...]
  transfers between devices with their start and end apart: 3 -> 10, of which waited for: 3 -> 7; matrix products, arithmetic and copies ran while one was open for 0% -> 4% of each run, Pallas kernels for 0% -> 0%
where the time goes in v6:
time: 500 us; the launch traced here: 492 us
  blocking collectives  258 us (52%)
  waiting for transfers between devices  132 us (26%)
  starting transfers between devices  41.7 us (8%)
  local copies, waits for them, and re-layouts  20.1 us (4%)
  between operations  17.8 us (4%)
  matrix products  12.6 us (3%)
  other arithmetic  9.93 us (2%)
    unnamed x6, waiting for transfers between devices  52.4 us
    all_gather x2, blocking collectives, half_pipeline(): rows = lax.all_gather(sources[0], 'zhi', axis=0, tiled=True)  51.1 us
    all_to_all x2, blocking collectives, half_pipeline(): pieces = lax.all_to_all(product, ('segment', 'core'), 0, 0, tiled=True)  48.6 us
    reduce_scatter x2, waiting for transfers between devices, reduce_logits(): logits = lax.psum_scatter(logits, 'y', scatter_dimension=0, tiled=True)  35.4 us
    all_gather x2, blocking collectives, finish_half(): carried = lax.all_gather(carried, 'zhi', axis=0, tiled=True)  34 us
    all_to_all x5, waiting for transfers between devices, spread_gather(): lax.all_to_all(spread.reshape((size * value.shape[0],) + value.shape[1:])...  32.5 us
    all_to_all x5, starting transfers between devices, spread_gather(): lax.all_to_all(spread.reshape((size * value.shape[0],) + value.shape[1:])...  28 us
    all_to_all x1, blocking collectives, half_pipeline(): lax.all_to_all(spread.reshape(tokens, -1), ('segment', 'core'), 0, 0, til...  25.7 us
  transfers between devices with their start and end apart: 10, of which 7 were waited for; matrix products, arithmetic and copies ran while one was open for 4% of the time, Pallas kernels for 0%

profile of v6, /device:TPU:1, one launch (start us, length us, event | category | flops | bytes accessed | tf_op | source)
XLA Modules:
  0.0 492.0 jit_solution(10683863820929576948)
XLA Ops:
  7.2 1.0 fusion.15
  8.2 29.5 %all-gather = bf16[1,256,896]{2,1,0:T(8,128)(2,1)S(1)} all-gather(bf16[1,64,896]{2,1,0:T(8,128)(2,1)S(1)} %get-tuple-element.25), channel_id=2, replica_groups=mesh['segment'=4,'y'=4,'zhi'=4,'zlo'=4,'core'=2] {'zhi'}, dimensions={1}, use_global_device_ids=true | all-gather | bytes 573440 | tf_op jit(solution)/shard_map/all_gather | solution.py:31
  37.9 22.8 %all_to_all.100 = bf16[4,256,896]{2,1,0:T(8,128)(2,1)S(1)} all-to-all(bf16[4,256,896]{2,1,0:T(8,128)(2,1)S(1)} %broadcast_in_dim.17), channel_id=1, replica_groups=mesh['segment'=4,'y'=4,'zhi'=4,'zlo'=4,'core'=2] {'y'}, dimensions={0} | all-to-all | bytes 3670016 | tf_op jit(solution)/shard_map/all_to_all | solution.py:18
  60.7 1.1 convolution_convert_fusion.1
  62.1 23.5 %all_to_all.101 = bf16[8,128,448]{1,2,0:T(8,128)(2,1)S(1)} all-to-all(bf16[8,128,448]{1,2,0:T(8,128)(2,1)S(1)} %copy_bitcast_fusion.2), channel_id=1, replica_groups=mesh['segment'=4,'y'=4,'zhi'=4,'zlo'=4,'core'=2] {'segment','core'}, dimensions={0} | all-to-all | bytes 1835008 | tf_op jit(solution)/shard_map/all_to_all | solution.py:38
  85.9 8.9 %all_to_all.102 = f32[4,32,448]{2,1,0:T(8,128)S(1)} all-to-all(f32[4,32,448]{2,1,0:T(8,128)S(1)} %bitcast.156), channel_id=1, replica_groups=mesh['segment'=4,'y'=4,'zhi'=4,'zlo'=4,'core'=2] {'zlo'}, dimensions={0} | all-to-all | bytes 458752 | tf_op jit(solution)/shard_map/all_to_all | solution.py:24
  94.9 6.9 %psum.28 = f32[32]{0:T(128)S(1)} all-reduce(f32[32]{0:T(128)S(1)} %multiply_reduce_fusion.3), channel_id=1, replica_groups=mesh['segment'=4,'y'=4,'zhi'=4,'zlo'=4,'core'=2] {'y'}, use_global_device_ids=true, to_apply=%region_6.0 | all-reduce | flops 32 | bytes 256 | tf_op jit(solution)/shard_map/psum | solution.py:44
  101.8 11.5 %psum.29 = f32[32]{0:T(128)S(1)} all-reduce(f32[32]{0:T(128)S(1)} %psum.28), channel_id=1, replica_groups=mesh['segment'=4,'y'=4,'zhi'=4,'zlo'=4,'core'=2] {'zhi'}, use_global_device_ids=true, to_apply=%region_7.0 | all-reduce | flops 32 | bytes 256 | tf_op jit(solution)/shard_map/psum | solution.py:45
  113.3 11.6 %all_gather.19 = bf16[128,448]{1,0:T(8,128)(2,1)S(1)} all-gather(bf16[32,448]{1,0:T(8,128)(2,1)S(1)} %multiply_convert_fusion.3), channel_id=1, replica_groups=mesh['segment'=4,'y'=4,'zhi'=4,'zlo'=4,'core'=2] {'zlo'}, dimensions={0}, use_global_device_ids=true | all-gather | bytes 143360 | tf_op jit(solution)/shard_map/all_gather | solution.py:49
  125.2 25.7 %all_to_all.103 = bf16[8,128,448]{1,2,0:T(8,128)(2,1)S(1)} all-to-all(bf16[8,128,448]{1,2,0:T(8,128)(2,1)S(1)} %broadcast_in_dim.18), channel_id=1, replica_groups=mesh['segment'=4,'y'=4,'zhi'=4,'zlo'=4,'core'=2] {'segment','core'}, dimensions={0} | all-to-all | bytes 1835008 | tf_op jit(solution)/shard_map/all_to_all | solution.py:51
  151.8 2.1 fusion.4
  153.9 21.6 %all-gather.1 = bf16[1,256,896]{2,1,0:T(8,128)(2,1)S(1)} all-gather(bf16[1,64,896]{2,1,0:T(8,128)(2,1)S(1)} %get-tuple-element.4), channel_id=3, replica_groups=mesh['segment'=4,'y'=4,'zhi'=4,'zlo'=4,'core'=2] {'zhi'}, dimensions={1}, use_global_device_ids=true | all-gather | bytes 573440 | tf_op jit(solution)/shard_map/all_gather | solution.py:31
  175.5 1.4 broadcast_in_dim.19
  176.9 3.6 all-to-all-start.4
  181.2 22.1 %all-to-all-done.4 = bf16[4,256,896]{2,1,0:T(8,128)(2,1)S(1)} async-done(((bf16[4,256,896]{2,1,0:T(8,128)(2,1)}), bf16[4,256,896]{2,1,0:T(8,128)(2,1)S(1)}, u32[]{:S(2)}, u32[]{:S(2)}) %all-to-all-start.4) | async-done | bytes 1835040 | tf_op jit(solution)/shard_map/all_to_all | solution.py:18
  203.3 1.1 convolution_convert_fusion
  204.6 25.1 %all_to_all.104 = bf16[8,128,448]{1,2,0:T(8,128)(2,1)S(1)} all-to-all(bf16[8,128,448]{1,2,0:T(8,128)(2,1)S(1)} %copy_bitcast_fusion.1), channel_id=1, replica_groups=mesh['segment'=4,'y'=4,'zhi'=4,'zlo'=4,'core'=2] {'segment','core'}, dimensions={0} | all-to-all | bytes 1835008 | tf_op jit(solution)/shard_map/all_to_all | solution.py:38
  229.9 8.7 %all_to_all.105 = f32[4,32,448]{2,1,0:T(8,128)S(1)} all-to-all(f32[4,32,448]{2,1,0:T(8,128)S(1)} %bitcast.157), channel_id=1, replica_groups=mesh['segment'=4,'y'=4,'zhi'=4,'zlo'=4,'core'=2] {'zlo'}, dimensions={0} | all-to-all | bytes 458752 | tf_op jit(solution)/shard_map/all_to_all | solution.py:24
  238.8 6.9 %psum.30 = f32[32]{0:T(128)S(1)} all-reduce(f32[32]{0:T(128)S(1)} %multiply_reduce_fusion.2), channel_id=1, replica_groups=mesh['segment'=4,'y'=4,'zhi'=4,'zlo'=4,'core'=2] {'y'}, use_global_device_ids=true, to_apply=%region_13.0 | all-reduce | flops 32 | bytes 256 | tf_op jit(solution)/shard_map/psum | solution.py:44
  245.7 10.4 %psum.31 = f32[32]{0:T(128)S(1)} all-reduce(f32[32]{0:T(128)S(1)} %psum.30), channel_id=1, replica_groups=mesh['segment'=4,'y'=4,'zhi'=4,'zlo'=4,'core'=2] {'zhi'}, use_global_device_ids=true, to_apply=%region_14.0 | all-reduce | flops 32 | bytes 256 | tf_op jit(solution)/shard_map/psum | solution.py:45
  256.2 10.9 %all_gather.21 = bf16[128,448]{1,0:T(8,128)(2,1)S(1)} all-gather(bf16[32,448]{1,0:T(8,128)(2,1)S(1)} %multiply_convert_fusion.2), channel_id=1, replica_groups=mesh['segment'=4,'y'=4,'zhi'=4,'zlo'=4,'core'=2] {'zlo'}, dimensions={0}, use_global_device_ids=true | all-gather | bytes 143360 | tf_op jit(solution)/shard_map/all_gather | solution.py:49
  267.3 1.0 broadcast_in_dim.20
  268.4 13.6 %all-to-all-start.7 = ((bf16[8,128,448]{1,2,0:T(8,128)(2,1)}), bf16[8,128,448]{1,2,0:T(8,128)(2,1)S(1)}, u32[]{:S(2)}, u32[]{:S(2)}) async-start(bf16[8,128,448]{1,2,0:T(8,128)(2,1)} %broadcast_in_dim.20), calls=%async_computation.8 | async-start | bytes 1835008 | tf_op jit(solution)/shard_map/all_to_all | solution.py:51
  282.0 2.0 copy.94
  284.1 11.6 %all-to-all-done.7 = bf16[8,128,448]{1,2,0:T(8,128)(2,1)S(1)} async-done(((bf16[8,128,448]{1,2,0:T(8,128)(2,1)}), bf16[8,128,448]{1,2,0:T(8,128)(2,1)S(1)}, u32[]{:S(2)}, u32[]{:S(2)}) %all-to-all-start.7) | async-done | bytes 917536 | tf_op jit(solution)/shard_map/all_to_all | solution.py:51
  295.7 2.1 fusion.12
  299.0 24.6 %reduce-scatter.13.cloned.1.call-done = f32[64,500]{1,0:T(8,128)} async-done(((f32[256,500]{1,0:T(8,128)}), f32[64,500]{1,0:T(8,128)}) %reduce-scatter.13.cloned.1.call-update) | async-done | bytes 128016
  323.6 1.0 copy.95
  325.1 35.3 %reduce-scatter.11.cloned.1.call-done = f32[256,500]{0,1:T(8,128)} async-done(((f32[1024,500]{0,1:T(8,128)}), f32[256,500]{0,1:T(8,128)}) %reduce-scatter.11.cloned.1.call-update) | async-done | bytes 512016 | tf_op jit(solution)/shard_map/reduce_scatter | solution.py:60
  360.5 2.0 copy.96
  363.3 8.0 %all-to-all-start.8 = ((f32[32,1,192]{2,1,0:T(1,128)}), f32[32,1,192]{2,1,0:T(1,128)S(1)}, u32[]{:S(2)}, u32[]{:S(2)}) async-start(f32[32,1,192]{2,1,0:T(1,128)} %reshape.149), calls=%async_computation.9 | async-start | bytes 65536 | tf_op jit(solution)/shard_map/all_to_all | solution.py:18
  371.3 7.4 %all-to-all-done.8 = f32[32,1,192]{2,1,0:T(1,128)S(1)} async-done(((f32[32,1,192]{2,1,0:T(1,128)}), f32[32,1,192]{2,1,0:T(1,128)S(1)}, u32[]{:S(2)}, u32[]{:S(2)}) %all-to-all-start.8) | async-done | bytes 24608 | tf_op jit(solution)/shard_map/all_to_all | solution.py:18
  380.8 27.0 %reduce-scatter.15.cloned.1.call-done = f32[64,500]{1,0:T(8,128)} async-done(((f32[256,500]{1,0:T(8,128)}), f32[64,500]{1,0:T(8,128)}) %reduce-scatter.15.cloned.1.call-update) | async-done | bytes 128016
  408.9 1.0 copy.97
  411.1 8.5 %all-to-all-start.10 = ((f32[32,1,192]{2,1,0:T(1,128)}), f32[32,1,192]{2,1,0:T(1,128)S(1)}, u32[]{:S(2)}, u32[]{:S(2)}) async-start(f32[32,1,192]{2,1,0:T(1,128)} %reshape.151), calls=%async_computation.12 | async-start | bytes 65536 | tf_op jit(solution)/shard_map/all_to_all | solution.py:18
  419.5 18.4 %all_gather.22 = bf16[256,504]{1,0:T(8,128)(2,1)S(1)} all-gather(bf16[64,504]{1,0:T(8,128)(2,1)S(1)} %copy.86), channel_id=1, replica_groups=mesh['segment'=4,'y'=4,'zhi'=4,'zlo'=4,'core'=2] {'zhi'}, dimensions={0}, use_global_device_ids=true | all-gather | bytes 322560 | tf_op jit(solution)/shard_map/all_gather | solution.py:123
  438.1 1.1 broadcast_in_dim.21
  439.1 3.8 all-to-all-start.9
  444.5 15.6 %all_gather.23 = bf16[256,504]{1,0:T(8,128)(2,1)S(1)} all-gather(bf16[64,504]{1,0:T(8,128)(2,1)S(1)} %copy.91), channel_id=1, replica_groups=mesh['segment'=4,'y'=4,'zhi'=4,'zlo'=4,'core'=2] {'zhi'}, dimensions={0}, use_global_device_ids=true | all-gather | bytes 322560 | tf_op jit(solution)/shard_map/all_gather | solution.py:123
  460.2 1.1 broadcast_in_dim.22
  461.3 4.1 all-to-all-start.11
  465.5 1.3 copy.88
  466.8 2.2 convert_reduce_fusion.3
  469.0 3.1 fusion.1
  472.1 3.0 all-to-all-done.11
  475.1 1.3 copy.93
  476.5 2.3 convert_reduce_fusion.2
  481.3 3.1 convolution_add_fusion
  (94 shorter events, 12.0 us)
Async XLA Ops:
  7.2 53.6 %copy-start = (bf16[1,896,448]{1,2,0:T(8,128)(2,1)S(1)}, bf16[1,896,448]{1,2,0:T(8,128)(2,1)}, u32[]{:S(2)}) copy-start(bf16[1,896,448]{1,2,0:T(8,128)(2,1)} %param.9) | copy-start | bytes 2408452
  62.1 51.2 %copy-start.7 = (f32[448]{0:T(512)S(1)}, f32[448]{0:T(512)}, u32[]{:S(2)}) copy-start(f32[448]{0:T(512)} %param.10) | copy-start | bytes 5380
  94.7 57.1 %copy-start.4 = (bf16[448,500]{1,0:T(8,128)(2,1)S(1)}, bf16[448,500]{1,0:T(8,128)(2,1)}, u32[]{:S(2)}) copy-start(bf16[448,500]{1,0:T(8,128)(2,1)} %param.11) | copy-start | bytes 1344004
  150.9 0.9 copy-start.1
  176.9 26.4 %all-to-all-start.4 = ((bf16[4,256,896]{2,1,0:T(8,128)(2,1)}), bf16[4,256,896]{2,1,0:T(8,128)(2,1)S(1)}, u32[]{:S(2)}, u32[]{:S(2)}) async-start(bf16[4,256,896]{2,1,0:T(8,128)(2,1)} %broadcast_in_dim.19), calls=%async_computation.5 | async-start | bytes 3670016 | tf_op jit(solution)/shard_map/all_to_all | solution.py:18
  180.5 101.5 %reduce-scatter.9.cloned.1.call-start = ((), (), s32[]{:S(2)}) async-start(), calls=%async_computation.16 | async-start | bytes 2580480 | tf_op jit(solution)/shard_map/reduce_scatter | solution.py:60
  268.4 27.3 %all-to-all-start.7 = ((bf16[8,128,448]{1,2,0:T(8,128)(2,1)}), bf16[8,128,448]{1,2,0:T(8,128)(2,1)S(1)}, u32[]{:S(2)}, u32[]{:S(2)}) async-start(bf16[8,128,448]{1,2,0:T(8,128)(2,1)} %broadcast_in_dim.20), calls=%async_computation.8 | async-start | bytes 1835008 | tf_op jit(solution)/shard_map/all_to_all | solution.py:51
  282.0 41.6 %reduce-scatter.13.cloned.1.call-start = ((), (), s32[]{:S(2)}) async-start(), calls=%async_computation.18 | async-start | bytes 655360
  284.0 76.4 %reduce-scatter.11.cloned.1.call-start = ((), (), s32[]{:S(2)}) async-start(), calls=%async_computation.17 | async-start | bytes 2580480 | tf_op jit(solution)/shard_map/reduce_scatter | solution.py:60
  295.7 2.1 copy-start.2
  297.7 0.7 copy-start.9
  297.7 0.9 copy-start.8
  297.7 1.1 copy-start.6
  297.7 1.2 copy-start.5
  297.8 110.0 %reduce-scatter.15.cloned.1.call-start = ((), (), s32[]{:S(2)}) async-start(), calls=%async_computation.19 | async-start | bytes 655360
  363.3 15.5 %all-to-all-start.8 = ((f32[32,1,192]{2,1,0:T(1,128)}), f32[32,1,192]{2,1,0:T(1,128)S(1)}, u32[]{:S(2)}, u32[]{:S(2)}) async-start(f32[32,1,192]{2,1,0:T(1,128)} %reshape.149), calls=%async_computation.9 | async-start | bytes 65536 | tf_op jit(solution)/shard_map/all_to_all | solution.py:18
  411.1 27.0 %all-to-all-start.10 = ((f32[32,1,192]{2,1,0:T(1,128)}), f32[32,1,192]{2,1,0:T(1,128)S(1)}, u32[]{:S(2)}, u32[]{:S(2)}) async-start(f32[32,1,192]{2,1,0:T(1,128)} %reshape.151), calls=%async_computation.12 | async-start | bytes 65536 | tf_op jit(solution)/shard_map/all_to_all | solution.py:18
  439.1 21.1 %all-to-all-start.9 = ((bf16[4,256,504]{1,2,0:T(8,128)(2,1)}), bf16[4,256,504]{1,2,0:T(8,128)(2,1)S(1)}, u32[]{:S(2)}, u32[]{:S(2)}) async-start(bf16[4,256,504]{1,2,0:T(8,128)(2,1)} %broadcast_in_dim.21), calls=%async_computation.10 | async-start | bytes 2064384 | tf_op jit(solution)/shard_map/all_to_all | solution.py:18
  461.3 13.8 %all-to-all-start.11 = ((bf16[4,256,504]{1,2,0:T(8,128)(2,1)}), bf16[4,256,504]{1,2,0:T(8,128)(2,1)S(1)}, u32[]{:S(2)}, u32[]{:S(2)}) async-start(bf16[4,256,504]{1,2,0:T(8,128)(2,1)} %broadcast_in_dim.22), calls=%async_computation.13 | async-start | bytes 2064384 | tf_op jit(solution)/shard_map/all_to_all | solution.py:18
  472.1 9.2 %copy-start.3 = (bf16[8,128,448]{1,2,0:T(8,128)(2,1)S(1)}, bf16[8,128,448]{1,2,0:T(8,128)(2,1)}, u32[]{:S(2)}) copy-start(bf16[8,128,448]{1,2,0:T(8,128)(2,1)} %copy-done.2) | copy-start | bytes 2752516
Sparse Core Ops, SparseCore 0:
  184.2 37.9 reduce-scatter.8
  285.8 37.6 reduce-scatter.12
  326.7 33.7 reduce-scatter.10
  363.7 44.0 reduce-scatter.14

commit v7 on v5

--- a/solution.py
+++ b/solution.py
@@ -52,8 +52,8 @@
     united = scatter_sum(united, "zlo", sizes["zlo"])
 
     squares = jnp.sum(united * united, axis=1)
-    squares = lax.psum(squares, "y")
-    squares = lax.psum(squares, "zhi")
+    n_seq = sizes["y"] * sizes["zhi"]
+    squares = jnp.sum(spread_gather(squares[None], SEQ, n_seq), axis=0)
     hidden_part = (
         united * lax.rsqrt(squares / D + norm_eps)[:, None] * norm_gain[None, :]
     ).astype(jnp.bfloat16)
@@ -64,8 +64,8 @@
     )
 
     logits = jnp.dot(hidden, head_weight, preferred_element_type=jnp.float32)
-    logits = lax.psum_scatter(logits, "y", scatter_dimension=0, tiled=True)
-    logits = lax.psum_scatter(logits, "zhi", scatter_dimension=0, tiled=True)
+    logits = scatter_sum(logits, "y", sizes["y"])
+    logits = scatter_sum(logits, "zhi", sizes["zhi"])
 
     seq_index = lax.axis_index("y") * sizes["zhi"] + lax.axis_index("zhi")
     positions = seq_index * tok_local + jnp.arange(tok_local, dtype=jnp.int32)

time: 436 us -> 431 us (0.989)
  waiting for transfers between devices: 115 us -> 78.8 us
  blocking collectives: 271 us -> 291 us
  local copies, waits for them, and re-layouts: 6.9 us -> 20.4 us
  between operations: 16.6 us -> 3.24 us
  starting transfers between devices: 6.95 us -> 16.8 us
    reduce_scatter x2 -> x0, waiting for transfers between devices: 108 us -> none  [the longest x1 61.3 us: on_device(): logits = lax.psum_scatter(logits, 'zhi', scatter_dimension=0, tiled=True)]
    all_to_all x1 -> x2, blocking collectives: 16 us -> 66.2 us  [scatter_sum(): pieces = lax.all_to_all(value, axes, 0, 0, tiled=True)]
    all_to_all x0 -> x1, waiting for transfers between devices: none -> 49.8 us  [scatter_sum(): pieces = lax.all_to_all(value, axes, 0, 0, tiled=True)]
    all_to_all x1 -> x2, waiting for transfers between devices: 7.77 us -> 29 us  [spread_gather(): lax.all_to_all(spread.reshape((size * value.shape[0],) + value.shape[1:])...]
    psum x2 -> x0, blocking collectives: 19 us -> none  [the longest x1 12.1 us: on_device(): squares = lax.psum(squares, 'zhi')]
    all_to_all x2, blocking collectives: 71.8 us -> 64.2 us  [spread_gather(): lax.all_to_all(spread.reshape((size * value.shape[0],) + value.shape[1:])...]
    all_to_all x1 -> x2, starting transfers between devices: 6.87 us -> 12.4 us  [spread_gather(): lax.all_to_all(spread.reshape((size * value.shape[0],) + value.shape[1:])...]
    reduce_sum x1 -> x3, other arithmetic: 0.04 us -> 5.05 us  [scatter_sum(): jnp.sum(pieces.reshape((size, value.shape[0] // size) + value.shape[1:]),...]
where the time goes in v7:
time: 431 us; the launch traced here: 428 us
  blocking collectives  291 us (68%)
  waiting for transfers between devices  78.8 us (18%)
  local copies, waits for them, and re-layouts  20.4 us (5%)
  starting transfers between devices  16.8 us (4%)
  other arithmetic  9.58 us (2%)
  matrix products  8.66 us (2%)
    all_to_all x2, blocking collectives, scatter_sum(): pieces = lax.all_to_all(value, axes, 0, 0, tiled=True)  66.2 us
    all_to_all x2, blocking collectives, spread_gather(): lax.all_to_all(spread.reshape((size * value.shape[0],) + value.shape[1:])...  64.2 us
    all_to_all x1, waiting for transfers between devices, scatter_sum(): pieces = lax.all_to_all(value, axes, 0, 0, tiled=True)  49.8 us
    all_gather x1, blocking collectives, on_device(): rows = lax.all_gather(sources[0], 'zhi', axis=0, tiled=True)  45.8 us
    all_gather x1, blocking collectives, on_device(): carried = lax.all_gather(carried, 'zhi', axis=0, tiled=True)  39.1 us
    all_to_all x1, blocking collectives, on_device(): pieces = lax.all_to_all(product, ('segment', 'core'), 0, 0, tiled=True)  32.4 us
    all_to_all x1, blocking collectives, on_device(): lax.all_to_all(spread.reshape(tokens, -1), ('segment', 'core'), 0, 0, til...  31.9 us
    all_to_all x2, waiting for transfers between devices, spread_gather(): lax.all_to_all(spread.reshape((size * value.shape[0],) + value.shape[1:])...  29 us
  transfers between devices with their start and end apart: 3, of which 3 were waited for; matrix products, arithmetic and copies ran while one was open for 0% of the time, Pallas kernels for 0%

profile of v7, /device:TPU:1, one launch (start us, length us, event | category | flops | bytes accessed | tf_op | source)
XLA Modules:
  0.0 428.3 jit_solution(4695788935823462560)
XLA Ops:
  0.6 0.0 copy-start
  0.6 45.8 %all-gather = bf16[1,512,896]{2,1,0:T(8,128)(2,1)S(1)} all-gather(bf16[1,128,896]{2,1,0:T(8,128)(2,1)} %param.8), channel_id=2, replica_groups=mesh['segment'=4,'y'=4,'zhi'=4,'zlo'=4,'core'=2] {'zhi'}, dimensions={1}, use_global_device_ids=true | all-gather | bytes 1146880 | tf_op jit(solution)/shard_map/all_gather | solution.py:42
  46.4 0.3 broadcast_in_dim.10
  46.7 43.4 %all_to_all.71 = bf16[4,512,896]{2,1,0:T(8,128)(2,1)S(1)} all-to-all(bf16[4,512,896]{2,1,0:T(8,128)(2,1)S(1)} %broadcast_in_dim.10), channel_id=1, replica_groups=mesh['segment'=4,'y'=4,'zhi'=4,'zlo'=4,'core'=2] {'y'}, dimensions={0} | all-to-all | bytes 7340032 | tf_op jit(solution)/shard_map/all_to_all | solution.py:18
  90.1 0.0 copy-done
  90.1 2.1 convolution_convert_fusion
  92.2 0.1 copy.64
  92.3 32.4 %all_to_all.72 = bf16[8,256,448]{1,2,0:T(8,128)(2,1)S(1)} all-to-all(bf16[8,256,448]{1,2,0:T(8,128)(2,1)S(1)} %bitcast.73), channel_id=1, replica_groups=mesh['segment'=4,'y'=4,'zhi'=4,'zlo'=4,'core'=2] {'segment','core'}, dimensions={0} | all-to-all | bytes 3670016 | tf_op jit(solution)/shard_map/all_to_all | solution.py:49
  124.8 0.3 convert_reduce_fusion
  125.0 0.2 copy.47
  125.2 16.0 %all_to_all.73 = f32[4,64,448]{2,1,0:T(8,128)S(1)} all-to-all(f32[4,64,448]{2,1,0:T(8,128)S(1)} %bitcast.78), channel_id=1, replica_groups=mesh['segment'=4,'y'=4,'zhi'=4,'zlo'=4,'core'=2] {'zlo'}, dimensions={0} | all-to-all | bytes 917504 | tf_op jit(solution)/shard_map/all_to_all | solution.py:24
  141.2 0.1 multiply_reduce_fusion.1
  141.4 20.8 %all_to_all.74 = f32[16,1,64]{2,1,0:T(1,128)S(1)} all-to-all(f32[16,1,64]{2,1,0:T(1,128)S(1)} %reshape.113), channel_id=1, replica_groups=mesh['segment'=4,'y'=4,'zhi'=4,'zlo'=4,'core'=2] {'y','zhi'}, dimensions={0} | all-to-all | bytes 8192 | tf_op jit(solution)/shard_map/all_to_all | solution.py:18
  162.2 0.0 copy-done.6
  162.2 0.1 multiply_convert_fusion.1
  162.3 11.3 %all_gather.10 = bf16[256,448]{1,0:T(8,128)(2,1)S(1)} all-gather(bf16[64,448]{1,0:T(8,128)(2,1)S(1)} %multiply_convert_fusion.1), channel_id=1, replica_groups=mesh['segment'=4,'y'=4,'zhi'=4,'zlo'=4,'core'=2] {'zlo'}, dimensions={0}, use_global_device_ids=true | all-gather | bytes 286720 | tf_op jit(solution)/shard_map/all_gather | solution.py:60
  173.6 0.1 copy.49
  173.8 0.1 broadcast_in_dim.11
  173.9 31.9 %all_to_all.75 = bf16[8,256,448]{1,2,0:T(8,128)(2,1)S(1)} all-to-all(bf16[8,256,448]{1,2,0:T(8,128)(2,1)S(1)} %broadcast_in_dim.11), channel_id=1, replica_groups=mesh['segment'=4,'y'=4,'zhi'=4,'zlo'=4,'core'=2] {'segment','core'}, dimensions={0} | all-to-all | bytes 3670016 | tf_op jit(solution)/shard_map/all_to_all | solution.py:62
  205.7 2.3 copy.50
  208.0 4.5 %dot_general.12 = bf16[4,512,448]{1,0,2:T(4,128)(2,1)} reshape(bf16[8,256,448]{1,0,2:T(8,128)(2,1)} %copy.50) | data formatting | bytes 3670016 | tf_op jit(solution)/shard_map/dot_general | solution.py:66
  212.6 2.9 fusion.2
  215.5 50.2 %all_to_all.76 = f32[4,512,500]{1,2,0:T(8,128)} all-to-all(f32[4,512,500]{1,2,0:T(8,128)S(1)} %fusion.2), channel_id=1, replica_groups=mesh['segment'=4,'y'=4,'zhi'=4,'zlo'=4,'core'=2] {'y'}, dimensions={0} | all-to-all | bytes 8192000 | tf_op jit(solution)/shard_map/all_to_all | solution.py:24
  265.7 3.7 reduce_sum.122
  269.4 2.6 all_to_all.56
  272.0 2.3 copy.52
  274.3 4.4 %all-to-all-start.6 = ((f32[4,128,500]{1,2,0:T(8,128)}), f32[4,128,500]{1,2,0:T(8,128)}, u32[]{:S(2)}, u32[]{:S(2)}) async-start(f32[4,128,500]{1,2,0:T(8,128)} %copy.52), calls=%async_computation.6 | async-start | bytes 2064384 | tf_op jit(solution)/shard_map/all_to_all | solution.py:24
  278.7 0.2 reduce-window.8
  278.9 0.1 compare_reduce_fusion
  279.0 0.0 copy-done.5
  279.1 49.8 %all-to-all-done.6 = f32[4,128,500]{1,2,0:T(8,128)} async-done(((f32[4,128,500]{1,2,0:T(8,128)}), f32[4,128,500]{1,2,0:T(8,128)}, u32[]{:S(2)}, u32[]{:S(2)}) %all-to-all-start.6) | async-done | bytes 1024032 | tf_op jit(solution)/shard_map/all_to_all | solution.py:24
  328.9 1.3 reduce_sum.123
  330.2 0.1 reduce_max.18
  330.3 0.1 exponential_reduce_fusion
  330.4 0.3 multiply_reduce_fusion
  330.7 0.6 reshape.114
  331.3 7.9 %all-to-all-start.7 = ((f32[32,3,128]{2,1,0:T(4,128)}), f32[32,3,128]{2,1,0:T(4,128)S(1)}, u32[]{:S(2)}, u32[]{:S(2)}) async-start(f32[32,3,128]{2,1,0:T(4,128)} %reshape.114), calls=%async_computation.7 | async-start | bytes 131072 | tf_op jit(solution)/shard_map/all_to_all | solution.py:18
  339.3 7.9 %all-to-all-done.7 = f32[32,3,128]{2,1,0:T(4,128)S(1)} async-done(((f32[32,3,128]{2,1,0:T(4,128)}), f32[32,3,128]{2,1,0:T(4,128)S(1)}, u32[]{:S(2)}, u32[]{:S(2)}) %all-to-all-start.7) | async-done | bytes 49184 | tf_op jit(solution)/shard_map/all_to_all | solution.py:18
  347.3 0.3 multiply_convert_fusion
  347.7 0.1 concatenate.3
  347.7 39.1 %all_gather.11 = bf16[512,504]{0,1:T(8,128)(2,1)S(1)} all-gather(bf16[128,504]{0,1:T(8,128)(2,1)S(1)} %concatenate.3), channel_id=1, replica_groups=mesh['segment'=4,'y'=4,'zhi'=4,'zlo'=4,'core'=2] {'zhi'}, dimensions={0}, use_global_device_ids=true | all-gather | bytes 645120 | tf_op jit(solution)/shard_map/all_gather | solution.py:115
  386.9 1.5 broadcast_in_dim.12
  388.3 4.4 %all-to-all-start.8 = ((bf16[4,512,504]{1,2,0:T(8,128)(2,1)}), bf16[4,512,504]{1,2,0:T(8,128)(2,1)}, u32[]{:S(2)}, u32[]{:S(2)}) async-start(bf16[4,512,504]{1,2,0:T(8,128)(2,1)} %broadcast_in_dim.12), calls=%async_computation.8 | async-start | bytes 4128768 | tf_op jit(solution)/shard_map/all_to_all | solution.py:18
  392.8 1.5 copy.60
  394.3 21.1 %all-to-all-done.8 = bf16[4,512,504]{1,2,0:T(8,128)(2,1)} async-done(((bf16[4,512,504]{1,2,0:T(8,128)(2,1)}), bf16[4,512,504]{1,2,0:T(8,128)(2,1)}, u32[]{:S(2)}, u32[]{:S(2)}) %all-to-all-start.8) | async-done | bytes 2064416 | tf_op jit(solution)/shard_map/all_to_all | solution.py:18
  415.4 4.1 copy.55
  419.5 2.8 convert_reduce_fusion.1
  422.3 3.6 fusion
  (29 shorter events, 0.3 us)
Async XLA Ops:
  0.6 89.5 %copy-start = (bf16[1,896,448]{1,2,0:T(8,128)(2,1)S(1)}, bf16[1,896,448]{1,2,0:T(8,128)(2,1)}, u32[]{:S(2)}) copy-start(bf16[1,896,448]{1,2,0:T(8,128)(2,1)} %param.9) | copy-start | bytes 2408452
  124.8 37.4 %copy-start.6 = (f32[448]{0:T(512)S(1)}, f32[448]{0:T(512)}, u32[]{:S(2)}) copy-start(f32[448]{0:T(512)} %param.10) | copy-start | bytes 5380
  208.0 4.5 %copy-start.2 = (bf16[448,500]{1,0:T(8,128)(2,1)S(1)}, bf16[448,500]{1,0:T(8,128)(2,1)}, u32[]{:S(2)}) copy-start(bf16[448,500]{1,0:T(8,128)(2,1)} %param.11) | copy-start | bytes 1344004
  272.0 6.7 %copy-start.3 = (f32[128,8]{0,1:T(8,128)S(1)}, f32[128,8]{0,1:T(8,128)}, u32[]{:S(2)}) copy-start(f32[128,8]{0,1:T(8,128)} %param.15) | copy-start | bytes 12292
  272.0 6.8 %copy-start.7 = (s32[12]{0:T(128)S(1)}, s32[12]{0:T(128)}, u32[]{:S(2)}) copy-start(s32[12]{0:T(128)} %param.12) | copy-start | bytes 148
  272.0 7.1 %copy-start.5 = (s32[128,8]{0,1:T(8,128)S(1)}, s32[128,8]{0,1:T(8,128)}, u32[]{:S(2)}) copy-start(s32[128,8]{0,1:T(8,128)} %param.14) | copy-start | bytes 12292
  274.3 56.1 %copy-start.4 = (s32[128]{0:T(128)S(1)}, s32[128]{0:T(128)}, u32[]{:S(2)}) copy-start(s32[128]{0:T(128)} %param.13) | copy-start | bytes 1540
  274.3 54.6 %all-to-all-start.6 = ((f32[4,128,500]{1,2,0:T(8,128)}), f32[4,128,500]{1,2,0:T(8,128)}, u32[]{:S(2)}, u32[]{:S(2)}) async-start(f32[4,128,500]{1,2,0:T(8,128)} %copy.52), calls=%async_computation.6 | async-start | bytes 2064384 | tf_op jit(solution)/shard_map/all_to_all | solution.py:24
  331.3 15.8 %all-to-all-start.7 = ((f32[32,3,128]{2,1,0:T(4,128)}), f32[32,3,128]{2,1,0:T(4,128)S(1)}, u32[]{:S(2)}, u32[]{:S(2)}) async-start(f32[32,3,128]{2,1,0:T(4,128)} %reshape.114), calls=%async_computation.7 | async-start | bytes 131072 | tf_op jit(solution)/shard_map/all_to_all | solution.py:18
  388.3 27.0 %all-to-all-start.8 = ((bf16[4,512,504]{1,2,0:T(8,128)(2,1)}), bf16[4,512,504]{1,2,0:T(8,128)(2,1)}, u32[]{:S(2)}, u32[]{:S(2)}) async-start(bf16[4,512,504]{1,2,0:T(8,128)(2,1)} %broadcast_in_dim.12), calls=%async_computation.8 | async-start | bytes 4128768 | tf_op jit(solution)/shard_map/all_to_all | solution.py:18
  394.3 28.0 %copy-start.1 = (bf16[8,56,8,256]{3,2,0,1:T(8,128)(2,1)S(1)}, bf16[8,56,8,256]{3,2,0,1:T(8,128)(2,1)}, u32[]{:S(2)}) copy-start(bf16[8,56,8,256]{3,2,0,1:T(8,128)(2,1)} %copy.60) | copy-start | bytes 5505028

commit v8 on v7

--- a/solution.py
+++ b/solution.py
@@ -39,11 +39,27 @@
     tok_local = sources.shape[1]
     n_sm = sizes["segment"] * sizes["zlo"] * sizes["core"]
 
-    rows = lax.all_gather(sources[0], "zhi", axis=0, tiled=True)
-    rows = spread_gather(rows, "y", sizes["y"])
-    tokens = rows.shape[0]
-    product = jnp.dot(rows, unite_weight[0], preferred_element_type=jnp.float32)
-    product = lax.optimization_barrier(product.astype(jnp.bfloat16))
+    n_zhi, n_y = sizes["zhi"], sizes["y"]
+    own = sources[0]
+    own_y = spread_gather(own, "y", n_y).reshape(n_y, 1, tok_local, -1)
+    zhi_all = lax.all_gather(own, "zhi", axis=0, tiled=True).reshape(n_zhi, tok_local, -1)
+    me = lax.axis_index("zhi")
+    others = lax.dynamic_slice_in_dim(
+        jnp.concatenate([zhi_all, zhi_all], axis=0), me + 1, n_zhi - 1, axis=0
+    )
+    others_y = spread_gather(others.reshape((n_zhi - 1) * tok_local, -1), "y", n_y)
+    rotated = jnp.concatenate(
+        [own_y, others_y.reshape(n_y, n_zhi - 1, tok_local, -1)], axis=1
+    )
+    tokens = n_y * n_zhi * tok_local
+    part = jnp.dot(
+        rotated.reshape(tokens, -1), unite_weight[0], preferred_element_type=jnp.float32
+    ).astype(jnp.bfloat16)
+    part = part.reshape(n_y, n_zhi, tok_local, -1)
+    product = lax.dynamic_slice_in_dim(
+        jnp.concatenate([part, part], axis=1), (n_zhi - me) % n_zhi, n_zhi, axis=1
+    ).reshape(tokens, -1)
+    product = lax.optimization_barrier(product)
 
     n_sc = sizes["segment"] * sizes["core"]
     pieces = lax.all_to_all(product, ("segment", "core"), 0, 0, tiled=True)

time: 431 us -> 441 us (1.023)
  blocking collectives: 291 us -> 242 us
  waiting for transfers between devices: 78.8 us -> 112 us
  local copies, waits for them, and re-layouts: 20.4 us -> 29.8 us
  starting transfers between devices: 16.8 us -> 26.2 us
  other arithmetic: 9.58 us -> 14.4 us
    all_to_all x2 -> x1, blocking collectives: 64.2 us -> 20.7 us  [spread_gather(): lax.all_to_all(spread.reshape((size * value.shape[0],) + value.shape[1:])...]
    all_to_all x2 -> x4, waiting for transfers between devices: 29 us -> 61.9 us  [spread_gather(): lax.all_to_all(spread.reshape((size * value.shape[0],) + value.shape[1:])...]
    all_to_all x2 -> x4, starting transfers between devices: 12.4 us -> 21.8 us  [spread_gather(): lax.all_to_all(spread.reshape((size * value.shape[0],) + value.shape[1:])...]
    reshape x0 -> x2, local copies, waits for them, and re-layouts: none -> 7.21 us  [the longest x1 4.13 us: on_device(): part = part.reshape(n_y, n_zhi, tok_local, -1)]
    concatenate x0 -> x3, other arithmetic: none -> 6.41 us  [the longest x1 4.57 us: on_device(): jnp.concatenate([part, part], axis=1)]
  transfers between devices with their start and end apart: 3 -> 5, of which waited for: 3 -> 4; matrix products, arithmetic and copies ran while one was open for 0% -> 0% of each run, Pallas kernels for 0% -> 0%
where the time goes in v8:
time: 441 us; the launch traced here: 438 us
  blocking collectives  242 us (55%)
  waiting for transfers between devices  112 us (25%)
  local copies, waits for them, and re-layouts  29.8 us (7%)
  starting transfers between devices  26.2 us (6%)
  other arithmetic  14.4 us (3%)
  matrix products  9.83 us (2%)
    all_to_all x2, blocking collectives, scatter_sum(): pieces = lax.all_to_all(value, axes, 0, 0, tiled=True)  66.2 us
    all_to_all x4, waiting for transfers between devices, spread_gather(): lax.all_to_all(spread.reshape((size * value.shape[0],) + value.shape[1:])...  61.9 us
    all_to_all x1, waiting for transfers between devices, scatter_sum(): pieces = lax.all_to_all(value, axes, 0, 0, tiled=True)  49.8 us
    all_gather x1, blocking collectives, on_device(): lax.all_gather(own, 'zhi', axis=0, tiled=True).reshape(n_zhi, tok_local, -1)  44.5 us
    all_gather x1, blocking collectives, on_device(): carried = lax.all_gather(carried, 'zhi', axis=0, tiled=True)  37.8 us
    all_to_all x1, blocking collectives, on_device(): lax.all_to_all(spread.reshape(tokens, -1), ('segment', 'core'), 0, 0, til...  31.9 us
    all_to_all x1, blocking collectives, on_device(): pieces = lax.all_to_all(product, ('segment', 'core'), 0, 0, tiled=True)  30.2 us
    all_to_all x4, starting transfers between devices, spread_gather(): lax.all_to_all(spread.reshape((size * value.shape[0],) + value.shape[1:])...  21.8 us
  transfers between devices with their start and end apart: 5, of which 4 were waited for; matrix products, arithmetic and copies ran while one was open for 0% of the time, Pallas kernels for 0%

profile of v8, /device:TPU:1, one launch (start us, length us, event | category | flops | bytes accessed | tf_op | source)
XLA Modules:
  0.0 437.8 jit_solution(8672819530071927414)
XLA Ops:
  0.7 2.0 broadcast_in_dim.17
  2.7 5.0 %all-to-all-start = ((bf16[4,128,896]{2,1,0:T(8,128)(2,1)}), bf16[4,128,896]{2,1,0:T(8,128)(2,1)S(1)}, u32[]{:S(2)}, u32[]{:S(2)}) async-start(bf16[4,128,896]{2,1,0:T(8,128)(2,1)} %broadcast_in_dim.17), calls=%async_computation | async-start | bytes 1835008 | tf_op jit(solution)/shard_map/all_to_all | solution.py:18
  7.7 44.5 %all-gather = bf16[1,512,896]{2,1,0:T(8,128)(2,1)S(1)} all-gather(bf16[1,128,896]{2,1,0:T(8,128)(2,1)S(1)} %copy-done.2), channel_id=2, replica_groups=mesh['segment'=4,'y'=4,'zhi'=4,'zlo'=4,'core'=2] {'zhi'}, dimensions={1}, use_global_device_ids=true | all-gather | bytes 1146880 | tf_op jit(solution)/shard_map/all_gather | solution.py:45
  52.2 0.3 fusion.6
  52.5 1.9 broadcast_in_dim.19
  54.3 4.3 all-to-all-start.1
  58.6 31.9 %all-to-all-done.1 = bf16[4,384,896]{2,1,0:T(8,128)(2,1)S(1)} async-done(((bf16[4,384,896]{2,1,0:T(8,128)(2,1)}), bf16[4,384,896]{2,1,0:T(8,128)(2,1)S(1)}, u32[]{:S(2)}, u32[]{:S(2)}) %all-to-all-start.1) | async-done | bytes 2752544 | tf_op jit(solution)/shard_map/all_to_all | solution.py:18
  90.5 1.6 pad_maximum_fusion
  92.0 3.4 convolution_convert_fusion
  95.4 4.1 reshape.141
  99.5 4.6 %fusion.2 = bf16[4,4,128,448]{2,1,0,3:T(4,128)(2,1)} fusion(s32[]{:T(128)S(6)} %select_n.20, bf16[4,4,128,448]{2,1,0,3:T(4,128)(2,1)S(1)} %reshape.141), kind=kLoop, calls=%fused_computation.7 | loop fusion | flops 3670016 | bytes 3670020 | tf_op jit(solution)/shard_map/concatenate | solution.py:60
  104.1 3.1 reshape.142
  107.2 0.1 copy.69
  107.3 30.2 %all_to_all.74 = bf16[8,256,448]{1,2,0:T(8,128)(2,1)S(1)} all-to-all(bf16[8,256,448]{1,2,0:T(8,128)(2,1)S(1)} %bitcast.85), channel_id=1, replica_groups=mesh['segment'=4,'y'=4,'zhi'=4,'zlo'=4,'core'=2] {'segment','core'}, dimensions={0} | all-to-all | bytes 3670016 | tf_op jit(solution)/shard_map/all_to_all | solution.py:65
  137.5 0.3 convert_reduce_fusion
  137.7 0.2 copy.52
  137.9 15.9 %all_to_all.75 = f32[4,64,448]{2,1,0:T(8,128)S(1)} all-to-all(f32[4,64,448]{2,1,0:T(8,128)S(1)} %bitcast.92), channel_id=1, replica_groups=mesh['segment'=4,'y'=4,'zhi'=4,'zlo'=4,'core'=2] {'zlo'}, dimensions={0} | all-to-all | bytes 917504 | tf_op jit(solution)/shard_map/all_to_all | solution.py:24
  153.9 0.1 multiply_reduce_fusion.1
  154.0 20.7 %all_to_all.76 = f32[16,1,64]{2,1,0:T(1,128)S(1)} all-to-all(f32[16,1,64]{2,1,0:T(1,128)S(1)} %reshape.143), channel_id=1, replica_groups=mesh['segment'=4,'y'=4,'zhi'=4,'zlo'=4,'core'=2] {'y','zhi'}, dimensions={0} | all-to-all | bytes 8192 | tf_op jit(solution)/shard_map/all_to_all | solution.py:18
  174.9 11.3 %all_gather.10 = bf16[256,448]{1,0:T(8,128)(2,1)S(1)} all-gather(bf16[64,448]{1,0:T(8,128)(2,1)S(1)} %multiply_convert_fusion.1), channel_id=1, replica_groups=mesh['segment'=4,'y'=4,'zhi'=4,'zlo'=4,'core'=2] {'zlo'}, dimensions={0}, use_global_device_ids=true | all-gather | bytes 286720 | tf_op jit(solution)/shard_map/all_gather | solution.py:76
  186.2 0.1 copy.54
  186.3 0.1 broadcast_in_dim.20
  186.5 31.9 %all_to_all.77 = bf16[8,256,448]{1,2,0:T(8,128)(2,1)S(1)} all-to-all(bf16[8,256,448]{1,2,0:T(8,128)(2,1)S(1)} %broadcast_in_dim.20), channel_id=1, replica_groups=mesh['segment'=4,'y'=4,'zhi'=4,'zlo'=4,'core'=2] {'segment','core'}, dimensions={0} | all-to-all | bytes 3670016 | tf_op jit(solution)/shard_map/all_to_all | solution.py:78
  218.3 2.3 copy.55
  220.6 4.5 %dot_general.12 = bf16[4,512,448]{1,0,2:T(4,128)(2,1)} reshape(bf16[8,256,448]{1,0,2:T(8,128)(2,1)} %copy.55) | data formatting | bytes 3670016 | tf_op jit(solution)/shard_map/dot_general | solution.py:82
  225.1 2.9 fusion.3
  228.1 50.2 %all_to_all.78 = f32[4,512,500]{1,2,0:T(8,128)} all-to-all(f32[4,512,500]{1,2,0:T(8,128)S(1)} %fusion.3), channel_id=1, replica_groups=mesh['segment'=4,'y'=4,'zhi'=4,'zlo'=4,'core'=2] {'y'}, dimensions={0} | all-to-all | bytes 8192000 | tf_op jit(solution)/shard_map/all_to_all | solution.py:24
  278.3 3.7 reduce_sum.122
  282.0 2.6 all_to_all.58
  284.6 2.3 copy.57
  286.9 4.4 %all-to-all-start.7 = ((f32[4,128,500]{1,2,0:T(8,128)}), f32[4,128,500]{1,2,0:T(8,128)}, u32[]{:S(2)}, u32[]{:S(2)}) async-start(f32[4,128,500]{1,2,0:T(8,128)} %copy.57), calls=%async_computation.7 | async-start | bytes 2064384 | tf_op jit(solution)/shard_map/all_to_all | solution.py:24
  291.3 0.2 reduce-window.8
  291.7 49.8 %all-to-all-done.7 = f32[4,128,500]{1,2,0:T(8,128)} async-done(((f32[4,128,500]{1,2,0:T(8,128)}), f32[4,128,500]{1,2,0:T(8,128)}, u32[]{:S(2)}, u32[]{:S(2)}) %all-to-all-start.7) | async-done | bytes 1024032 | tf_op jit(solution)/shard_map/all_to_all | solution.py:24
  341.4 1.3 reduce_sum.123
  342.8 0.1 exponential_reduce_fusion
  342.9 0.3 multiply_reduce_fusion
  343.2 0.6 reshape.144
  343.9 8.1 %all-to-all-start.8 = ((f32[32,3,128]{2,1,0:T(4,128)}), f32[32,3,128]{2,1,0:T(4,128)S(1)}, u32[]{:S(2)}, u32[]{:S(2)}) async-start(f32[32,3,128]{2,1,0:T(4,128)} %reshape.144), calls=%async_computation.8 | async-start | bytes 131072 | tf_op jit(solution)/shard_map/all_to_all | solution.py:18
  352.0 7.8 %all-to-all-done.8 = f32[32,3,128]{2,1,0:T(4,128)S(1)} async-done(((f32[32,3,128]{2,1,0:T(4,128)}), f32[32,3,128]{2,1,0:T(4,128)S(1)}, u32[]{:S(2)}, u32[]{:S(2)}) %all-to-all-start.8) | async-done | bytes 49184 | tf_op jit(solution)/shard_map/all_to_all | solution.py:18
  359.9 0.3 multiply_convert_fusion
  360.3 37.8 %all_gather.11 = bf16[512,504]{0,1:T(8,128)(2,1)S(1)} all-gather(bf16[128,504]{0,1:T(8,128)(2,1)S(1)} %concatenate.15), channel_id=1, replica_groups=mesh['segment'=4,'y'=4,'zhi'=4,'zlo'=4,'core'=2] {'zhi'}, dimensions={0}, use_global_device_ids=true | all-gather | bytes 645120 | tf_op jit(solution)/shard_map/all_gather | solution.py:131
  398.1 1.4 broadcast_in_dim.21
  399.5 4.4 %all-to-all-start.9 = ((bf16[4,512,504]{1,2,0:T(8,128)(2,1)}), bf16[4,512,504]{1,2,0:T(8,128)(2,1)}, u32[]{:S(2)}, u32[]{:S(2)}) async-start(bf16[4,512,504]{1,2,0:T(8,128)(2,1)} %broadcast_in_dim.21), calls=%async_computation.9 | async-start | bytes 4128768 | tf_op jit(solution)/shard_map/all_to_all | solution.py:18
  404.0 1.5 copy.65
  405.5 22.3 %all-to-all-done.9 = bf16[4,512,504]{1,2,0:T(8,128)(2,1)} async-done(((bf16[4,512,504]{1,2,0:T(8,128)(2,1)}), bf16[4,512,504]{1,2,0:T(8,128)(2,1)}, u32[]{:S(2)}, u32[]{:S(2)}) %all-to-all-start.9) | async-done | bytes 2064416 | tf_op jit(solution)/shard_map/all_to_all | solution.py:18
  427.7 2.8 copy.60
  430.5 1.2 convert_reduce_fusion.1
  431.8 3.5 fusion
  (40 shorter events, 0.6 us)
Async XLA Ops:
  0.6 91.4 %copy-start = (bf16[1,896,448]{1,2,0:T(8,128)(2,1)S(1)}, bf16[1,896,448]{1,2,0:T(8,128)(2,1)}, u32[]{:S(2)}) copy-start(bf16[1,896,448]{1,2,0:T(8,128)(2,1)} %param.9) | copy-start | bytes 2408452
  0.6 7.1 %copy-start.2 = (bf16[1,128,896]{2,1,0:T(8,128)(2,1)S(1)}, bf16[1,128,896]{2,1,0:T(8,128)(2,1)}, u32[]{:S(2)}) copy-start(bf16[1,128,896]{2,1,0:T(8,128)(2,1)} %param.8) | copy-start | bytes 688132
  2.7 49.8 %all-to-all-start = ((bf16[4,128,896]{2,1,0:T(8,128)(2,1)}), bf16[4,128,896]{2,1,0:T(8,128)(2,1)S(1)}, u32[]{:S(2)}, u32[]{:S(2)}) async-start(bf16[4,128,896]{2,1,0:T(8,128)(2,1)} %broadcast_in_dim.17), calls=%async_computation | async-start | bytes 1835008 | tf_op jit(solution)/shard_map/all_to_all | solution.py:18
  52.5 1.9 copy-start.1
  54.3 36.1 %all-to-all-start.1 = ((bf16[4,384,896]{2,1,0:T(8,128)(2,1)}), bf16[4,384,896]{2,1,0:T(8,128)(2,1)S(1)}, u32[]{:S(2)}, u32[]{:S(2)}) async-start(bf16[4,384,896]{2,1,0:T(8,128)(2,1)} %broadcast_in_dim.19), calls=%async_computation.1 | async-start | bytes 5505024 | tf_op jit(solution)/shard_map/all_to_all | solution.py:18
  137.5 37.3 %copy-start.7 = (f32[448]{0:T(512)S(1)}, f32[448]{0:T(512)}, u32[]{:S(2)}) copy-start(f32[448]{0:T(512)} %param.10) | copy-start | bytes 5380
  220.6 4.5 %copy-start.3 = (bf16[448,500]{1,0:T(8,128)(2,1)S(1)}, bf16[448,500]{1,0:T(8,128)(2,1)}, u32[]{:S(2)}) copy-start(bf16[448,500]{1,0:T(8,128)(2,1)} %param.11) | copy-start | bytes 1344004
  284.5 6.7 %copy-start.8 = (s32[12]{0:T(128)S(1)}, s32[12]{0:T(128)}, u32[]{:S(2)}) copy-start(s32[12]{0:T(128)} %param.12) | copy-start | bytes 148
  284.5 6.9 %copy-start.4 = (f32[128,8]{0,1:T(8,128)S(1)}, f32[128,8]{0,1:T(8,128)}, u32[]{:S(2)}) copy-start(f32[128,8]{0,1:T(8,128)} %param.15) | copy-start | bytes 12292
  284.5 7.1 %copy-start.6 = (s32[128,8]{0,1:T(8,128)S(1)}, s32[128,8]{0,1:T(8,128)}, u32[]{:S(2)}) copy-start(s32[128,8]{0,1:T(8,128)} %param.14) | copy-start | bytes 12292
  286.9 56.0 %copy-start.5 = (s32[128]{0:T(128)S(1)}, s32[128]{0:T(128)}, u32[]{:S(2)}) copy-start(s32[128]{0:T(128)} %param.13) | copy-start | bytes 1540
  286.9 54.5 %all-to-all-start.7 = ((f32[4,128,500]{1,2,0:T(8,128)}), f32[4,128,500]{1,2,0:T(8,128)}, u32[]{:S(2)}, u32[]{:S(2)}) async-start(f32[4,128,500]{1,2,0:T(8,128)} %copy.57), calls=%async_computation.7 | async-start | bytes 2064384 | tf_op jit(solution)/shard_map/all_to_all | solution.py:24
  343.9 15.9 %all-to-all-start.8 = ((f32[32,3,128]{2,1,0:T(4,128)}), f32[32,3,128]{2,1,0:T(4,128)S(1)}, u32[]{:S(2)}, u32[]{:S(2)}) async-start(f32[32,3,128]{2,1,0:T(4,128)} %reshape.144), calls=%async_computation.8 | async-start | bytes 131072 | tf_op jit(solution)/shard_map/all_to_all | solution.py:18
  399.5 28.2 %all-to-all-start.9 = ((bf16[4,512,504]{1,2,0:T(8,128)(2,1)}), bf16[4,512,504]{1,2,0:T(8,128)(2,1)}, u32[]{:S(2)}, u32[]{:S(2)}) async-start(bf16[4,512,504]{1,2,0:T(8,128)(2,1)} %broadcast_in_dim.21), calls=%async_computation.9 | async-start | bytes 4128768 | tf_op jit(solution)/shard_map/all_to_all | solution.py:18

commit v9 on v7

--- a/solution.py
+++ b/solution.py
@@ -59,11 +59,12 @@
     ).astype(jnp.bfloat16)
     hidden_chunk = lax.all_gather(hidden_part, "zlo", axis=0, tiled=True)
     spread = jnp.broadcast_to(hidden_chunk[None], (n_sc,) + hidden_chunk.shape)
-    hidden = lax.all_to_all(
-        spread.reshape(tokens, -1), ("segment", "core"), 0, 0, tiled=True
-    )
+    hidden3 = lax.all_to_all(spread, ("segment", "core"), 0, 0, tiled=False)
+    hidden = hidden3.reshape(tokens, -1)
 
-    logits = jnp.dot(hidden, head_weight, preferred_element_type=jnp.float32)
+    logits = jnp.einsum(
+        "cti,iv->ctv", hidden3, head_weight, preferred_element_type=jnp.float32
+    ).reshape(tokens, -1)
     logits = scatter_sum(logits, "y", sizes["y"])
     logits = scatter_sum(logits, "zhi", sizes["zhi"])
 

time: 431 us -> 433 us (level)
    dot_general x1 -> x0, local copies, waits for them, and re-layouts: 4.52 us -> none  [on_device(): logits = jnp.dot(hidden, head_weight, preferred_element_type=jnp.float32)]
where the time goes in v9:
time: 433 us; the launch traced here: 430 us
  blocking collectives  293 us (68%)
  waiting for transfers between devices  78.8 us (18%)
  local copies, waits for them, and re-layouts  19.1 us (4%)
  starting transfers between devices  16.7 us (4%)
  other arithmetic  9.58 us (2%)
  matrix products  8.95 us (2%)
    all_to_all x2, blocking collectives, scatter_sum(): pieces = lax.all_to_all(value, axes, 0, 0, tiled=True)  68.4 us
    all_to_all x2, blocking collectives, spread_gather(): lax.all_to_all(spread.reshape((size * value.shape[0],) + value.shape[1:])...  64.2 us
    all_to_all x1, waiting for transfers between devices, scatter_sum(): pieces = lax.all_to_all(value, axes, 0, 0, tiled=True)  49.8 us
    all_gather x1, blocking collectives, on_device(): rows = lax.all_gather(sources[0], 'zhi', axis=0, tiled=True)  45.8 us
    all_gather x1, blocking collectives, on_device(): carried = lax.all_gather(carried, 'zhi', axis=0, tiled=True)  39.1 us
    all_to_all x1, blocking collectives, on_device(): pieces = lax.all_to_all(product, ('segment', 'core'), 0, 0, tiled=True)  32.4 us
    all_to_all x1, blocking collectives, on_device(): hidden3 = lax.all_to_all(spread, ('segment', 'core'), 0, 0, tiled=False)  32 us
    all_to_all x2, waiting for transfers between devices, spread_gather(): lax.all_to_all(spread.reshape((size * value.shape[0],) + value.shape[1:])...  29 us
  transfers between devices with their start and end apart: 3, of which 3 were waited for; matrix products, arithmetic and copies ran while one was open for 0% of the time, Pallas kernels for 0%

profile of v9, /device:TPU:1, one launch (start us, length us, event | category | flops | bytes accessed | tf_op | source)
XLA Modules:
  0.0 429.7 jit_solution(597771692819570052)
XLA Ops:
  0.6 0.0 copy-start
  0.6 45.8 %all-gather = bf16[1,512,896]{2,1,0:T(8,128)(2,1)S(1)} all-gather(bf16[1,128,896]{2,1,0:T(8,128)(2,1)} %param.8), channel_id=2, replica_groups=mesh['segment'=4,'y'=4,'zhi'=4,'zlo'=4,'core'=2] {'zhi'}, dimensions={1}, use_global_device_ids=true | all-gather | bytes 1146880 | tf_op jit(solution)/shard_map/all_gather | solution.py:42
  46.4 0.3 broadcast_in_dim.10
  46.7 43.4 %all_to_all.70 = bf16[4,512,896]{2,1,0:T(8,128)(2,1)S(1)} all-to-all(bf16[4,512,896]{2,1,0:T(8,128)(2,1)S(1)} %broadcast_in_dim.10), channel_id=1, replica_groups=mesh['segment'=4,'y'=4,'zhi'=4,'zlo'=4,'core'=2] {'y'}, dimensions={0} | all-to-all | bytes 7340032 | tf_op jit(solution)/shard_map/all_to_all | solution.py:18
  90.1 2.1 convolution_convert_fusion
  92.2 0.1 copy.77
  92.3 32.4 %all_to_all.71 = bf16[8,256,448]{1,2,0:T(8,128)(2,1)S(1)} all-to-all(bf16[8,256,448]{1,2,0:T(8,128)(2,1)S(1)} %bitcast.73), channel_id=1, replica_groups=mesh['segment'=4,'y'=4,'zhi'=4,'zlo'=4,'core'=2] {'segment','core'}, dimensions={0} | all-to-all | bytes 3670016 | tf_op jit(solution)/shard_map/all_to_all | solution.py:49
  124.8 0.3 convert_reduce_fusion
  125.0 0.2 copy.60
  125.2 16.0 %all_to_all.72 = f32[4,64,448]{2,1,0:T(8,128)S(1)} all-to-all(f32[4,64,448]{2,1,0:T(8,128)S(1)} %bitcast.79), channel_id=1, replica_groups=mesh['segment'=4,'y'=4,'zhi'=4,'zlo'=4,'core'=2] {'zlo'}, dimensions={0} | all-to-all | bytes 917504 | tf_op jit(solution)/shard_map/all_to_all | solution.py:24
  141.2 0.1 multiply_reduce_fusion.1
  141.4 20.8 %all_to_all.73 = f32[16,1,64]{2,1,0:T(1,128)S(1)} all-to-all(f32[16,1,64]{2,1,0:T(1,128)S(1)} %reshape.112), channel_id=1, replica_groups=mesh['segment'=4,'y'=4,'zhi'=4,'zlo'=4,'core'=2] {'y','zhi'}, dimensions={0} | all-to-all | bytes 8192 | tf_op jit(solution)/shard_map/all_to_all | solution.py:18
  162.2 0.1 multiply_convert_fusion.1
  162.3 11.3 %all_gather.10 = bf16[256,448]{1,0:T(8,128)(2,1)S(1)} all-gather(bf16[64,448]{1,0:T(8,128)(2,1)S(1)} %multiply_convert_fusion.1), channel_id=1, replica_groups=mesh['segment'=4,'y'=4,'zhi'=4,'zlo'=4,'core'=2] {'zlo'}, dimensions={0}, use_global_device_ids=true | all-gather | bytes 286720 | tf_op jit(solution)/shard_map/all_gather | solution.py:60
  173.6 0.1 copy.62
  173.8 0.1 broadcast_in_dim.11
  173.9 0.0 copy-start.2
  173.9 32.0 %all_to_all.74 = bf16[8,256,448]{1,2,0:T(8,128)(2,1)S(1)} all-to-all(bf16[8,256,448]{1,2,0:T(8,128)(2,1)S(1)} %broadcast_in_dim.11), channel_id=1, replica_groups=mesh['segment'=4,'y'=4,'zhi'=4,'zlo'=4,'core'=2] {'segment','core'}, dimensions={0} | all-to-all | bytes 3670016 | tf_op jit(solution)/shard_map/all_to_all | solution.py:62
  205.9 3.2 fusion.3
  209.1 5.2 %copy.64 = f32[4,512,500]{1,2,0:T(8,128)} copy(f32[4,512,500]{2,1,0:T(8,128)} %bitcast.71) | data formatting | bytes 8192000 | tf_op jit(solution)/shard_map/all_to_all | solution.py:24
  214.3 52.5 %all_to_all.75 = f32[4,512,500]{1,2,0:T(8,128)} all-to-all(f32[4,512,500]{1,2,0:T(8,128)} %copy.64), channel_id=1, replica_groups=mesh['segment'=4,'y'=4,'zhi'=4,'zlo'=4,'core'=2] {'y'}, dimensions={0} | all-to-all | bytes 8192000 | tf_op jit(solution)/shard_map/all_to_all | solution.py:24
  266.8 3.7 reduce_sum.122
  270.5 2.5 copy.65
  273.0 2.6 copy.66
  275.7 4.4 %all-to-all-start.6 = ((f32[4,128,500]{1,2,0:T(8,128)}), f32[4,128,500]{1,2,0:T(8,128)}, u32[]{:S(2)}, u32[]{:S(2)}) async-start(f32[4,128,500]{1,2,0:T(8,128)} %copy.66), calls=%async_computation.6 | async-start | bytes 2064384 | tf_op jit(solution)/shard_map/all_to_all | solution.py:24
  280.1 0.0 copy-done.3
  280.1 0.0 copy-done.7
  280.1 0.2 reduce-window.8
  280.3 0.1 compare_reduce_fusion
  280.4 49.8 %all-to-all-done.6 = f32[4,128,500]{1,2,0:T(8,128)} async-done(((f32[4,128,500]{1,2,0:T(8,128)}), f32[4,128,500]{1,2,0:T(8,128)}, u32[]{:S(2)}, u32[]{:S(2)}) %all-to-all-start.6) | async-done | bytes 1024032 | tf_op jit(solution)/shard_map/all_to_all | solution.py:24
  330.2 1.3 reduce_sum.123
  331.5 0.1 reduce_max.18
  331.6 0.1 exponential_reduce_fusion
  331.7 0.0 copy-done.4
  331.7 0.3 multiply_reduce_fusion
  332.0 0.6 reshape.113
  332.7 7.9 %all-to-all-start.7 = ((f32[32,3,128]{2,1,0:T(4,128)}), f32[32,3,128]{2,1,0:T(4,128)S(1)}, u32[]{:S(2)}, u32[]{:S(2)}) async-start(f32[32,3,128]{2,1,0:T(4,128)} %reshape.113), calls=%async_computation.7 | async-start | bytes 131072 | tf_op jit(solution)/shard_map/all_to_all | solution.py:18
  340.6 7.9 %all-to-all-done.7 = f32[32,3,128]{2,1,0:T(4,128)S(1)} async-done(((f32[32,3,128]{2,1,0:T(4,128)}), f32[32,3,128]{2,1,0:T(4,128)S(1)}, u32[]{:S(2)}, u32[]{:S(2)}) %all-to-all-start.7) | async-done | bytes 49184 | tf_op jit(solution)/shard_map/all_to_all | solution.py:18
  348.7 0.3 multiply_convert_fusion
  349.0 0.1 concatenate.3
  349.1 39.1 %all_gather.11 = bf16[512,504]{0,1:T(8,128)(2,1)S(1)} all-gather(bf16[128,504]{0,1:T(8,128)(2,1)S(1)} %concatenate.3), channel_id=1, replica_groups=mesh['segment'=4,'y'=4,'zhi'=4,'zlo'=4,'core'=2] {'zhi'}, dimensions={0}, use_global_device_ids=true | all-gather | bytes 645120 | tf_op jit(solution)/shard_map/all_gather | solution.py:116
  388.2 1.5 broadcast_in_dim.12
  389.7 4.4 %all-to-all-start.8 = ((bf16[4,512,504]{1,2,0:T(8,128)(2,1)}), bf16[4,512,504]{1,2,0:T(8,128)(2,1)}, u32[]{:S(2)}, u32[]{:S(2)}) async-start(bf16[4,512,504]{1,2,0:T(8,128)(2,1)} %broadcast_in_dim.12), calls=%async_computation.8 | async-start | bytes 4128768 | tf_op jit(solution)/shard_map/all_to_all | solution.py:18
  394.1 1.5 copy.75
  395.6 21.1 %all-to-all-done.8 = bf16[4,512,504]{1,2,0:T(8,128)(2,1)} async-done(((bf16[4,512,504]{1,2,0:T(8,128)(2,1)}), bf16[4,512,504]{1,2,0:T(8,128)(2,1)}, u32[]{:S(2)}, u32[]{:S(2)}) %all-to-all-start.8) | async-done | bytes 2064416 | tf_op jit(solution)/shard_map/all_to_all | solution.py:18
  416.7 4.1 copy.69
  420.8 2.8 convert_reduce_fusion.1
  423.7 3.6 fusion
  (28 shorter events, 0.3 us)
Async XLA Ops:
  0.6 89.5 %copy-start = (bf16[1,896,448]{1,2,0:T(8,128)(2,1)S(1)}, bf16[1,896,448]{1,2,0:T(8,128)(2,1)}, u32[]{:S(2)}) copy-start(bf16[1,896,448]{1,2,0:T(8,128)(2,1)} %param.9) | copy-start | bytes 2408452
  124.8 37.4 %copy-start.6 = (f32[448]{0:T(512)S(1)}, f32[448]{0:T(512)}, u32[]{:S(2)}) copy-start(f32[448]{0:T(512)} %param.10) | copy-start | bytes 5380
  173.9 32.0 %copy-start.2 = (bf16[448,500]{1,0:T(8,128)(2,1)S(1)}, bf16[448,500]{1,0:T(8,128)(2,1)}, u32[]{:S(2)}) copy-start(bf16[448,500]{1,0:T(8,128)(2,1)} %param.11) | copy-start | bytes 1344004
  273.0 7.0 %copy-start.3 = (f32[128,8]{0,1:T(8,128)S(1)}, f32[128,8]{0,1:T(8,128)}, u32[]{:S(2)}) copy-start(f32[128,8]{0,1:T(8,128)} %param.15) | copy-start | bytes 12292
  273.0 7.1 %copy-start.7 = (s32[12]{0:T(128)S(1)}, s32[12]{0:T(128)}, u32[]{:S(2)}) copy-start(s32[12]{0:T(128)} %param.12) | copy-start | bytes 148
  273.0 7.4 %copy-start.5 = (s32[128,8]{0,1:T(8,128)S(1)}, s32[128,8]{0,1:T(8,128)}, u32[]{:S(2)}) copy-start(s32[128,8]{0,1:T(8,128)} %param.14) | copy-start | bytes 12292
  275.7 56.0 %copy-start.4 = (s32[128]{0:T(128)S(1)}, s32[128]{0:T(128)}, u32[]{:S(2)}) copy-start(s32[128]{0:T(128)} %param.13) | copy-start | bytes 1540
  275.7 54.6 %all-to-all-start.6 = ((f32[4,128,500]{1,2,0:T(8,128)}), f32[4,128,500]{1,2,0:T(8,128)}, u32[]{:S(2)}, u32[]{:S(2)}) async-start(f32[4,128,500]{1,2,0:T(8,128)} %copy.66), calls=%async_computation.6 | async-start | bytes 2064384 | tf_op jit(solution)/shard_map/all_to_all | solution.py:24
  332.7 15.8 %all-to-all-start.7 = ((f32[32,3,128]{2,1,0:T(4,128)}), f32[32,3,128]{2,1,0:T(4,128)S(1)}, u32[]{:S(2)}, u32[]{:S(2)}) async-start(f32[32,3,128]{2,1,0:T(4,128)} %reshape.113), calls=%async_computation.7 | async-start | bytes 131072 | tf_op jit(solution)/shard_map/all_to_all | solution.py:18
  389.7 27.0 %all-to-all-start.8 = ((bf16[4,512,504]{1,2,0:T(8,128)(2,1)}), bf16[4,512,504]{1,2,0:T(8,128)(2,1)}, u32[]{:S(2)}, u32[]{:S(2)}) async-start(bf16[4,512,504]{1,2,0:T(8,128)(2,1)} %broadcast_in_dim.12), calls=%async_computation.8 | async-start | bytes 4128768 | tf_op jit(solution)/shard_map/all_to_all | solution.py:18
  395.6 28.0 %copy-start.1 = (bf16[8,56,8,256]{3,2,0,1:T(8,128)(2,1)S(1)}, bf16[8,56,8,256]{3,2,0,1:T(8,128)(2,1)}, u32[]{:S(2)}) copy-start(bf16[8,56,8,256]{3,2,0,1:T(8,128)(2,1)} %copy.75) | copy-start | bytes 5505028

commit v10 on v7

--- a/solution.py
+++ b/solution.py
@@ -112,19 +112,39 @@
         axis=1,
     )
     carried = jnp.concatenate([logit_grad, extra], axis=1)
-    carried = lax.all_gather(carried, "zhi", axis=0, tiled=True)
-    carried = spread_gather(carried, "y", sizes["y"])
+    n_y, n_zhi = sizes["y"], sizes["zhi"]
+    me = lax.axis_index("zhi")
+    own_y = spread_gather(carried, "y", n_y).reshape(n_y, 1, tok_local, -1)
+    zhi_all = lax.all_gather(carried, "zhi", axis=0, tiled=True).reshape(n_zhi, tok_local, -1)
+    others = lax.dynamic_slice_in_dim(
+        jnp.concatenate([zhi_all, zhi_all], axis=0), me + 1, n_zhi - 1, axis=0
+    )
+    others_y = spread_gather(others.reshape((n_zhi - 1) * tok_local, -1), "y", n_y)
+    others_y = others_y.reshape(n_y, n_zhi - 1, tok_local, -1)
 
-    loss_sum = jnp.sum(
-        carried[:, vocab_width].astype(jnp.float32)
-        + carried[:, vocab_width + 1].astype(jnp.float32)
+    rotated_extra = jnp.concatenate(
+        [own_y[..., vocab_width:], others_y[..., vocab_width:]], axis=1
     )
-    count = jnp.sum(carried[:, vocab_width + 2].astype(jnp.float32))
+    extra_all = lax.dynamic_slice_in_dim(
+        jnp.concatenate([rotated_extra, rotated_extra], axis=1), (n_zhi - me) % n_zhi, n_zhi, axis=1
+    ).reshape(-1, extra.shape[1]).astype(jnp.float32)
+    loss_sum = jnp.sum(extra_all[:, 0] + extra_all[:, 1])
+    count = jnp.sum(extra_all[:, 2])
     mean_loss = loss_sum / jnp.maximum(count, 1.0)
 
+    hidden4 = hidden.reshape(n_y, n_zhi, tok_local, -1)
+    hidden_own = lax.dynamic_slice_in_dim(hidden4, me, 1, axis=1)
+    hidden_others = lax.dynamic_slice_in_dim(
+        jnp.concatenate([hidden4, hidden4], axis=1), me + 1, n_zhi - 1, axis=1
+    )
     head_grad = lax.dot_general(
-        hidden,
-        carried[:, :vocab_width],
+        hidden_own.reshape(-1, hidden.shape[1]),
+        own_y[..., :vocab_width].reshape(-1, vocab_width),
+        (((0,), (0,)), ((), ())),
+        preferred_element_type=jnp.float32,
+    ) + lax.dot_general(
+        hidden_others.reshape(-1, hidden.shape[1]),
+        others_y[..., :vocab_width].reshape(-1, vocab_width),
         (((0,), (0,)), ((), ())),
         preferred_element_type=jnp.float32,
     )

time: 431 us -> 425 us (0.986)
  waiting for transfers between devices: 78.8 us -> 68.1 us
  starting transfers between devices: 16.8 us -> 21.3 us
    all_to_all x2 -> x3, waiting for transfers between devices: 29 us -> 18.3 us  [spread_gather(): lax.all_to_all(spread.reshape((size * value.shape[0],) + value.shape[1:])...]
    reshape x0 -> x2, local copies, waits for them, and re-layouts: none -> 4.82 us  [on_device(): hidden4 = hidden.reshape(n_y, n_zhi, tok_local, -1)]
    all_to_all x2 -> x3, starting transfers between devices: 12.4 us -> 16.9 us  [spread_gather(): lax.all_to_all(spread.reshape((size * value.shape[0],) + value.shape[1:])...]
  transfers between devices with their start and end apart: 3 -> 4, of which waited for: 3 -> 3; matrix products, arithmetic and copies ran while one was open for 0% -> 3% of each run, Pallas kernels for 0% -> 0%
where the time goes in v10:
time: 425 us; the launch traced here: 424 us
  blocking collectives  291 us (68%)
  waiting for transfers between devices  68.1 us (16%)
  local copies, waits for them, and re-layouts  22 us (5%)
  starting transfers between devices  21.3 us (5%)
  matrix products  10.9 us (3%)
  other arithmetic  7.66 us (2%)
    all_to_all x2, blocking collectives, scatter_sum(): pieces = lax.all_to_all(value, axes, 0, 0, tiled=True)  66.2 us
    all_to_all x2, blocking collectives, spread_gather(): lax.all_to_all(spread.reshape((size * value.shape[0],) + value.shape[1:])...  64.2 us
    all_to_all x1, waiting for transfers between devices, scatter_sum(): pieces = lax.all_to_all(value, axes, 0, 0, tiled=True)  49.8 us
    all_gather x1, blocking collectives, on_device(): rows = lax.all_gather(sources[0], 'zhi', axis=0, tiled=True)  45.8 us
    all_gather x1, blocking collectives, on_device(): lax.all_gather(carried, 'zhi', axis=0, tiled=True)  39.4 us
    all_to_all x1, blocking collectives, on_device(): pieces = lax.all_to_all(product, ('segment', 'core'), 0, 0, tiled=True)  32.4 us
    all_to_all x1, blocking collectives, on_device(): lax.all_to_all(spread.reshape(tokens, -1), ('segment', 'core'), 0, 0, til...  31.9 us
    all_to_all x3, waiting for transfers between devices, spread_gather(): lax.all_to_all(spread.reshape((size * value.shape[0],) + value.shape[1:])...  18.3 us
  transfers between devices with their start and end apart: 4, of which 3 were waited for; matrix products, arithmetic and copies ran while one was open for 3% of the time, Pallas kernels for 0%

profile of v10, /device:TPU:1, one launch (start us, length us, event | category | flops | bytes accessed | tf_op | source)
XLA Modules:
  0.0 424.4 jit_solution(9677354110452273488)
XLA Ops:
  0.6 45.8 %all-gather = bf16[1,512,896]{2,1,0:T(8,128)(2,1)S(1)} all-gather(bf16[1,128,896]{2,1,0:T(8,128)(2,1)} %param.8), channel_id=2, replica_groups=mesh['segment'=4,'y'=4,'zhi'=4,'zlo'=4,'core'=2] {'zhi'}, dimensions={1}, use_global_device_ids=true | all-gather | bytes 1146880 | tf_op jit(solution)/shard_map/all_gather | solution.py:42
  46.4 0.3 broadcast_in_dim.14
  46.7 43.4 %all_to_all.71 = bf16[4,512,896]{2,1,0:T(8,128)(2,1)S(1)} all-to-all(bf16[4,512,896]{2,1,0:T(8,128)(2,1)S(1)} %broadcast_in_dim.14), channel_id=1, replica_groups=mesh['segment'=4,'y'=4,'zhi'=4,'zlo'=4,'core'=2] {'y'}, dimensions={0} | all-to-all | bytes 7340032 | tf_op jit(solution)/shard_map/all_to_all | solution.py:18
  90.1 2.1 convolution_convert_fusion
  92.2 0.1 copy.119
  92.3 32.4 %all_to_all.72 = bf16[8,256,448]{1,2,0:T(8,128)(2,1)S(1)} all-to-all(bf16[8,256,448]{1,2,0:T(8,128)(2,1)S(1)} %bitcast.89), channel_id=1, replica_groups=mesh['segment'=4,'y'=4,'zhi'=4,'zlo'=4,'core'=2] {'segment','core'}, dimensions={0} | all-to-all | bytes 3670016 | tf_op jit(solution)/shard_map/all_to_all | solution.py:49
  124.8 0.3 convert_reduce_fusion
  125.0 0.2 copy.86
  125.3 16.0 %all_to_all.73 = f32[4,64,448]{2,1,0:T(8,128)S(1)} all-to-all(f32[4,64,448]{2,1,0:T(8,128)S(1)} %bitcast.94), channel_id=1, replica_groups=mesh['segment'=4,'y'=4,'zhi'=4,'zlo'=4,'core'=2] {'zlo'}, dimensions={0} | all-to-all | bytes 917504 | tf_op jit(solution)/shard_map/all_to_all | solution.py:24
  141.4 20.8 %all_to_all.74 = f32[16,1,64]{2,1,0:T(1,128)S(1)} all-to-all(f32[16,1,64]{2,1,0:T(1,128)S(1)} %reshape.143), channel_id=1, replica_groups=mesh['segment'=4,'y'=4,'zhi'=4,'zlo'=4,'core'=2] {'y','zhi'}, dimensions={0} | all-to-all | bytes 8192 | tf_op jit(solution)/shard_map/all_to_all | solution.py:18
  162.3 11.3 %all_gather.10 = bf16[256,448]{1,0:T(8,128)(2,1)S(1)} all-gather(bf16[64,448]{1,0:T(8,128)(2,1)S(1)} %multiply_convert_fusion.1), channel_id=1, replica_groups=mesh['segment'=4,'y'=4,'zhi'=4,'zlo'=4,'core'=2] {'zlo'}, dimensions={0}, use_global_device_ids=true | all-gather | bytes 286720 | tf_op jit(solution)/shard_map/all_gather | solution.py:60
  173.6 0.1 copy.88
  173.9 31.9 %all_to_all.75 = bf16[8,256,448]{1,2,0:T(8,128)(2,1)S(1)} all-to-all(bf16[8,256,448]{1,2,0:T(8,128)(2,1)S(1)} %broadcast_in_dim.15), channel_id=1, replica_groups=mesh['segment'=4,'y'=4,'zhi'=4,'zlo'=4,'core'=2] {'segment','core'}, dimensions={0} | all-to-all | bytes 3670016 | tf_op jit(solution)/shard_map/all_to_all | solution.py:62
  205.8 1.0 copy.89
  206.8 2.2 dot_general.15
  209.0 2.9 fusion
  211.9 50.2 %all_to_all.76 = f32[4,512,500]{1,2,0:T(8,128)} all-to-all(f32[4,512,500]{1,2,0:T(8,128)S(1)} %fusion), channel_id=1, replica_groups=mesh['segment'=4,'y'=4,'zhi'=4,'zlo'=4,'core'=2] {'y'}, dimensions={0} | all-to-all | bytes 8192000 | tf_op jit(solution)/shard_map/all_to_all | solution.py:24
  262.1 3.7 reduce_sum.122
  265.8 2.6 all_to_all.56
  268.4 2.3 copy.91
  270.7 4.4 %all-to-all-start.6 = ((f32[4,128,500]{1,2,0:T(8,128)}), f32[4,128,500]{1,2,0:T(8,128)}, u32[]{:S(2)}, u32[]{:S(2)}) async-start(f32[4,128,500]{1,2,0:T(8,128)} %copy.91), calls=%async_computation.6 | async-start | bytes 2064384 | tf_op jit(solution)/shard_map/all_to_all | solution.py:24
  275.2 0.2 reduce-window.8
  275.5 49.8 %all-to-all-done.6 = f32[4,128,500]{1,2,0:T(8,128)} async-done(((f32[4,128,500]{1,2,0:T(8,128)}), f32[4,128,500]{1,2,0:T(8,128)}, u32[]{:S(2)}, u32[]{:S(2)}) %all-to-all-start.6) | async-done | bytes 1024032 | tf_op jit(solution)/shard_map/all_to_all | solution.py:24
  325.3 1.3 reduce_sum.123
  326.8 0.3 multiply_reduce_fusion
  327.1 0.6 reshape.144
  327.8 8.3 %all-to-all-start.7 = ((f32[32,3,128]{2,1,0:T(4,128)}), f32[32,3,128]{2,1,0:T(4,128)S(1)}, u32[]{:S(2)}, u32[]{:S(2)}) async-start(f32[32,3,128]{2,1,0:T(4,128)} %reshape.144), calls=%async_computation.7 | async-start | bytes 131072 | tf_op jit(solution)/shard_map/all_to_all | solution.py:18
  336.1 7.8 %all-to-all-done.7 = f32[32,3,128]{2,1,0:T(4,128)S(1)} async-done(((f32[32,3,128]{2,1,0:T(4,128)}), f32[32,3,128]{2,1,0:T(4,128)S(1)}, u32[]{:S(2)}, u32[]{:S(2)}) %all-to-all-start.7) | async-done | bytes 49184 | tf_op jit(solution)/shard_map/all_to_all | solution.py:18
  344.0 0.3 multiply_convert_fusion
  344.4 0.9 broadcast_in_dim.16
  345.2 4.1 all-to-all-start.8
  349.4 39.4 %all_gather.11 = bf16[512,504]{0,1:T(8,128)(2,1)} all-gather(bf16[128,504]{0,1:T(8,128)(2,1)S(1)} %concatenate.14), channel_id=1, replica_groups=mesh['segment'=4,'y'=4,'zhi'=4,'zlo'=4,'core'=2] {'zhi'}, dimensions={0}, use_global_device_ids=true | all-gather | bytes 645120 | tf_op jit(solution)/shard_map/all_gather | solution.py:118
  388.8 1.2 copy.94
  390.1 0.2 fusion.20
  390.2 0.3 copy.95
  390.5 1.3 broadcast_in_dim.18
  391.8 4.5 %all-to-all-start.9 = ((bf16[4,384,504]{1,2,0:T(8,128)(2,1)}), bf16[4,384,504]{1,2,0:T(8,128)(2,1)}, u32[]{:S(2)}, u32[]{:S(2)}) async-start(bf16[4,384,504]{1,2,0:T(8,128)(2,1)} %broadcast_in_dim.18), calls=%async_computation.9 | async-start | bytes 3096576 | tf_op jit(solution)/shard_map/all_to_all | solution.py:18
  396.4 1.5 reshape.148
  397.8 3.4 copy.104
  401.2 0.9 constant_dynamic-slice_fusion
  402.1 0.7 slice.108
  402.8 2.4 convolution_bitcast_fusion
  405.3 10.5 %all-to-all-done.9 = bf16[4,384,504]{1,2,0:T(8,128)(2,1)} async-done(((bf16[4,384,504]{1,2,0:T(8,128)(2,1)}), bf16[4,384,504]{1,2,0:T(8,128)(2,1)}, u32[]{:S(2)}, u32[]{:S(2)}) %all-to-all-start.9) | async-done | bytes 1548320 | tf_op jit(solution)/shard_map/all_to_all | solution.py:18
  415.8 1.7 copy.96
  417.5 0.2 slice.109
  417.7 0.2 copy.98
  418.0 0.6 slice_reduce_fusion
  419.9 3.4 fusion.11
  (44 shorter events, 1.0 us)
Async XLA Ops:
  0.6 89.5 %copy-start = (bf16[1,896,448]{1,2,0:T(8,128)(2,1)S(1)}, bf16[1,896,448]{1,2,0:T(8,128)(2,1)}, u32[]{:S(2)}) copy-start(bf16[1,896,448]{1,2,0:T(8,128)(2,1)} %param.9) | copy-start | bytes 2408452
  125.0 37.2 %copy-start.6 = (f32[448]{0:T(512)S(1)}, f32[448]{0:T(512)}, u32[]{:S(2)}) copy-start(f32[448]{0:T(512)} %param.10) | copy-start | bytes 5380
  206.8 2.2 copy-start.2
  268.4 6.7 %copy-start.3 = (f32[128,8]{0,1:T(8,128)S(1)}, f32[128,8]{0,1:T(8,128)}, u32[]{:S(2)}) copy-start(f32[128,8]{0,1:T(8,128)} %param.15) | copy-start | bytes 12292
  268.4 6.8 %copy-start.7 = (s32[12]{0:T(128)S(1)}, s32[12]{0:T(128)}, u32[]{:S(2)}) copy-start(s32[12]{0:T(128)} %param.12) | copy-start | bytes 148
  268.4 7.1 %copy-start.5 = (s32[128,8]{0,1:T(8,128)S(1)}, s32[128,8]{0,1:T(8,128)}, u32[]{:S(2)}) copy-start(s32[128,8]{0,1:T(8,128)} %param.14) | copy-start | bytes 12292
  270.7 56.1 %copy-start.4 = (s32[128]{0:T(128)S(1)}, s32[128]{0:T(128)}, u32[]{:S(2)}) copy-start(s32[128]{0:T(128)} %param.13) | copy-start | bytes 1540
  270.7 54.6 %all-to-all-start.6 = ((f32[4,128,500]{1,2,0:T(8,128)}), f32[4,128,500]{1,2,0:T(8,128)}, u32[]{:S(2)}, u32[]{:S(2)}) async-start(f32[4,128,500]{1,2,0:T(8,128)} %copy.91), calls=%async_computation.6 | async-start | bytes 2064384 | tf_op jit(solution)/shard_map/all_to_all | solution.py:24
  327.8 16.1 %all-to-all-start.7 = ((f32[32,3,128]{2,1,0:T(4,128)}), f32[32,3,128]{2,1,0:T(4,128)S(1)}, u32[]{:S(2)}, u32[]{:S(2)}) async-start(f32[32,3,128]{2,1,0:T(4,128)} %reshape.144), calls=%async_computation.7 | async-start | bytes 131072 | tf_op jit(solution)/shard_map/all_to_all | solution.py:18
  345.2 45.2 %all-to-all-start.8 = ((bf16[4,128,504]{1,2,0:T(8,128)(2,1)}), bf16[4,128,504]{1,2,0:T(8,128)(2,1)}, u32[]{:S(2)}, u32[]{:S(2)}) async-start(bf16[4,128,504]{1,2,0:T(8,128)(2,1)} %broadcast_in_dim.16), calls=%async_computation.8 | async-start | bytes 1032192 | tf_op jit(solution)/shard_map/all_to_all | solution.py:18
  391.8 24.0 %all-to-all-start.9 = ((bf16[4,384,504]{1,2,0:T(8,128)(2,1)}), bf16[4,384,504]{1,2,0:T(8,128)(2,1)}, u32[]{:S(2)}, u32[]{:S(2)}) async-start(bf16[4,384,504]{1,2,0:T(8,128)(2,1)} %broadcast_in_dim.18), calls=%async_computation.9 | async-start | bytes 3096576 | tf_op jit(solution)/shard_map/all_to_all | solution.py:18
  397.8 3.4 copy-start.1

commit v11 on v10

--- a/solution.py
+++ b/solution.py
@@ -39,8 +39,23 @@
     tok_local = sources.shape[1]
     n_sm = sizes["segment"] * sizes["zlo"] * sizes["core"]
 
-    rows = lax.all_gather(sources[0], "zhi", axis=0, tiled=True)
-    rows = spread_gather(rows, "y", sizes["y"])
+    n_y, n_zhi = sizes["y"], sizes["zhi"]
+    me = lax.axis_index("zhi")
+    own = sources[0]
+    own_y = spread_gather(own, "y", n_y).reshape(n_y, 1, tok_local, -1)
+    zhi_all = lax.all_gather(own, "zhi", axis=0, tiled=True).reshape(n_zhi, tok_local, -1)
+    others = lax.dynamic_slice_in_dim(
+        jnp.concatenate([zhi_all, zhi_all], axis=0), me + 1, n_zhi - 1, axis=0
+    )
+    others_y = spread_gather(others.reshape((n_zhi - 1) * tok_local, -1), "y", n_y)
+    others_y = others_y.reshape(n_y, n_zhi - 1, tok_local, -1)
+    rows = jnp.zeros((n_y, n_zhi, tok_local, own.shape[1]), own.dtype)
+    rows = lax.dynamic_update_slice_in_dim(rows, own_y, me, axis=1)
+    for k in range(n_zhi - 1):
+        rows = lax.dynamic_update_slice_in_dim(
+            rows, others_y[:, k : k + 1], (me + 1 + k) % n_zhi, axis=1
+        )
+    rows = rows.reshape(n_y * n_zhi * tok_local, -1)
     tokens = rows.shape[0]
     product = jnp.dot(rows, unite_weight[0], preferred_element_type=jnp.float32)
     product = lax.optimization_barrier(product.astype(jnp.bfloat16))
@@ -112,8 +127,6 @@
         axis=1,
     )
     carried = jnp.concatenate([logit_grad, extra], axis=1)
-    n_y, n_zhi = sizes["y"], sizes["zhi"]
-    me = lax.axis_index("zhi")
     own_y = spread_gather(carried, "y", n_y).reshape(n_y, 1, tok_local, -1)
     zhi_all = lax.all_gather(carried, "zhi", axis=0, tiled=True).reshape(n_zhi, tok_local, -1)
     others = lax.dynamic_slice_in_dim(

time: 425 us -> 428 us (level)
  blocking collectives: 291 us -> 244 us
  waiting for transfers between devices: 68.1 us -> 94.3 us
  local copies, waits for them, and re-layouts: 22 us -> 32 us
  starting transfers between devices: 21.3 us -> 30.3 us
    all_to_all x2 -> x1, blocking collectives: 64.2 us -> 20.7 us  [spread_gather(): lax.all_to_all(spread.reshape((size * value.shape[0],) + value.shape[1:])...]
    all_to_all x3 -> x5, waiting for transfers between devices: 18.3 us -> 44.5 us  [spread_gather(): lax.all_to_all(spread.reshape((size * value.shape[0],) + value.shape[1:])...]
    all_to_all x3 -> x5, starting transfers between devices: 16.9 us -> 25.9 us  [spread_gather(): lax.all_to_all(spread.reshape((size * value.shape[0],) + value.shape[1:])...]
  transfers between devices with their start and end apart: 4 -> 6, of which waited for: 3 -> 4; matrix products, arithmetic and copies ran while one was open for 3% -> 3% of each run, Pallas kernels for 0% -> 0%
where the time goes in v11:
time: 428 us; the launch traced here: 425 us
  blocking collectives  244 us (57%)
  waiting for transfers between devices  94.3 us (22%)
  local copies, waits for them, and re-layouts  32 us (7%)
  starting transfers between devices  30.3 us (7%)
  matrix products  12.9 us (3%)
  other arithmetic  7.95 us (2%)
    all_to_all x2, blocking collectives, scatter_sum(): pieces = lax.all_to_all(value, axes, 0, 0, tiled=True)  66.2 us
    all_to_all x1, waiting for transfers between devices, scatter_sum(): pieces = lax.all_to_all(value, axes, 0, 0, tiled=True)  49.8 us
    all_to_all x5, waiting for transfers between devices, spread_gather(): lax.all_to_all(spread.reshape((size * value.shape[0],) + value.shape[1:])...  44.5 us
    all_gather x1, blocking collectives, on_device(): lax.all_gather(own, 'zhi', axis=0, tiled=True).reshape(n_zhi, tok_local, -1)  44.5 us
    all_gather x1, blocking collectives, on_device(): lax.all_gather(carried, 'zhi', axis=0, tiled=True)  39.6 us
    all_to_all x1, blocking collectives, on_device(): lax.all_to_all(spread.reshape(tokens, -1), ('segment', 'core'), 0, 0, til...  31.9 us
    all_to_all x1, blocking collectives, on_device(): pieces = lax.all_to_all(product, ('segment', 'core'), 0, 0, tiled=True)  30.2 us
    all_to_all x5, starting transfers between devices, spread_gather(): lax.all_to_all(spread.reshape((size * value.shape[0],) + value.shape[1:])...  25.9 us
  transfers between devices with their start and end apart: 6, of which 4 were waited for; matrix products, arithmetic and copies ran while one was open for 3% of the time, Pallas kernels for 0%

profile of v11, /device:TPU:1, one launch (start us, length us, event | category | flops | bytes accessed | tf_op | source)
XLA Modules:
  0.0 424.9 jit_solution(7225482324980679232)
XLA Ops:
  0.7 2.0 broadcast_in_dim.24
  2.7 5.0 %all-to-all-start = ((bf16[4,128,896]{2,1,0:T(8,128)(2,1)}), bf16[4,128,896]{2,1,0:T(8,128)(2,1)S(1)}, u32[]{:S(2)}, u32[]{:S(2)}) async-start(bf16[4,128,896]{2,1,0:T(8,128)(2,1)} %broadcast_in_dim.24), calls=%async_computation | async-start | bytes 1835008 | tf_op jit(solution)/shard_map/all_to_all | solution.py:18
  7.7 44.5 %all-gather = bf16[1,512,896]{2,1,0:T(8,128)(2,1)S(1)} all-gather(bf16[1,128,896]{2,1,0:T(8,128)(2,1)S(1)} %copy-done.4), channel_id=2, replica_groups=mesh['segment'=4,'y'=4,'zhi'=4,'zlo'=4,'core'=2] {'zhi'}, dimensions={1}, use_global_device_ids=true | all-gather | bytes 1146880 | tf_op jit(solution)/shard_map/all_gather | solution.py:46
  52.2 0.3 fusion.17
  52.5 1.8 broadcast_in_dim.26
  54.3 4.3 %all-to-all-start.1 = ((bf16[4,384,896]{2,1,0:T(8,128)(2,1)}), bf16[4,384,896]{2,1,0:T(8,128)(2,1)S(1)}, u32[]{:S(2)}, u32[]{:S(2)}) async-start(bf16[4,384,896]{2,1,0:T(8,128)(2,1)} %broadcast_in_dim.26), calls=%async_computation.1 | async-start | bytes 5505024 | tf_op jit(solution)/shard_map/all_to_all | solution.py:18
  58.6 2.3 broadcast_in_dim.22
  60.9 1.0 bitcast_dynamic-update-slice_fusion
  61.9 28.6 %all-to-all-done.1 = bf16[4,384,896]{2,1,0:T(8,128)(2,1)S(1)} async-done(((bf16[4,384,896]{2,1,0:T(8,128)(2,1)}), bf16[4,384,896]{2,1,0:T(8,128)(2,1)S(1)}, u32[]{:S(2)}, u32[]{:S(2)}) %all-to-all-start.1) | async-done | bytes 2752544 | tf_op jit(solution)/shard_map/all_to_all | solution.py:18
  90.4 1.0 slice_dynamic-update-slice_fusion.2
  91.5 1.0 slice_dynamic-update-slice_fusion.1
  92.5 1.0 slice_dynamic-update-slice_fusion
  93.5 4.1 convolution_convert_fusion
  97.8 30.2 %all_to_all.74 = bf16[8,256,448]{1,2,0:T(8,128)(2,1)S(1)} all-to-all(bf16[8,256,448]{1,2,0:T(8,128)(2,1)S(1)} %bitcast.97), channel_id=1, replica_groups=mesh['segment'=4,'y'=4,'zhi'=4,'zlo'=4,'core'=2] {'segment','core'}, dimensions={0} | all-to-all | bytes 3670016 | tf_op jit(solution)/shard_map/all_to_all | solution.py:64
  128.4 15.9 %all_to_all.75 = f32[4,64,448]{2,1,0:T(8,128)S(1)} all-to-all(f32[4,64,448]{2,1,0:T(8,128)S(1)} %bitcast.102), channel_id=1, replica_groups=mesh['segment'=4,'y'=4,'zhi'=4,'zlo'=4,'core'=2] {'zlo'}, dimensions={0} | all-to-all | bytes 917504 | tf_op jit(solution)/shard_map/all_to_all | solution.py:24
  144.5 20.7 %all_to_all.76 = f32[16,1,64]{2,1,0:T(1,128)S(1)} all-to-all(f32[16,1,64]{2,1,0:T(1,128)S(1)} %reshape.165), channel_id=1, replica_groups=mesh['segment'=4,'y'=4,'zhi'=4,'zlo'=4,'core'=2] {'y','zhi'}, dimensions={0} | all-to-all | bytes 8192 | tf_op jit(solution)/shard_map/all_to_all | solution.py:18
  165.3 11.3 %all_gather.10 = bf16[256,448]{1,0:T(8,128)(2,1)S(1)} all-gather(bf16[64,448]{1,0:T(8,128)(2,1)S(1)} %multiply_convert_fusion.1), channel_id=1, replica_groups=mesh['segment'=4,'y'=4,'zhi'=4,'zlo'=4,'core'=2] {'zlo'}, dimensions={0}, use_global_device_ids=true | all-gather | bytes 286720 | tf_op jit(solution)/shard_map/all_gather | solution.py:75
  176.9 31.9 %all_to_all.77 = bf16[8,256,448]{1,2,0:T(8,128)(2,1)S(1)} all-to-all(bf16[8,256,448]{1,2,0:T(8,128)(2,1)S(1)} %broadcast_in_dim.27), channel_id=1, replica_groups=mesh['segment'=4,'y'=4,'zhi'=4,'zlo'=4,'core'=2] {'segment','core'}, dimensions={0} | all-to-all | bytes 3670016 | tf_op jit(solution)/shard_map/all_to_all | solution.py:77
  208.8 1.0 copy.89
  209.8 2.2 dot_general.15
  212.0 2.9 fusion
  214.9 50.2 %all_to_all.78 = f32[4,512,500]{1,2,0:T(8,128)} all-to-all(f32[4,512,500]{1,2,0:T(8,128)S(1)} %fusion), channel_id=1, replica_groups=mesh['segment'=4,'y'=4,'zhi'=4,'zlo'=4,'core'=2] {'y'}, dimensions={0} | all-to-all | bytes 8192000 | tf_op jit(solution)/shard_map/all_to_all | solution.py:24
  265.2 3.7 reduce_sum.122
  268.9 2.6 all_to_all.58
  271.4 2.3 copy.91
  273.7 4.4 %all-to-all-start.7 = ((f32[4,128,500]{1,2,0:T(8,128)}), f32[4,128,500]{1,2,0:T(8,128)}, u32[]{:S(2)}, u32[]{:S(2)}) async-start(f32[4,128,500]{1,2,0:T(8,128)} %copy.91), calls=%async_computation.7 | async-start | bytes 2064384 | tf_op jit(solution)/shard_map/all_to_all | solution.py:24
  278.5 49.8 %all-to-all-done.7 = f32[4,128,500]{1,2,0:T(8,128)} async-done(((f32[4,128,500]{1,2,0:T(8,128)}), f32[4,128,500]{1,2,0:T(8,128)}, u32[]{:S(2)}, u32[]{:S(2)}) %all-to-all-start.7) | async-done | bytes 1024032 | tf_op jit(solution)/shard_map/all_to_all | solution.py:24
  328.3 1.3 reduce_sum.123
  329.8 0.3 multiply_reduce_fusion
  330.1 0.6 reshape.166
  330.8 7.9 %all-to-all-start.8 = ((f32[32,3,128]{2,1,0:T(4,128)}), f32[32,3,128]{2,1,0:T(4,128)S(1)}, u32[]{:S(2)}, u32[]{:S(2)}) async-start(f32[32,3,128]{2,1,0:T(4,128)} %reshape.166), calls=%async_computation.8 | async-start | bytes 131072 | tf_op jit(solution)/shard_map/all_to_all | solution.py:18
  338.7 7.9 %all-to-all-done.8 = f32[32,3,128]{2,1,0:T(4,128)S(1)} async-done(((f32[32,3,128]{2,1,0:T(4,128)}), f32[32,3,128]{2,1,0:T(4,128)S(1)}, u32[]{:S(2)}, u32[]{:S(2)}) %all-to-all-start.8) | async-done | bytes 49184 | tf_op jit(solution)/shard_map/all_to_all | solution.py:18
  346.8 0.3 multiply_convert_fusion
  347.2 0.9 broadcast_in_dim.28
  348.0 4.1 all-to-all-start.9
  352.2 39.6 %all_gather.11 = bf16[512,504]{0,1:T(8,128)(2,1)} all-gather(bf16[128,504]{0,1:T(8,128)(2,1)S(1)} %concatenate.18), channel_id=1, replica_groups=mesh['segment'=4,'y'=4,'zhi'=4,'zlo'=4,'core'=2] {'zhi'}, dimensions={0}, use_global_device_ids=true | all-gather | bytes 645120 | tf_op jit(solution)/shard_map/all_gather | solution.py:131
  391.7 1.2 copy.94
  393.4 1.3 broadcast_in_dim.30
  394.7 4.5 %all-to-all-start.10 = ((bf16[4,384,504]{1,2,0:T(8,128)(2,1)}), bf16[4,384,504]{1,2,0:T(8,128)(2,1)}, u32[]{:S(2)}, u32[]{:S(2)}) async-start(bf16[4,384,504]{1,2,0:T(8,128)(2,1)} %broadcast_in_dim.30), calls=%async_computation.10 | async-start | bytes 3096576 | tf_op jit(solution)/shard_map/all_to_all | solution.py:18
  399.3 1.5 reshape.170
  400.7 3.4 copy.104
  404.1 0.9 constant_dynamic-slice_fusion
  405.1 0.7 slice.123
  405.8 2.4 convolution_bitcast_fusion
  408.2 8.0 %all-to-all-done.10 = bf16[4,384,504]{1,2,0:T(8,128)(2,1)} async-done(((bf16[4,384,504]{1,2,0:T(8,128)(2,1)}), bf16[4,384,504]{1,2,0:T(8,128)(2,1)}, u32[]{:S(2)}, u32[]{:S(2)}) %all-to-all-start.10) | async-done | bytes 1548320 | tf_op jit(solution)/shard_map/all_to_all | solution.py:18
  416.2 1.7 copy.96
  418.5 0.6 slice_reduce_fusion
  420.3 3.4 fusion.11
  (60 shorter events, 2.8 us)
Async XLA Ops:
  0.6 92.9 %copy-start = (bf16[1,896,448]{1,2,0:T(8,128)(2,1)S(1)}, bf16[1,896,448]{1,2,0:T(8,128)(2,1)}, u32[]{:S(2)}) copy-start(bf16[1,896,448]{1,2,0:T(8,128)(2,1)} %param.9) | copy-start | bytes 2408452
  0.6 7.1 %copy-start.4 = (bf16[1,128,896]{2,1,0:T(8,128)(2,1)S(1)}, bf16[1,128,896]{2,1,0:T(8,128)(2,1)}, u32[]{:S(2)}) copy-start(bf16[1,128,896]{2,1,0:T(8,128)(2,1)} %param.8) | copy-start | bytes 688132
  2.7 49.8 %all-to-all-start = ((bf16[4,128,896]{2,1,0:T(8,128)(2,1)}), bf16[4,128,896]{2,1,0:T(8,128)(2,1)S(1)}, u32[]{:S(2)}, u32[]{:S(2)}) async-start(bf16[4,128,896]{2,1,0:T(8,128)(2,1)} %broadcast_in_dim.24), calls=%async_computation | async-start | bytes 1835008 | tf_op jit(solution)/shard_map/all_to_all | solution.py:18
  52.5 1.8 copy-start.2
  54.3 36.1 %all-to-all-start.1 = ((bf16[4,384,896]{2,1,0:T(8,128)(2,1)}), bf16[4,384,896]{2,1,0:T(8,128)(2,1)S(1)}, u32[]{:S(2)}, u32[]{:S(2)}) async-start(bf16[4,384,896]{2,1,0:T(8,128)(2,1)} %broadcast_in_dim.26), calls=%async_computation.1 | async-start | bytes 5505024 | tf_op jit(solution)/shard_map/all_to_all | solution.py:18
  58.6 2.3 copy-start.3
  128.2 37.0 %copy-start.9 = (f32[448]{0:T(512)S(1)}, f32[448]{0:T(512)}, u32[]{:S(2)}) copy-start(f32[448]{0:T(512)} %param.10) | copy-start | bytes 5380
  209.8 2.2 copy-start.5
  271.4 6.7 %copy-start.10 = (s32[12]{0:T(128)S(1)}, s32[12]{0:T(128)}, u32[]{:S(2)}) copy-start(s32[12]{0:T(128)} %param.12) | copy-start | bytes 148
  271.4 6.9 %copy-start.6 = (f32[128,8]{0,1:T(8,128)S(1)}, f32[128,8]{0,1:T(8,128)}, u32[]{:S(2)}) copy-start(f32[128,8]{0,1:T(8,128)} %param.15) | copy-start | bytes 12292
  271.4 7.1 %copy-start.8 = (s32[128,8]{0,1:T(8,128)S(1)}, s32[128,8]{0,1:T(8,128)}, u32[]{:S(2)}) copy-start(s32[128,8]{0,1:T(8,128)} %param.14) | copy-start | bytes 12292
  273.7 56.1 %copy-start.7 = (s32[128]{0:T(128)S(1)}, s32[128]{0:T(128)}, u32[]{:S(2)}) copy-start(s32[128]{0:T(128)} %param.13) | copy-start | bytes 1540
  273.7 54.6 %all-to-all-start.7 = ((f32[4,128,500]{1,2,0:T(8,128)}), f32[4,128,500]{1,2,0:T(8,128)}, u32[]{:S(2)}, u32[]{:S(2)}) async-start(f32[4,128,500]{1,2,0:T(8,128)} %copy.91), calls=%async_computation.7 | async-start | bytes 2064384 | tf_op jit(solution)/shard_map/all_to_all | solution.py:24
  330.8 15.8 %all-to-all-start.8 = ((f32[32,3,128]{2,1,0:T(4,128)}), f32[32,3,128]{2,1,0:T(4,128)S(1)}, u32[]{:S(2)}, u32[]{:S(2)}) async-start(f32[32,3,128]{2,1,0:T(4,128)} %reshape.166), calls=%async_computation.8 | async-start | bytes 131072 | tf_op jit(solution)/shard_map/all_to_all | solution.py:18
  348.0 45.4 %all-to-all-start.9 = ((bf16[4,128,504]{1,2,0:T(8,128)(2,1)}), bf16[4,128,504]{1,2,0:T(8,128)(2,1)}, u32[]{:S(2)}, u32[]{:S(2)}) async-start(bf16[4,128,504]{1,2,0:T(8,128)(2,1)} %broadcast_in_dim.28), calls=%async_computation.9 | async-start | bytes 1032192 | tf_op jit(solution)/shard_map/all_to_all | solution.py:18
  394.7 21.5 %all-to-all-start.10 = ((bf16[4,384,504]{1,2,0:T(8,128)(2,1)}), bf16[4,384,504]{1,2,0:T(8,128)(2,1)}, u32[]{:S(2)}, u32[]{:S(2)}) async-start(bf16[4,384,504]{1,2,0:T(8,128)(2,1)} %broadcast_in_dim.30), calls=%async_computation.10 | async-start | bytes 3096576 | tf_op jit(solution)/shard_map/all_to_all | solution.py:18
  400.7 3.4 copy-start.1

commit v12 on v10

--- a/solution.py
+++ b/solution.py
@@ -51,13 +51,14 @@
     united = jnp.sum(pieces.reshape(n_sc, chunk, -1).astype(jnp.float32), axis=0)
     united = scatter_sum(united, "zlo", sizes["zlo"])
 
+    n_seq = sizes["y"] * sizes["zhi"]
     squares = jnp.sum(united * united, axis=1)
-    n_seq = sizes["y"] * sizes["zhi"]
-    squares = jnp.sum(spread_gather(squares[None], SEQ, n_seq), axis=0)
-    hidden_part = (
-        united * lax.rsqrt(squares / D + norm_eps)[:, None] * norm_gain[None, :]
+    squares = spread_gather(squares[None], ("y", "zhi", "zlo"), n_seq * sizes["zlo"])
+    squares = jnp.sum(squares.reshape(n_seq, sizes["zlo"] * squares.shape[-1]), axis=0)
+    united_chunk = lax.all_gather(united, "zlo", axis=0, tiled=True)
+    hidden_chunk = (
+        united_chunk * lax.rsqrt(squares / D + norm_eps)[:, None] * norm_gain[None, :]
     ).astype(jnp.bfloat16)
-    hidden_chunk = lax.all_gather(hidden_part, "zlo", axis=0, tiled=True)
     spread = jnp.broadcast_to(hidden_chunk[None], (n_sc,) + hidden_chunk.shape)
     hidden = lax.all_to_all(
         spread.reshape(tokens, -1), ("segment", "core"), 0, 0, tiled=True

time: 425 us -> 421 us (level)
  blocking collectives: 291 us -> 271 us
  starting transfers between devices: 21.3 us -> 35.8 us
    all_to_all x2 -> x1, blocking collectives: 64.2 us -> 43.4 us  [spread_gather(): lax.all_to_all(spread.reshape((size * value.shape[0],) + value.shape[1:])...]
    all_to_all x3 -> x4, starting transfers between devices: 16.9 us -> 24.9 us  [spread_gather(): lax.all_to_all(spread.reshape((size * value.shape[0],) + value.shape[1:])...]
    all_to_all x1, starting transfers between devices: 4.39 us -> 11 us  [scatter_sum(): pieces = lax.all_to_all(value, axes, 0, 0, tiled=True)]
    all_to_all x3 -> x4, waiting for transfers between devices: 18.3 us -> 17.3 us  [spread_gather(): lax.all_to_all(spread.reshape((size * value.shape[0],) + value.shape[1:])...]
  transfers between devices with their start and end apart: 4 -> 5, of which waited for: 3 -> 3; matrix products, arithmetic and copies ran while one was open for 3% -> 3% of each run, Pallas kernels for 0% -> 0%
where the time goes in v12:
time: 421 us; the launch traced here: 420 us
  blocking collectives  271 us (64%)
  waiting for transfers between devices  67 us (16%)
  starting transfers between devices  35.8 us (9%)
  local copies, waits for them, and re-layouts  23.3 us (6%)
  matrix products  10.9 us (3%)
  other arithmetic  8.43 us (2%)
    all_to_all x2, blocking collectives, scatter_sum(): pieces = lax.all_to_all(value, axes, 0, 0, tiled=True)  66.7 us
    all_to_all x1, waiting for transfers between devices, scatter_sum(): pieces = lax.all_to_all(value, axes, 0, 0, tiled=True)  49.7 us
    all_gather x1, blocking collectives, on_device(): rows = lax.all_gather(sources[0], 'zhi', axis=0, tiled=True)  45.8 us
    all_to_all x1, blocking collectives, spread_gather(): lax.all_to_all(spread.reshape((size * value.shape[0],) + value.shape[1:])...  43.4 us
    all_gather x1, blocking collectives, on_device(): lax.all_gather(carried, 'zhi', axis=0, tiled=True)  39 us
    all_to_all x1, blocking collectives, on_device(): pieces = lax.all_to_all(product, ('segment', 'core'), 0, 0, tiled=True)  32.4 us
    all_to_all x1, blocking collectives, on_device(): lax.all_to_all(spread.reshape(tokens, -1), ('segment', 'core'), 0, 0, til...  30.5 us
    all_to_all x4, starting transfers between devices, spread_gather(): lax.all_to_all(spread.reshape((size * value.shape[0],) + value.shape[1:])...  24.9 us
  transfers between devices with their start and end apart: 5, of which 3 were waited for; matrix products, arithmetic and copies ran while one was open for 3% of the time, Pallas kernels for 0%

profile of v12, /device:TPU:1, one launch (start us, length us, event | category | flops | bytes accessed | tf_op | source)
XLA Modules:
  0.0 419.7 jit_solution(6693472070316285342)
XLA Ops:
  0.6 45.8 %all-gather = bf16[1,512,896]{2,1,0:T(8,128)(2,1)S(1)} all-gather(bf16[1,128,896]{2,1,0:T(8,128)(2,1)} %param.8), channel_id=2, replica_groups=mesh['segment'=4,'y'=4,'zhi'=4,'zlo'=4,'core'=2] {'zhi'}, dimensions={1}, use_global_device_ids=true | all-gather | bytes 1146880 | tf_op jit(solution)/shard_map/all_gather | solution.py:42
  46.4 0.3 broadcast_in_dim.14
  46.7 43.4 %all_to_all.71 = bf16[4,512,896]{2,1,0:T(8,128)(2,1)S(1)} all-to-all(bf16[4,512,896]{2,1,0:T(8,128)(2,1)S(1)} %broadcast_in_dim.14), channel_id=1, replica_groups=mesh['segment'=4,'y'=4,'zhi'=4,'zlo'=4,'core'=2] {'y'}, dimensions={0} | all-to-all | bytes 7340032 | tf_op jit(solution)/shard_map/all_to_all | solution.py:18
  90.1 2.1 convolution_convert_fusion
  92.3 32.4 %all_to_all.72 = bf16[8,256,448]{1,2,0:T(8,128)(2,1)S(1)} all-to-all(bf16[8,256,448]{1,2,0:T(8,128)(2,1)S(1)} %bitcast.88), channel_id=1, replica_groups=mesh['segment'=4,'y'=4,'zhi'=4,'zlo'=4,'core'=2] {'segment','core'}, dimensions={0} | all-to-all | bytes 3670016 | tf_op jit(solution)/shard_map/all_to_all | solution.py:49
  124.8 0.3 convert_reduce_fusion
  125.0 0.2 copy.108
  125.3 16.0 %all_to_all.73 = f32[4,64,448]{2,1,0:T(8,128)S(1)} all-to-all(f32[4,64,448]{2,1,0:T(8,128)S(1)} %bitcast.93), channel_id=1, replica_groups=mesh['segment'=4,'y'=4,'zhi'=4,'zlo'=4,'core'=2] {'zlo'}, dimensions={0} | all-to-all | bytes 917504 | tf_op jit(solution)/shard_map/all_to_all | solution.py:24
  141.4 0.6 reshape.147
  142.0 8.3 %all-to-all-start.3 = ((f32[64,1,64]{2,1,0:T(1,128)}), f32[64,1,64]{2,1,0:T(1,128)S(1)}, u32[]{:S(2)}, u32[]{:S(2)}) async-start(f32[64,1,64]{2,1,0:T(1,128)} %reshape.147), calls=%async_computation.3 | async-start | bytes 65536 | tf_op jit(solution)/shard_map/all_to_all | solution.py:18
  150.3 13.3 %all_gather.10 = f32[256,448]{1,0:T(8,128)S(1)} all-gather(f32[64,448]{1,0:T(8,128)S(1)} %reduce_sum.119), channel_id=1, replica_groups=mesh['segment'=4,'y'=4,'zhi'=4,'zlo'=4,'core'=2] {'zlo'}, dimensions={0}, use_global_device_ids=true | all-gather | bytes 573440 | tf_op jit(solution)/shard_map/all_gather | solution.py:58
  163.6 0.2 copy.109
  163.8 0.5 broadcast.62
  164.3 0.7 reduce.10
  165.4 30.5 %all_to_all.74 = bf16[8,256,448]{1,2,0:T(8,128)(2,1)S(1)} all-to-all(bf16[8,256,448]{1,2,0:T(8,128)(2,1)S(1)} %broadcast_in_dim.15), channel_id=1, replica_groups=mesh['segment'=4,'y'=4,'zhi'=4,'zlo'=4,'core'=2] {'segment','core'}, dimensions={0} | all-to-all | bytes 3670016 | tf_op jit(solution)/shard_map/all_to_all | solution.py:63
  195.9 1.0 copy.110
  197.0 2.2 dot_general.15
  199.1 2.9 fusion
  202.1 50.8 %all_to_all.75 = f32[4,512,500]{1,2,0:T(8,128)} all-to-all(f32[4,512,500]{1,2,0:T(8,128)S(1)} %fusion), channel_id=1, replica_groups=mesh['segment'=4,'y'=4,'zhi'=4,'zlo'=4,'core'=2] {'y'}, dimensions={0} | all-to-all | bytes 8192000 | tf_op jit(solution)/shard_map/all_to_all | solution.py:24
  252.8 3.7 reduce_sum.122
  256.6 2.6 all_to_all.56
  259.1 2.3 copy.112
  261.4 11.0 %all-to-all-start.6 = ((f32[4,128,500]{1,2,0:T(8,128)}), f32[4,128,500]{1,2,0:T(8,128)}, u32[]{:S(2)}, u32[]{:S(2)}) async-start(f32[4,128,500]{1,2,0:T(8,128)} %copy.112), calls=%async_computation.6 | async-start | bytes 2064384 | tf_op jit(solution)/shard_map/all_to_all | solution.py:24
  272.4 0.2 reduce-window.8
  272.8 49.7 %all-to-all-done.6 = f32[4,128,500]{1,2,0:T(8,128)} async-done(((f32[4,128,500]{1,2,0:T(8,128)}), f32[4,128,500]{1,2,0:T(8,128)}, u32[]{:S(2)}, u32[]{:S(2)}) %all-to-all-start.6) | async-done | bytes 1024032 | tf_op jit(solution)/shard_map/all_to_all | solution.py:24
  322.5 1.3 reduce_sum.123
  324.0 0.3 multiply_reduce_fusion
  324.3 0.6 reshape.149
  324.9 7.9 %all-to-all-start.7 = ((f32[32,3,128]{2,1,0:T(4,128)}), f32[32,3,128]{2,1,0:T(4,128)S(1)}, u32[]{:S(2)}, u32[]{:S(2)}) async-start(f32[32,3,128]{2,1,0:T(4,128)} %reshape.149), calls=%async_computation.7 | async-start | bytes 131072 | tf_op jit(solution)/shard_map/all_to_all | solution.py:18
  332.9 7.8 %all-to-all-done.7 = f32[32,3,128]{2,1,0:T(4,128)S(1)} async-done(((f32[32,3,128]{2,1,0:T(4,128)}), f32[32,3,128]{2,1,0:T(4,128)S(1)}, u32[]{:S(2)}, u32[]{:S(2)}) %all-to-all-start.7) | async-done | bytes 49184 | tf_op jit(solution)/shard_map/all_to_all | solution.py:18
  340.8 0.3 multiply_convert_fusion.1
  341.2 0.9 broadcast_in_dim.16
  342.0 4.1 all-to-all-start.8
  346.2 39.0 %all_gather.11 = bf16[512,504]{0,1:T(8,128)(2,1)} all-gather(bf16[128,504]{0,1:T(8,128)(2,1)S(1)} %concatenate.14), channel_id=1, replica_groups=mesh['segment'=4,'y'=4,'zhi'=4,'zlo'=4,'core'=2] {'zhi'}, dimensions={0}, use_global_device_ids=true | all-gather | bytes 645120 | tf_op jit(solution)/shard_map/all_gather | solution.py:119
  385.1 1.2 copy.115
  386.6 0.3 copy.116
  386.8 1.3 broadcast_in_dim.18
  388.2 4.5 %all-to-all-start.9 = ((bf16[4,384,504]{1,2,0:T(8,128)(2,1)}), bf16[4,384,504]{1,2,0:T(8,128)(2,1)}, u32[]{:S(2)}, u32[]{:S(2)}) async-start(bf16[4,384,504]{1,2,0:T(8,128)(2,1)} %broadcast_in_dim.18), calls=%async_computation.9 | async-start | bytes 3096576 | tf_op jit(solution)/shard_map/all_to_all | solution.py:18
  392.7 1.5 reshape.153
  394.2 3.4 copy.125
  397.5 0.9 constant_dynamic-slice_fusion
  398.5 0.7 slice.108
  399.2 2.4 convolution_bitcast_fusion
  401.6 9.5 %all-to-all-done.9 = bf16[4,384,504]{1,2,0:T(8,128)(2,1)} async-done(((bf16[4,384,504]{1,2,0:T(8,128)(2,1)}), bf16[4,384,504]{1,2,0:T(8,128)(2,1)}, u32[]{:S(2)}, u32[]{:S(2)}) %all-to-all-start.9) | async-done | bytes 1548320 | tf_op jit(solution)/shard_map/all_to_all | solution.py:18
  411.1 1.7 copy.117
  413.0 0.2 copy.119
  413.3 0.6 slice_reduce_fusion
  415.2 3.4 fusion.11
  (48 shorter events, 1.6 us)
Async XLA Ops:
  0.6 89.5 %copy-start = (bf16[1,896,448]{1,2,0:T(8,128)(2,1)S(1)}, bf16[1,896,448]{1,2,0:T(8,128)(2,1)}, u32[]{:S(2)}) copy-start(bf16[1,896,448]{1,2,0:T(8,128)(2,1)} %param.9) | copy-start | bytes 2408452
  125.2 39.9 %copy-start.6 = (f32[448]{0:T(512)S(1)}, f32[448]{0:T(512)}, u32[]{:S(2)}) copy-start(f32[448]{0:T(512)} %param.10) | copy-start | bytes 5380
  142.0 21.8 %all-to-all-start.3 = ((f32[64,1,64]{2,1,0:T(1,128)}), f32[64,1,64]{2,1,0:T(1,128)S(1)}, u32[]{:S(2)}, u32[]{:S(2)}) async-start(f32[64,1,64]{2,1,0:T(1,128)} %reshape.147), calls=%async_computation.3 | async-start | bytes 65536 | tf_op jit(solution)/shard_map/all_to_all | solution.py:18
  197.0 2.2 copy-start.2
  259.1 13.3 %copy-start.3 = (f32[128,8]{0,1:T(8,128)S(1)}, f32[128,8]{0,1:T(8,128)}, u32[]{:S(2)}) copy-start(f32[128,8]{0,1:T(8,128)} %param.15) | copy-start | bytes 12292
  259.1 13.3 %copy-start.7 = (s32[12]{0:T(128)S(1)}, s32[12]{0:T(128)}, u32[]{:S(2)}) copy-start(s32[12]{0:T(128)} %param.12) | copy-start | bytes 148
  259.1 13.6 %copy-start.5 = (s32[128,8]{0,1:T(8,128)S(1)}, s32[128,8]{0,1:T(8,128)}, u32[]{:S(2)}) copy-start(s32[128,8]{0,1:T(8,128)} %param.14) | copy-start | bytes 12292
  261.4 62.5 %copy-start.4 = (s32[128]{0:T(128)S(1)}, s32[128]{0:T(128)}, u32[]{:S(2)}) copy-start(s32[128]{0:T(128)} %param.13) | copy-start | bytes 1540
  261.4 61.0 %all-to-all-start.6 = ((f32[4,128,500]{1,2,0:T(8,128)}), f32[4,128,500]{1,2,0:T(8,128)}, u32[]{:S(2)}, u32[]{:S(2)}) async-start(f32[4,128,500]{1,2,0:T(8,128)} %copy.112), calls=%async_computation.6 | async-start | bytes 2064384 | tf_op jit(solution)/shard_map/all_to_all | solution.py:24
  324.9 15.7 %all-to-all-start.7 = ((f32[32,3,128]{2,1,0:T(4,128)}), f32[32,3,128]{2,1,0:T(4,128)S(1)}, u32[]{:S(2)}, u32[]{:S(2)}) async-start(f32[32,3,128]{2,1,0:T(4,128)} %reshape.149), calls=%async_computation.7 | async-start | bytes 131072 | tf_op jit(solution)/shard_map/all_to_all | solution.py:18
  342.0 44.8 %all-to-all-start.8 = ((bf16[4,128,504]{1,2,0:T(8,128)(2,1)}), bf16[4,128,504]{1,2,0:T(8,128)(2,1)}, u32[]{:S(2)}, u32[]{:S(2)}) async-start(bf16[4,128,504]{1,2,0:T(8,128)(2,1)} %broadcast_in_dim.16), calls=%async_computation.8 | async-start | bytes 1032192 | tf_op jit(solution)/shard_map/all_to_all | solution.py:18
  388.2 22.9 %all-to-all-start.9 = ((bf16[4,384,504]{1,2,0:T(8,128)(2,1)}), bf16[4,384,504]{1,2,0:T(8,128)(2,1)}, u32[]{:S(2)}, u32[]{:S(2)}) async-start(bf16[4,384,504]{1,2,0:T(8,128)(2,1)} %broadcast_in_dim.18), calls=%async_computation.9 | async-start | bytes 3096576 | tf_op jit(solution)/shard_map/all_to_all | solution.py:18
  394.2 3.4 copy-start.1
